TPU v7x, 512 devices: a whole 4x4x16 slice. The times are simulated.
512 devices in a mesh: seq: 16 (over z), exp: 32 (over x, y, core).
Axes of the slice: x: 4, y: 4, z: 16, core: 2. Of those that a mesh axis runs over, the one named last changes fastest.
Arguments:
- queries: bfloat16 [2048, 8192], P('seq', 'exp'), may hold values from -6 to 6
- key_matrix: bfloat16 [2048, 8192], P('seq', 'exp'), may hold values from -6 to 6
- values: bfloat16 [2048, 8192], P('seq', 'exp'), may hold values from -6 to 6
- log_decay: float32 [64, 2048], P('exp', 'seq'), may hold values from -3 to 0
- residual: bfloat16 [2048, 3072], P('seq'), may hold values from -6 to 6
- out_weight: bfloat16 [3072, 8192], P('seq', 'exp'), may hold values from -0.0625 to 0.0625
- router: bfloat16 [3072, 32], replicated, may hold values from -0.109375 to 0.109375
- expert_ids: int32 [2048, 2], P('seq'), may hold values from 0 to 31, all different within a row; in each aligned block of 128 rows (0 to 127, 128 to 255, ...) at most 12 rows name the same one
- up_weight: bfloat16 [32, 3072, 4608], P('exp', None, 'seq'), may hold values from -0.109375 to 0.109375
- down_weight: bfloat16 [32, 4608, 3072], P('exp', 'seq'), may hold values from -0.09375 to 0.09375
Outputs:
- layer_out: bfloat16 [2048, 3072], P(('seq', 'exp'))
Inputs may be any that keep to these rules, and one draw needn't show every extreme that they name: `expert_ids`: in each aligned block of 128 rows (one sequence block) no expert is named by more than 12 rows, a bound that some block reaches; a row names 2 different experts.
All inputs are finite; a program needn't handle non-finite values.
Results may differ from a plain program's by a relative error of at most 0.015.
Values may be sent and summed in bfloat16 or wider, within the bound.
No kernel may reach another device: no remote copies, remote signals or barrier semaphores. Data moves between devices by JAX's collectives and lax.ppermute only.
A program may use at most 64 MiB of HBM per device.

v0:
```python
import jax
import jax.numpy as jnp
from jax import lax
from jax.sharding import PartitionSpec as P


def prefix(x, axis, combine, identity):
    length, index = (lax.axis_size(axis), lax.axis_index(axis))
    everything = jax.tree.map(
        lambda part, kind: lax.all_gather(part.astype(kind), axis), x, (jnp.bfloat16, jnp.bfloat16)
    )
    start = jax.tree.map(
        lambda part, zero: jnp.broadcast_to(jnp.asarray(zero, part.dtype), part.shape), x, identity
    )

    def turn(k, before):
        reached = k < index
        new = combine(
            before, jax.tree.map(lambda part, own: part[k].astype(own.dtype), everything, x)
        )
        return jax.tree.map(lambda a, b: jnp.where(reached, a, b), new, before)

    return lax.fori_loop(0, length, turn, start)


def compose(earlier, later):
    return (earlier[0] * later[0], later[0][:, None, None] * earlier[1] + later[1])


def shards(
    queries,
    key_matrix,
    values,
    log_decay,
    residual,
    out_weight,
    router,
    expert_ids,
    up_weight,
    down_weight,
):
    rows = queries.shape[0]
    heads_here = log_decay.shape[0]
    width = queries.shape[1] // heads_here

    def split_heads(array):
        return array.astype(jnp.float32).reshape(rows, heads_here, width).transpose(1, 0, 2)

    qloc = split_heads(queries)
    kloc = split_heads(key_matrix)
    vloc = split_heads(values)
    cum = jnp.cumsum(log_decay, axis=1)
    last = cum[:, -1:]
    carry_decay = jnp.exp(last[:, 0])
    kscaled = kloc * jnp.exp(last - cum)[:, :, None]
    local_state = jnp.einsum("hjd,hje->hde", kscaled, vloc, precision=lax.Precision.HIGHEST)
    empty = jnp.zeros((heads_here, width, width), jnp.float32)
    _, state_in = prefix(
        (carry_decay, local_state), "seq", compose, (jnp.ones_like(carry_decay), empty)
    )
    lower = jnp.arange(rows)[:, None] >= jnp.arange(rows)[None, :]
    diff = cum[:, :, None] - cum[:, None, :]
    weight = jnp.where(lower[None], jnp.exp(jnp.where(lower[None], diff, 0.0)), 0.0)
    scores = jnp.einsum("hid,hjd->hij", qloc, kloc, precision=lax.Precision.HIGHEST) * weight
    inner = jnp.einsum("hij,hjd->hid", scores, vloc, precision=lax.Precision.HIGHEST)
    outer = jnp.exp(cum)[:, :, None] * jnp.einsum(
        "hid,hde->hie", qloc, state_in, precision=lax.Precision.HIGHEST
    )
    mixed = inner + outer
    mixed = mixed * lax.rsqrt(jnp.mean(mixed * mixed, axis=-1, keepdims=True) + 1e-06)
    attn = mixed.transpose(1, 0, 2).reshape(rows, heads_here * width).astype(jnp.bfloat16)
    stream = residual.astype(jnp.float32)
    normed = (stream * lax.rsqrt(jnp.mean(stream * stream, axis=-1, keepdims=True) + 1e-05)).astype(
        jnp.bfloat16
    )
    logits = jnp.dot(normed, router, preferred_element_type=jnp.float32)
    count_experts = router.shape[1]
    select_experts = (
        expert_ids[:, :, None] == jnp.arange(count_experts, dtype=jnp.int32)[None, None, :]
    )
    chosen = jnp.sum(jnp.where(select_experts, logits[:, None, :], 0.0), axis=-1)
    score = jax.nn.sigmoid(chosen)
    gates = score / jnp.sum(score, axis=1, keepdims=True)
    topk = expert_ids.shape[1]
    owner = lax.axis_index("exp")
    capacity = 3 * rows * topk // (2 * lax.axis_size("exp"))
    mine = (expert_ids.reshape(-1) == owner).astype(jnp.int32)
    ranks = jnp.cumsum(mine) - mine
    slot_pick = (ranks[None, :] == jnp.arange(capacity, dtype=jnp.int32)[:, None]) & (
        mine[None, :] == 1
    )
    slot_pick = slot_pick.astype(jnp.float32).reshape(capacity, rows, topk)
    token_pick = jnp.sum(slot_pick, axis=2).astype(jnp.bfloat16)
    slot_rows = jnp.dot(token_pick, normed, preferred_element_type=jnp.float32).astype(jnp.bfloat16)
    gathered_rows, full_weight = (
        lax.all_gather(slot_rows, "seq", axis=0, tiled=True),
        lax.all_gather(out_weight, "seq", axis=0, tiled=True),
    )
    projected = lax.dot_general(
        attn, full_weight, (((1,), (1,)), ((), ())), preferred_element_type=jnp.float32
    )
    hidden = jax.nn.silu(
        jnp.dot(gathered_rows, up_weight[0], preferred_element_type=jnp.float32)
    ).astype(jnp.bfloat16)
    expert_out = lax.psum_scatter(
        jnp.dot(hidden, down_weight[0], preferred_element_type=jnp.float32).astype(jnp.bfloat16),
        "seq",
        scatter_dimension=0,
        tiled=True,
    ).astype(jnp.float32)
    combine = jnp.einsum("cbk,bk->bc", slot_pick, gates, precision=lax.Precision.HIGHEST)
    contribution = jnp.dot(combine, expert_out, precision=lax.Precision.HIGHEST)
    summed = lax.psum_scatter(
        (projected + contribution).astype(jnp.bfloat16), "exp", scatter_dimension=0, tiled=True
    ).astype(jnp.float32)
    own_rows = summed.shape[0]
    own = lax.dynamic_slice_in_dim(stream, owner * own_rows, own_rows, 0)
    return (own + summed).astype(jnp.bfloat16)


def solution(mesh):
    in_specs = (
        P("seq", "exp"),
        P("seq", "exp"),
        P("seq", "exp"),
        P("exp", "seq"),
        P("seq", None),
        P("seq", "exp"),
        P(),
        P("seq", None),
        P("exp", None, "seq"),
        P("exp", "seq", None),
    )
    out_specs = P(("seq", "exp"), None)
    return jax.shard_map(shards, mesh=mesh, in_specs=in_specs, out_specs=out_specs, check_vma=False)
```

profile of v0, /device:TPU:6, one launch (start us, length us, event | category | flops | bytes accessed | tf_op | source)
XLA Modules:
  0.0 382.7 jit_solution(2274321475533020910)
XLA Ops:
  6.6 1.2 reduce_window_sum.27
  8.0 1.0 copy.68
  9.0 1.7 convolution_convert_fusion.2
  12.6 1.4 multiply_reduce_fusion
  14.0 1.0 fusion.3
  17.5 36.6 %all-reduce = bf16[32]{0:T(256)(128)(2,1)S(1)} all-reduce(bf16[32]{0:T(256)(128)(2,1)S(1)} %dynamic-update-slice), channel_id=2, replica_groups=mesh['seq'=16,'exp'=32] {'seq'}, use_global_device_ids=true, to_apply=%add | all-reduce | flops 32 | bytes 128
  55.6 30.3 %all-gather.9.cloned.1.call-done = bf16[32,128,128]{2,1,0:T(8,128)(2,1)} async-done(((bf16[2,128,128]{2,1,0:T(8,128)(2,1)}), bf16[32,128,128]{2,1,0:T(8,128)(2,1)}) %all-gather.9.cloned.1.call-update) | async-done | bytes 1048592 | tf_op jit(solution)/shard_map/all_gather | solution.py:10
  85.9 15.5 %while.14 = (s32[]{:T(128)}, f32[2,128,128]{2,1,0:T(8,128)S(1)}, s32[]{:T(128)}, bf16[16,2]{1,0:T(8,128)(2,1)S(1)}, bf16[16,2,128,128]{3,2,1,0:T(8,128)(2,1)}, /*index=5*/s32[]{:T(128)}, s32[]{:T(128)}) while((s32[]{:T(128)}, f32[2,128,128]{2,1,0:T(8,128)S(1)}, s32[]{:T(128)}, bf16[16,2]{1,0:T(8,128)(2,1)S(1)}, ...), condition=%wide.region_2.3_spmd.clone, body=%wide.region_1.2_spmd.clone.sunk | while | flops 163846 | bytes 327805 | solution.py:23
  102.1 55.1 %all-gather.11.cloned.1.call-done = bf16[16,12,3072]{2,1,0:T(8,128)(2,1)} async-done(((bf16[1,12,3072]{2,1,0:T(8,128)(2,1)}), bf16[16,12,3072]{2,1,0:T(8,128)(2,1)}) %all-gather.11.cloned.1.call-update) | async-done | bytes 1179664 | tf_op jit(solution)/shard_map/all_gather | solution.py:96
  157.1 2.3 reshape.178
  159.4 4.7 %convolution_convert_fusion = bf16[192,3072]{1,0:T(8,128)(2,1)} fusion(bf16[1,288,3072]{2,1,0:T(8,128)(2,1)S(1)} %copy-done, bf16[192,3072]{1,0:T(8,128)(2,1)} %reshape.178, bf16[1,3072,288]{1,2,0:T(8,128)(2,1)} %param.20), kind=kOutput, calls=%fused_computation.3 | convolution fusion | flops 680343552 | bytes 5898240 | tf_op jit(solution)/shard_map/dot_general | solution.py:106
  164.2 42.8 %fusion = bf16[16,3072]{1,0:T(8,128)(2,1)S(1)} fusion(bf16[192,3072]{1,0:T(8,128)(2,1)} %convolution_convert_fusion), kind=kCustom, calls=%all-reduce-scatter | all-reduce-scatter fusion | flops 786433 | bytes 1280000
  206.9 3.1 collective-permute-start
  210.1 9.0 %collective-permute-start.1 = (bf16[16,3072]{1,0:T(8,128)(2,1)S(1)}, bf16[16,3072]{1,0:T(8,128)(2,1)S(1)}, u32[]{:S(2)}, u32[]{:S(2)}) collective-permute-start(bf16[16,3072]{1,0:T(8,128)(2,1)S(1)} %fusion), channel_id=1, source_target_pairs={{0,64},{32,96},{64,128},{96,160},{128,192},{160,224},{192,256},{22... | collective-permute-start | bytes 294920
  219.0 4.6 %collective-permute-start.2 = (bf16[16,3072]{1,0:T(8,128)(2,1)S(1)}, bf16[16,3072]{1,0:T(8,128)(2,1)S(1)}, u32[]{:S(2)}, u32[]{:S(2)}) collective-permute-start(bf16[16,3072]{1,0:T(8,128)(2,1)S(1)} %fusion), channel_id=1, source_target_pairs={{0,96},{32,128},{64,160},{96,192},{128,224},{160,256},{192,288},{2... | collective-permute-start | bytes 294920
  223.7 4.2 %collective-permute-start.3 = (bf16[12,3072]{1,0:T(8,128)(2,1)S(1)}, bf16[12,3072]{1,0:T(8,128)(2,1)S(1)}, u32[]{:S(2)}, u32[]{:S(2)}) collective-permute-start(bf16[12,3072]{1,0:T(8,128)(2,1)S(1)} %slice.16), channel_id=1, source_target_pairs={{0,128},{32,160},{64,192},{96,224},{128,256},{160,288},{192,320},{... | collective-permute-start | bytes 221192
  227.9 2.2 collective-permute-done.3
  230.7 1.9 concatenate
  232.7 2.1 fusion.34
  234.7 1.8 fusion.2
  236.6 1.3 convert_element_type.97
  237.9 1.3 dynamic-slice.3
  239.8 134.8 %all-reduce.6.cloned.1.call-done = bf16[128,3072]{1,0:T(8,128)(2,1)} async-done(((bf16[128,3072]{1,0:T(8,128)(2,1)}), bf16[128,3072]{1,0:T(8,128)(2,1)}) %all-reduce.6.cloned.1.call-update) | async-done | bytes 786448
  374.7 1.5 add_convert_fusion
  (94 shorter events, 21.3 us)
Async XLA Ops:
  6.5 152.9 %copy-start = (bf16[1,288,3072]{2,1,0:T(8,128)(2,1)S(1)}, bf16[1,288,3072]{2,1,0:T(8,128)(2,1)}, u32[]{:S(2)}) copy-start(bf16[1,288,3072]{2,1,0:T(8,128)(2,1)} %param.21) | copy-start | bytes 5308420
  6.5 9.5 %copy-start.6 = (u32[512]{0:T(512)S(1)}, u32[512]{0:T(512)}, u32[]{:S(2)}) copy-start(u32[512]{0:T(512)} %constant.67) | copy-start | bytes 6148
  6.5 7.5 %copy-start.1 = (bf16[128,3072]{1,0:T(8,128)(2,1)S(1)}, bf16[128,3072]{1,0:T(8,128)(2,1)}, u32[]{:S(2)}) copy-start(bf16[128,3072]{1,0:T(8,128)(2,1)} %param.16) | copy-start | bytes 2359300
  6.5 47.6 %copy-start.7 = (bf16[3072,32]{0,1:T(8,128)(2,1)S(1)}, bf16[3072,32]{0,1:T(8,128)(2,1)}, u32[]{:S(2)}) copy-start(bf16[3072,32]{0,1:T(8,128)(2,1)} %param.18) | copy-start | bytes 589828
  6.5 79.4 %all-gather.9.cloned.1.call-start = ((), (), s32[]{:S(2)}) async-start(), calls=%async_computation.1 | async-start | bytes 1114112 | tf_op jit(solution)/shard_map/all_gather | solution.py:10
  10.7 146.5 %all-gather.11.cloned.1.call-start = ((), (), s32[]{:S(2)}) async-start(), calls=%async_computation.2 | async-start | bytes 1671168 | tf_op jit(solution)/shard_map/all_gather | solution.py:96
  12.2 42.4 %copy-start.5 = (s32[128,2]{0,1:T(2,128)S(1)}, s32[128,2]{0,1:T(2,128)}, u32[]{:S(2)}) copy-start(s32[128,2]{0,1:T(2,128)} %param.19) | copy-start | bytes 3076
  12.2 42.5 %copy-start.4 = (bf16[128,256]{1,0:T(8,128)(2,1)S(1)}, bf16[128,256]{1,0:T(8,128)(2,1)}, u32[]{:S(2)}) copy-start(bf16[128,256]{1,0:T(8,128)(2,1)} %param.12) | copy-start | bytes 196612
  15.0 217.7 %all-gather.7.cloned.1.call-start = ((), (), s32[]{:S(2)}) async-start(), calls=%async_computation | async-start | bytes 1671168 | tf_op jit(solution)/shard_map/all_gather | solution.py:97
  15.7 358.9 %all-reduce.6.cloned.1.call-start = ((), (), s32[]{:S(2)}) async-start(), calls=%async_computation.3 | async-start | bytes 1572864
  54.6 47.1 %copy-start.2 = (bf16[128,256]{1,0:T(8,128)(2,1)S(1)}, bf16[128,256]{1,0:T(8,128)(2,1)}, u32[]{:S(2)}) copy-start(bf16[128,256]{1,0:T(8,128)(2,1)} %param.14) | copy-start | bytes 196612
  206.9 23.1 %collective-permute-start = (bf16[16,3072]{1,0:T(8,128)(2,1)S(1)}, bf16[16,3072]{1,0:T(8,128)(2,1)S(1)}, u32[]{:S(2)}, u32[]{:S(2)}) collective-permute-start(bf16[16,3072]{1,0:T(8,128)(2,1)S(1)} %fusion), channel_id=1, source_target_pairs={{0,32},{32,64},{64,96},{96,128},{128,160},{160,192},{192,224},{224... | collective-permute-start | bytes 294920
  210.1 20.0 %collective-permute-start.1 = (bf16[16,3072]{1,0:T(8,128)(2,1)S(1)}, bf16[16,3072]{1,0:T(8,128)(2,1)S(1)}, u32[]{:S(2)}, u32[]{:S(2)}) collective-permute-start(bf16[16,3072]{1,0:T(8,128)(2,1)S(1)} %fusion), channel_id=1, source_target_pairs={{0,64},{32,96},{64,128},{96,160},{128,192},{160,224},{192,256},{22... | collective-permute-start | bytes 294920
  219.0 11.7 %collective-permute-start.2 = (bf16[16,3072]{1,0:T(8,128)(2,1)S(1)}, bf16[16,3072]{1,0:T(8,128)(2,1)S(1)}, u32[]{:S(2)}, u32[]{:S(2)}) collective-permute-start(bf16[16,3072]{1,0:T(8,128)(2,1)S(1)} %fusion), channel_id=1, source_target_pairs={{0,96},{32,128},{64,160},{96,192},{128,224},{160,256},{192,288},{2... | collective-permute-start | bytes 294920
  223.7 6.4 %collective-permute-start.3 = (bf16[12,3072]{1,0:T(8,128)(2,1)S(1)}, bf16[12,3072]{1,0:T(8,128)(2,1)S(1)}, u32[]{:S(2)}, u32[]{:S(2)}) collective-permute-start(bf16[12,3072]{1,0:T(8,128)(2,1)S(1)} %slice.16), channel_id=1, source_target_pairs={{0,128},{32,160},{64,192},{96,224},{128,256},{160,288},{192,320},{... | collective-permute-start | bytes 221192
  230.1 0.6 copy-start.3
Sparse Core Ops, SparseCore 0:
  10.8 75.1 all-gather.8
  88.0 69.0 all-gather.10
  159.2 72.1 all-gather.6
  236.7 137.9 all-reduce.5
where the time goes:
time: 384 us; the launch traced here: 383 us
  waiting for transfers between devices  223 us (58%)
  blocking collectives  79.3 us (21%)
  other arithmetic  21.9 us (6%)
  starting transfers between devices  21.1 us (5%)
  between operations  15.3 us (4%)
  matrix products  12.4 us (3%)
  local copies, waits for them, and re-layouts  9.14 us (2%)
    unnamed x9, waiting for transfers between devices  138 us
    unnamed x2, blocking collectives  79.3 us
    all_gather x1, waiting for transfers between devices, shards(): lax.all_gather(slot_rows, 'seq', axis=0, tiled=True)  55.1 us
    all_gather x1, waiting for transfers between devices, prefix(): lax.all_gather(part.astype(kind), axis)  30.3 us
    unnamed x5, starting transfers between devices  21 us
    select_n x16, other arithmetic, turn(): return jax.tree.map(lambda a, b: jnp.where(reached, a, b), new, before)  14.9 us
  transfers between devices with their start and end apart: 8, of which 4 were waited for; matrix products, arithmetic and copies ran while one was open for 20% of the time, Pallas kernels for 0%

commit v1 on v0

v1 whole, which is shorter than its diff:
```python
import jax
import jax.numpy as jnp
from jax import lax
from jax.sharding import PartitionSpec as P


def halving_scatter(x, axis):
    n = x.shape[0]
    me = lax.axis_index(axis)
    buf = x
    for k in range(n.bit_length() - 1):
        half = buf.reshape(buf.shape[0] // 2, 2, *buf.shape[1:])
        upper = ((me >> k) & 1) == 1
        keep = jnp.where(upper, half[:, 1], half[:, 0])
        send = jnp.where(upper, half[:, 0], half[:, 1])
        got = lax.ppermute(send, axis, [(i, i ^ (1 << k)) for i in range(n)])
        buf = keep + got
    return buf[0]


def shards(
    queries,
    key_matrix,
    values,
    log_decay,
    residual,
    out_weight,
    router,
    expert_ids,
    up_weight,
    down_weight,
):
    rows = queries.shape[0]
    heads_here = log_decay.shape[0]
    width = queries.shape[1] // heads_here
    n_seq = lax.axis_size("seq")
    n_exp = lax.axis_size("exp")
    me_seq = lax.axis_index("seq")
    owner = lax.axis_index("exp")

    def split_heads(array):
        return array.astype(jnp.float32).reshape(rows, heads_here, width).transpose(1, 0, 2)

    qloc = split_heads(queries)
    kloc = split_heads(key_matrix)
    vloc = split_heads(values)
    cum = jnp.cumsum(log_decay, axis=1)
    last = cum[:, -1:]
    carry_decay = jnp.exp(last[:, 0])
    kscaled = kloc * jnp.exp(last - cum)[:, :, None]
    local_state = jnp.einsum("hjd,hje->hde", kscaled, vloc, precision=lax.Precision.HIGHEST)

    stream = residual.astype(jnp.float32)
    normed = (stream * lax.rsqrt(jnp.mean(stream * stream, axis=-1, keepdims=True) + 1e-05)).astype(
        jnp.bfloat16
    )
    logits = jnp.dot(normed, router, preferred_element_type=jnp.float32)
    count_experts = router.shape[1]
    select_experts = (
        expert_ids[:, :, None] == jnp.arange(count_experts, dtype=jnp.int32)[None, None, :]
    )
    chosen = jnp.sum(jnp.where(select_experts, logits[:, None, :], 0.0), axis=-1)
    score = jax.nn.sigmoid(chosen)
    gates = score / jnp.sum(score, axis=1, keepdims=True)
    topk = expert_ids.shape[1]
    capacity = 3 * rows * topk // (2 * n_exp)
    mine = (expert_ids.reshape(-1) == owner).astype(jnp.int32)
    ranks = jnp.cumsum(mine) - mine
    slot_pick = (ranks[None, :] == jnp.arange(capacity, dtype=jnp.int32)[:, None]) & (
        mine[None, :] == 1
    )
    slot_pick = slot_pick.astype(jnp.float32).reshape(capacity, rows, topk)
    token_pick = jnp.sum(slot_pick, axis=2).astype(jnp.bfloat16)
    slot_rows = jnp.dot(token_pick, normed, preferred_element_type=jnp.float32).astype(jnp.bfloat16)

    decay_hi = carry_decay.astype(jnp.bfloat16)
    decay_lo = (carry_decay - decay_hi.astype(jnp.float32)).astype(jnp.bfloat16)
    lane = 128
    pieces = [
        local_state.astype(jnp.bfloat16).reshape(-1),
        slot_rows.reshape(-1),
        out_weight.reshape(-1),
        jnp.pad(jnp.concatenate([decay_hi, decay_lo]), (0, lane - 2 * heads_here)),
    ]
    sizes = [p.shape[0] for p in pieces]
    flat = jnp.concatenate(pieces)
    total = flat.shape[0]
    padded = -(-total // (16 * lane)) * (16 * lane)
    flat = jnp.pad(flat, (0, padded - total)).reshape(padded // lane, lane)
    gathered = lax.all_gather(flat, "seq", axis=0, tiled=False).reshape(n_seq, padded)
    offsets = [sum(sizes[:i]) for i in range(len(sizes))]
    states = gathered[:, offsets[0] : offsets[0] + sizes[0]].reshape(n_seq, heads_here, width, width)
    gathered_rows = gathered[:, offsets[1] : offsets[1] + sizes[1]].reshape(
        n_seq * capacity, normed.shape[1]
    )
    full_weight = gathered[:, offsets[2] : offsets[2] + sizes[2]].reshape(
        n_seq * out_weight.shape[0], out_weight.shape[1]
    )
    decays = gathered[:, offsets[3] : offsets[3] + 2 * heads_here].astype(jnp.float32)
    decays = decays[:, :heads_here] + decays[:, heads_here:]

    blocks = jnp.arange(n_seq)
    between = (blocks[:, None] < blocks[None, :]) & (blocks[None, :] < me_seq)
    factors = jnp.where(between[:, :, None], decays[None, :, :], 1.0)
    reach = jnp.where((blocks < me_seq)[:, None], jnp.prod(factors, axis=1), 0.0)
    state_in = jnp.einsum(
        "jh,jhde->hde", reach, states.astype(jnp.float32), precision=lax.Precision.HIGHEST
    )

    lower = jnp.arange(rows)[:, None] >= jnp.arange(rows)[None, :]
    diff = cum[:, :, None] - cum[:, None, :]
    weight = jnp.where(lower[None], jnp.exp(jnp.where(lower[None], diff, 0.0)), 0.0)
    scores = jnp.einsum("hid,hjd->hij", qloc, kloc, precision=lax.Precision.HIGHEST) * weight
    inner = jnp.einsum("hij,hjd->hid", scores, vloc, precision=lax.Precision.HIGHEST)
    outer = jnp.exp(cum)[:, :, None] * jnp.einsum(
        "hid,hde->hie", qloc, state_in, precision=lax.Precision.HIGHEST
    )
    mixed = inner + outer
    mixed = mixed * lax.rsqrt(jnp.mean(mixed * mixed, axis=-1, keepdims=True) + 1e-06)
    attn = mixed.transpose(1, 0, 2).reshape(rows, heads_here * width).astype(jnp.bfloat16)

    projected = lax.dot_general(
        attn, full_weight, (((1,), (1,)), ((), ())), preferred_element_type=jnp.float32
    )
    hidden = jax.nn.silu(
        jnp.dot(gathered_rows, up_weight[0], preferred_element_type=jnp.float32)
    ).astype(jnp.bfloat16)
    expert_part = jnp.dot(hidden, down_weight[0], preferred_element_type=jnp.float32)
    expert_out = lax.psum_scatter(
        expert_part.astype(jnp.bfloat16).reshape(n_seq, capacity, -1),
        "seq",
        scatter_dimension=0,
        tiled=True,
    )[0].astype(jnp.float32)
    combine = jnp.einsum("cbk,bk->bc", slot_pick, gates, precision=lax.Precision.HIGHEST)
    contribution = jnp.dot(combine, expert_out, precision=lax.Precision.HIGHEST)
    partial = (projected + contribution).reshape(n_exp, rows // n_exp, -1)
    summed = halving_scatter(partial, "exp")
    own_rows = summed.shape[0]
    own = lax.dynamic_slice_in_dim(stream, owner * own_rows, own_rows, 0)
    return (own + summed).astype(jnp.bfloat16)


def solution(mesh):
    in_specs = (
        P("seq", "exp"),
        P("seq", "exp"),
        P("seq", "exp"),
        P("exp", "seq"),
        P("seq", None),
        P("seq", "exp"),
        P(),
        P("seq", None),
        P("exp", None, "seq"),
        P("exp", "seq", None),
    )
    out_specs = P(("seq", "exp"), None)
    return jax.shard_map(shards, mesh=mesh, in_specs=in_specs, out_specs=out_specs, check_vma=False)
```

time: 384 us -> 239 us (0.62)
  blocking collectives: 79.3 us -> 0 us
  waiting for transfers between devices: 223 us -> 158 us
  local copies, waits for them, and re-layouts: 9.14 us -> 20.6 us
  other arithmetic: 21.9 us -> 14.4 us
  starting transfers between devices: 21.1 us -> 16.3 us
    unnamed x9 -> x2, waiting for transfers between devices: 138 us -> 0.03 us
    unnamed x2 -> x0, blocking collectives: 79.3 us -> none
    reduce_scatter x0 -> x1, waiting for transfers between devices: none -> 53.4 us  [shards(): lax.psum_scatter(expert_part.astype(jnp.bfloat16).reshape(n_seq, capacity...]
    ppermute x0 -> x5, waiting for transfers between devices: none -> 23.4 us  [halving_scatter(): got = lax.ppermute(send, axis, [(i, i ^ 1 << k) for i in range(n)])]
    unnamed x5 -> x0, starting transfers between devices: 21 us -> none
    ppermute x0 -> x5, starting transfers between devices: none -> 16.3 us  [halving_scatter(): got = lax.ppermute(send, axis, [(i, i ^ 1 << k) for i in range(n)])]
    select_n x16 -> x6, other arithmetic: 14.9 us -> 1.99 us  [the longest x5 1.29 us: halving_scatter(): send = jnp.where(upper, half[:, 0], half[:, 1])]
    reshape x0 -> x4, local copies, waits for them, and re-layouts: none -> 5.9 us  [the longest x1 2.65 us: shards(): gathered[:, offsets[1]:offsets[1] + sizes[1]]]
  transfers between devices with their start and end apart: 8 -> 7, of which waited for: 4 -> 7; matrix products, arithmetic and copies ran while one was open for 20% -> 8% of each run, Pallas kernels for 0% -> 0%
where the time goes in v1:
time: 239 us
  waiting for transfers between devices  158 us (66%)
  local copies, waits for them, and re-layouts  20.6 us (9%)
  starting transfers between devices  16.3 us (7%)
  matrix products  15.5 us (6%)
  other arithmetic  14.4 us (6%)
  between operations  13.8 us (6%)
    all_gather x1, waiting for transfers between devices, shards(): lax.all_gather(flat, 'seq', axis=0, tiled=False).reshape(n_seq, padded)  81.1 us
    reduce_scatter x1, waiting for transfers between devices, shards(): lax.psum_scatter(expert_part.astype(jnp.bfloat16).reshape(n_seq, capacity...  53.4 us
    ppermute x5, waiting for transfers between devices, halving_scatter(): got = lax.ppermute(send, axis, [(i, i ^ 1 << k) for i in range(n)])  23.4 us
    ppermute x5, starting transfers between devices, halving_scatter(): got = lax.ppermute(send, axis, [(i, i ^ 1 << k) for i in range(n)])  16.3 us
    unnamed x28, local copies, waits for them, and re-layouts  8.41 us
  transfers between devices with their start and end apart: 7, of which 7 were waited for; matrix products, arithmetic and copies ran while one was open for 8% of the time, Pallas kernels for 0%

profile of v1, /device:TPU:6, one launch (start us, length us, event | category | flops | bytes accessed | tf_op | source)
XLA Modules:
  0.0 238.6 jit_solution(17452435743436337508)
XLA Ops:
  11.9 1.5 convolution_convert_fusion.1
  15.6 81.1 %all-gather.2.cloned.1.call-done = bf16[16,944,128]{2,1,0:T(8,128)(2,1)} async-done(((bf16[1,944,128]{2,1,0:T(8,128)(2,1)}), bf16[16,944,128]{2,1,0:T(8,128)(2,1)}) %all-gather.2.cloned.1.call-update) | async-done | bytes 3866640 | tf_op jit(solution)/shard_map/all_gather | solution.py:90
  96.7 3.1 %copy.212 = bf16[2,8,944,128]{3,1,2,0:T(8,128)(2,1)S(1)} copy(bf16[2,8,944,128]{3,2,1,0:T(8,128)(2,1)} %bitcast.201) | data formatting | bytes 7733248
  99.8 1.8 copy-done.1
  101.8 2.7 %reshape.280 = bf16[192,3072]{1,0:T(8,128)(2,1)} reshape(bf16[16,36864]{1,0:T(8,128)(2,1)S(1)} %slice.95) | data formatting | bytes 2359296 | tf_op jit(solution)/shard_map/reshape | solution.py:93
  104.4 3.7 %convolution_convert_fusion = bf16[192,3072]{1,0:T(8,128)(2,1)S(1)} fusion(bf16[1,288,3072]{2,1,0:T(8,128)(2,1)S(1)} %copy-done, bf16[192,3072]{1,0:T(8,128)(2,1)} %reshape.280, bf16[1,3072,288]{1,2,0:T(8,128)(2,1)} %param.18), kind=kOutput, calls=%fused_computation.1 | convolution fusion | flops 680343552 | bytes 5898240 | tf_op jit(solution)/shard_map/dot_general | solution.py:128
  110.1 2.7 %slice.94 = bf16[16,49152]{1,0:T(8,128)(2,1)} slice(bf16[16,120832]{1,0:T(8,128)(2,1)} %bitcast.196), slice={[0:16], [69632:118784]} | slice | bytes 3145728 | tf_op jit(solution)/shard_map/slice | solution.py:96
  116.0 1.9 reshape.279
  119.4 2.2 fusion.3
  123.8 1.8 fusion.47
  125.6 53.4 %reduce-scatter.2.cloned.1.call-done = bf16[1,12,3072]{2,1,0:T(8,128)(2,1)} async-done(((bf16[16,12,3072]{2,1,0:T(8,128)(2,1)}), bf16[1,12,3072]{2,1,0:T(8,128)(2,1)}) %reduce-scatter.2.cloned.1.call-update) | async-done | bytes 73744 | tf_op jit(solution)/shard_map/reduce_scatter | solution.py:129
  179.0 3.4 %convolution_add_fusion = f32[128,3072]{1,0:T(8,128)} fusion(f32[128,3072]{1,0:T(8,128)} %fusion.47, f32[128,12]{0,1:T(8,128)S(1)} %fusion.42, bf16[1,12,3072]{2,1,0:T(8,128)(2,1)} %reduce-scatter.2.cloned.1.call-done), kind=kOutput, calls=%fused_computation.2 | convolution fusion | flops 57016320 | bytes 3225600 | tf_op jit(solution)/shard_map/dot_general | solution.py:136
  182.4 1.8 reshape_reshape.3
  185.3 1.9 collective-permute-start
  187.2 2.6 %collective-permute-done = f32[16,4,3072]{2,1,0:T(4,128)} collective-permute-done((f32[16,4,3072]{2,1,0:T(4,128)}, f32[16,4,3072]{2,1,0:T(4,128)}, u32[]{:S(2)}, u32[]{:S(2)}) %collective-permute-start) | collective-permute-done | bytes 786464 | tf_op jit(solution)/shard_map/ppermute | solution.py:16
  192.2 3.4 %collective-permute-start.1 = (f32[8,4,3072]{2,1,0:T(4,128)S(1)}, f32[8,4,3072]{2,1,0:T(4,128)S(1)}, u32[]{:S(2)}, u32[]{:S(2)}) collective-permute-start(f32[8,4,3072]{2,1,0:T(4,128)S(1)} %select_bitcast_fusion.1), channel_id=1, source_target_pairs={{0,2},{1,3},{2,0},{3,1},{4,6},{5,7},{6,4},{7,5},{8,10},{9,11},{10,... | collective-permute-start | bytes 1179656 | tf_op jit(solution)/shard_map/ppermute | solution.py:16
  195.6 9.6 %collective-permute-done.1 = f32[8,4,3072]{2,1,0:T(4,128)S(1)} collective-permute-done((f32[8,4,3072]{2,1,0:T(4,128)S(1)}, f32[8,4,3072]{2,1,0:T(4,128)S(1)}, u32[]{:S(2)}, u32[]{:S(2)}) %collective-permute-start.1) | collective-permute-done | bytes 393248 | tf_op jit(solution)/shard_map/ppermute | solution.py:16
  206.6 4.9 %collective-permute-start.2 = (f32[4,4,3072]{2,1,0:T(4,128)S(1)}, f32[4,4,3072]{2,1,0:T(4,128)S(1)}, u32[]{:S(2)}, u32[]{:S(2)}) collective-permute-start(f32[4,4,3072]{2,1,0:T(4,128)S(1)} %select_bitcast_fusion.2), channel_id=1, source_target_pairs={{0,4},{1,5},{2,6},{3,7},{4,0},{5,1},{6,2},{7,3},{8,12},{9,13},{10,... | collective-permute-start | bytes 589832 | tf_op jit(solution)/shard_map/ppermute | solution.py:16
  211.5 4.6 %collective-permute-done.2 = f32[4,4,3072]{2,1,0:T(4,128)S(1)} collective-permute-done((f32[4,4,3072]{2,1,0:T(4,128)S(1)}, f32[4,4,3072]{2,1,0:T(4,128)S(1)}, u32[]{:S(2)}, u32[]{:S(2)}) %collective-permute-start.2) | collective-permute-done | bytes 196640 | tf_op jit(solution)/shard_map/ppermute | solution.py:16
  216.2 2.7 %collective-permute-start.3 = (f32[2,4,3072]{2,1,0:T(4,128)S(1)}, f32[2,4,3072]{2,1,0:T(4,128)S(1)}, u32[]{:S(2)}, u32[]{:S(2)}) collective-permute-start(f32[2,4,3072]{2,1,0:T(4,128)S(1)} %select_bitcast_fusion.3), channel_id=1, source_target_pairs={{0,8},{1,9},{2,10},{3,11},{4,12},{5,13},{6,14},{7,15},{8,0},{9,1},... | collective-permute-start | bytes 294920 | tf_op jit(solution)/shard_map/ppermute | solution.py:16
  218.9 3.8 %collective-permute-done.3 = f32[2,4,3072]{2,1,0:T(4,128)S(1)} collective-permute-done((f32[2,4,3072]{2,1,0:T(4,128)S(1)}, f32[2,4,3072]{2,1,0:T(4,128)S(1)}, u32[]{:S(2)}, u32[]{:S(2)}) %collective-permute-start.3) | collective-permute-done | bytes 98336 | tf_op jit(solution)/shard_map/ppermute | solution.py:16
  222.8 3.4 %collective-permute-start.4 = (f32[1,4,3072]{2,1,0:T(4,128)S(1)}, f32[1,4,3072]{2,1,0:T(4,128)S(1)}, u32[]{:S(2)}, u32[]{:S(2)}) collective-permute-start(f32[1,4,3072]{2,1,0:T(4,128)S(1)} %select_bitcast_fusion.4), channel_id=1, source_target_pairs={{0,16},{1,17},{2,18},{3,19},{4,20},{5,21},{6,22},{7,23},{8,24},{9,... | collective-permute-start | bytes 147464 | tf_op jit(solution)/shard_map/ppermute | solution.py:16
  227.5 2.8 %collective-permute-done.4 = f32[1,4,3072]{2,1,0:T(4,128)S(1)} collective-permute-done((f32[1,4,3072]{2,1,0:T(4,128)S(1)}, f32[1,4,3072]{2,1,0:T(4,128)S(1)}, u32[]{:S(2)}, u32[]{:S(2)}) %collective-permute-start.4) | collective-permute-done | bytes 49184 | tf_op jit(solution)/shard_map/ppermute | solution.py:16
  230.3 1.5 fusion.41
  (84 shorter events, 22.5 us)
Async XLA Ops:
  6.5 97.9 %copy-start = (bf16[1,288,3072]{2,1,0:T(8,128)(2,1)S(1)}, bf16[1,288,3072]{2,1,0:T(8,128)(2,1)}, u32[]{:S(2)}) copy-start(bf16[1,288,3072]{2,1,0:T(8,128)(2,1)} %param.19) | copy-start | bytes 5308420
  6.5 6.9 %copy-start.8 = (bf16[128,256]{1,0:T(8,128)(2,1)S(1)}, bf16[128,256]{1,0:T(8,128)(2,1)}, u32[]{:S(2)}) copy-start(bf16[128,256]{1,0:T(8,128)(2,1)} %param.11) | copy-start | bytes 196612
  6.5 7.0 %copy-start.6 = (bf16[192,256]{1,0:T(8,128)(2,1)S(1)}, bf16[192,256]{1,0:T(8,128)(2,1)}, u32[]{:S(2)}) copy-start(bf16[192,256]{1,0:T(8,128)(2,1)} %param.15) | copy-start | bytes 294916
  6.5 7.2 %copy-start.5 = (bf16[128,256]{1,0:T(8,128)(2,1)S(1)}, bf16[128,256]{1,0:T(8,128)(2,1)}, u32[]{:S(2)}) copy-start(bf16[128,256]{1,0:T(8,128)(2,1)} %param.12) | copy-start | bytes 196612
  6.5 90.2 %all-gather.2.cloned.1.call-start = ((), (), s32[]{:S(2)}) async-start(), calls=%async_computation.1 | async-start | bytes 4108288 | tf_op jit(solution)/shard_map/all_gather | solution.py:90
  10.3 4.5 %copy-start.2 = (bf16[128,3072]{1,0:T(8,128)(2,1)S(1)}, bf16[128,3072]{1,0:T(8,128)(2,1)}, u32[]{:S(2)}) copy-start(bf16[128,3072]{1,0:T(8,128)(2,1)} %param.14) | copy-start | bytes 2359300
  10.3 4.5 %copy-start.11 = (bf16[3072,32]{0,1:T(8,128)(2,1)S(1)}, bf16[3072,32]{0,1:T(8,128)(2,1)}, u32[]{:S(2)}) copy-start(bf16[3072,32]{0,1:T(8,128)(2,1)} %param.16) | copy-start | bytes 589828
  11.9 3.4 %copy-start.9 = (s32[128,2]{0,1:T(2,128)S(1)}, s32[128,2]{0,1:T(2,128)}, u32[]{:S(2)}) copy-start(s32[128,2]{0,1:T(2,128)} %param.17) | copy-start | bytes 3076
  11.9 3.5 %copy-start.7 = (bf16[128,256]{1,0:T(8,128)(2,1)S(1)}, bf16[128,256]{1,0:T(8,128)(2,1)}, u32[]{:S(2)}) copy-start(bf16[128,256]{1,0:T(8,128)(2,1)} %param.10) | copy-start | bytes 196612
  14.7 164.3 %reduce-scatter.2.cloned.1.call-start = ((), (), s32[]{:S(2)}) async-start(), calls=%async_computation.2 | async-start | bytes 1671168 | tf_op jit(solution)/shard_map/reduce_scatter | solution.py:129
  14.8 85.0 %copy-start.10 = (pred[16]{0:T(512)(128)(4,1)}, pred[16]{0:T(512)(128)(4,1)S(1)}, u32[]{:S(2)}) copy-start(pred[16]{0:T(512)(128)(4,1)S(1)} %iota_compare_fusion.4) | copy-start | bytes 52
  99.8 1.9 copy-start.1
  185.3 4.5 %collective-permute-start = (f32[16,4,3072]{2,1,0:T(4,128)}, f32[16,4,3072]{2,1,0:T(4,128)}, u32[]{:S(2)}, u32[]{:S(2)}) collective-permute-start(f32[16,4,3072]{2,1,0:T(4,128)} %select_bitcast_fusion), channel_id=1, source_target_pairs={{0,1},{1,0},{2,3},{3,2},{4,5},{5,4},{6,7},{7,6},{8,9},{9,8},{10,11... | collective-permute-start | bytes 2359304 | tf_op jit(solution)/shard_map/ppermute | solution.py:16
  191.2 0.9 copy-start.4
  192.2 13.1 %collective-permute-start.1 = (f32[8,4,3072]{2,1,0:T(4,128)S(1)}, f32[8,4,3072]{2,1,0:T(4,128)S(1)}, u32[]{:S(2)}, u32[]{:S(2)}) collective-permute-start(f32[8,4,3072]{2,1,0:T(4,128)S(1)} %select_bitcast_fusion.1), channel_id=1, source_target_pairs={{0,2},{1,3},{2,0},{3,1},{4,6},{5,7},{6,4},{7,5},{8,10},{9,11},{10,... | collective-permute-start | bytes 1179656 | tf_op jit(solution)/shard_map/ppermute | solution.py:16
  195.6 30.6 %copy-start.3 = (bf16[128,3072]{1,0:T(8,128)(2,1)S(1)}, bf16[128,3072]{1,0:T(8,128)(2,1)}, u32[]{:S(2)}) copy-start(bf16[128,3072]{1,0:T(8,128)(2,1)} %param.14) | copy-start | bytes 2359300
  206.6 9.5 %collective-permute-start.2 = (f32[4,4,3072]{2,1,0:T(4,128)S(1)}, f32[4,4,3072]{2,1,0:T(4,128)S(1)}, u32[]{:S(2)}, u32[]{:S(2)}) collective-permute-start(f32[4,4,3072]{2,1,0:T(4,128)S(1)} %select_bitcast_fusion.2), channel_id=1, source_target_pairs={{0,4},{1,5},{2,6},{3,7},{4,0},{5,1},{6,2},{7,3},{8,12},{9,13},{10,... | collective-permute-start | bytes 589832 | tf_op jit(solution)/shard_map/ppermute | solution.py:16
  216.2 6.5 %collective-permute-start.3 = (f32[2,4,3072]{2,1,0:T(4,128)S(1)}, f32[2,4,3072]{2,1,0:T(4,128)S(1)}, u32[]{:S(2)}, u32[]{:S(2)}) collective-permute-start(f32[2,4,3072]{2,1,0:T(4,128)S(1)} %select_bitcast_fusion.3), channel_id=1, source_target_pairs={{0,8},{1,9},{2,10},{3,11},{4,12},{5,13},{6,14},{7,15},{8,0},{9,1},... | collective-permute-start | bytes 294920 | tf_op jit(solution)/shard_map/ppermute | solution.py:16
  222.8 7.5 %collective-permute-start.4 = (f32[1,4,3072]{2,1,0:T(4,128)S(1)}, f32[1,4,3072]{2,1,0:T(4,128)S(1)}, u32[]{:S(2)}, u32[]{:S(2)}) collective-permute-start(f32[1,4,3072]{2,1,0:T(4,128)S(1)} %select_bitcast_fusion.4), channel_id=1, source_target_pairs={{0,16},{1,17},{2,18},{3,19},{4,20},{5,21},{6,22},{7,23},{8,24},{9,... | collective-permute-start | bytes 147464 | tf_op jit(solution)/shard_map/ppermute | solution.py:16
Sparse Core Ops, SparseCore 0:
  14.8 81.8 all-gather.1
  109.5 69.4 reduce-scatter.1

commit v2 on v1

--- a/solution.py
+++ b/solution.py
@@ -13,8 +13,8 @@
         upper = ((me >> k) & 1) == 1
         keep = jnp.where(upper, half[:, 1], half[:, 0])
         send = jnp.where(upper, half[:, 0], half[:, 1])
-        got = lax.ppermute(send, axis, [(i, i ^ (1 << k)) for i in range(n)])
-        buf = keep + got
+        got = lax.ppermute(send.astype(jnp.bfloat16), axis, [(i, i ^ (1 << k)) for i in range(n)])
+        buf = keep + got.astype(keep.dtype)
     return buf[0]
 
 
@@ -64,39 +64,50 @@
     gates = score / jnp.sum(score, axis=1, keepdims=True)
     topk = expert_ids.shape[1]
     capacity = 3 * rows * topk // (2 * n_exp)
+    slots = -(-capacity // 16) * 16
     mine = (expert_ids.reshape(-1) == owner).astype(jnp.int32)
     ranks = jnp.cumsum(mine) - mine
-    slot_pick = (ranks[None, :] == jnp.arange(capacity, dtype=jnp.int32)[:, None]) & (
+    slot_pick = (ranks[None, :] == jnp.arange(slots, dtype=jnp.int32)[:, None]) & (
         mine[None, :] == 1
     )
-    slot_pick = slot_pick.astype(jnp.float32).reshape(capacity, rows, topk)
+    slot_pick = slot_pick.astype(jnp.float32).reshape(slots, rows, topk)
     token_pick = jnp.sum(slot_pick, axis=2).astype(jnp.bfloat16)
     slot_rows = jnp.dot(token_pick, normed, preferred_element_type=jnp.float32).astype(jnp.bfloat16)
 
+    model = normed.shape[1]
     decay_hi = carry_decay.astype(jnp.bfloat16)
     decay_lo = (carry_decay - decay_hi.astype(jnp.float32)).astype(jnp.bfloat16)
-    lane = 128
+
+    def as_slab(v):
+        v = v.reshape(-1)
+        r = -(-v.shape[0] // model)
+        return jnp.pad(v, (0, r * model - v.shape[0])).reshape(r, model)
+
     pieces = [
-        local_state.astype(jnp.bfloat16).reshape(-1),
-        slot_rows.reshape(-1),
-        out_weight.reshape(-1),
-        jnp.pad(jnp.concatenate([decay_hi, decay_lo]), (0, lane - 2 * heads_here)),
+        slot_rows,
+        as_slab(out_weight),
+        as_slab(local_state.astype(jnp.bfloat16)),
+        as_slab(jnp.concatenate([decay_hi, decay_lo])),
     ]
     sizes = [p.shape[0] for p in pieces]
-    flat = jnp.concatenate(pieces)
-    total = flat.shape[0]
-    padded = -(-total // (16 * lane)) * (16 * lane)
-    flat = jnp.pad(flat, (0, padded - total)).reshape(padded // lane, lane)
-    gathered = lax.all_gather(flat, "seq", axis=0, tiled=False).reshape(n_seq, padded)
+    slab = jnp.concatenate(pieces)
+    total = slab.shape[0]
+    padded = -(-total // 16) * 16
+    slab = jnp.pad(slab, ((0, padded - total), (0, 0)))
+    gathered = lax.all_gather(slab, "seq", axis=0, tiled=False)
     offsets = [sum(sizes[:i]) for i in range(len(sizes))]
-    states = gathered[:, offsets[0] : offsets[0] + sizes[0]].reshape(n_seq, heads_here, width, width)
-    gathered_rows = gathered[:, offsets[1] : offsets[1] + sizes[1]].reshape(
-        n_seq * capacity, normed.shape[1]
+    gathered_rows = gathered[:, offsets[0] : offsets[0] + sizes[0]].reshape(n_seq * slots, model)
+    full_weight = (
+        gathered[:, offsets[1] : offsets[1] + sizes[1]]
+        .reshape(n_seq, -1)[:, : out_weight.size]
+        .reshape(n_seq * out_weight.shape[0], out_weight.shape[1])
     )
-    full_weight = gathered[:, offsets[2] : offsets[2] + sizes[2]].reshape(
-        n_seq * out_weight.shape[0], out_weight.shape[1]
+    states = (
+        gathered[:, offsets[2] : offsets[2] + sizes[2]]
+        .reshape(n_seq, -1)[:, : local_state.size]
+        .reshape(n_seq, heads_here, width, width)
     )
-    decays = gathered[:, offsets[3] : offsets[3] + 2 * heads_here].astype(jnp.float32)
+    decays = gathered[:, offsets[3], : 2 * heads_here].astype(jnp.float32)
     decays = decays[:, :heads_here] + decays[:, heads_here:]
 
     blocks = jnp.arange(n_seq)
@@ -127,7 +138,7 @@
     ).astype(jnp.bfloat16)
     expert_part = jnp.dot(hidden, down_weight[0], preferred_element_type=jnp.float32)
     expert_out = lax.psum_scatter(
-        expert_part.astype(jnp.bfloat16).reshape(n_seq, capacity, -1),
+        expert_part.astype(jnp.bfloat16).reshape(n_seq, slots, -1),
         "seq",
         scatter_dimension=0,
         tiled=True,

time: 239 us -> 229 us (0.958)
  waiting for transfers between devices: 158 us -> 151 us
  local copies, waits for them, and re-layouts: 20.6 us -> 17.2 us
    ppermute x5, waiting for transfers between devices: 23.4 us -> 16.5 us  [halving_scatter(): lax.ppermute(send.astype(jnp.bfloat16), axis, [(i, i ^ 1 << k) for i in r...]
    reshape x4 -> x3, local copies, waits for them, and re-layouts: 5.9 us -> 0.21 us  [as_slab(): return jnp.pad(v, (0, r * model - v.shape[0])).reshape(r, model)]
    unnamed x28 -> x30, local copies, waits for them, and re-layouts: 8.41 us -> 4.23 us
    another operation x5 -> x6, local copies, waits for them, and re-layouts: 0.48 us -> 3.87 us  [the longest x1 3.39 us: shards(): full_weight = gathered[:, offsets[1]:offsets[1] + sizes[1]].reshape(n_seq...]
    slice x3 -> x4, local copies, waits for them, and re-layouts: 2.86 us -> 5.69 us  [the longest x1 3.31 us: shards(): gathered[:, offsets[0]:offsets[0] + sizes[0]].reshape(n_seq * slots, model)]
where the time goes in v2:
time: 229 us
  waiting for transfers between devices  151 us (66%)
  local copies, waits for them, and re-layouts  17.2 us (8%)
  matrix products  16.7 us (7%)
  starting transfers between devices  16.3 us (7%)
  other arithmetic  13.9 us (6%)
  between operations  13.8 us (6%)
    all_gather x1, waiting for transfers between devices, shards(): gathered = lax.all_gather(slab, 'seq', axis=0, tiled=False)  82.3 us
    reduce_scatter x1, waiting for transfers between devices, shards(): lax.psum_scatter(expert_part.astype(jnp.bfloat16).reshape(n_seq, slots, -...  51.9 us
    ppermute x5, waiting for transfers between devices, halving_scatter(): lax.ppermute(send.astype(jnp.bfloat16), axis, [(i, i ^ 1 << k) for i in r...  16.5 us
    ppermute x5, starting transfers between devices, halving_scatter(): lax.ppermute(send.astype(jnp.bfloat16), axis, [(i, i ^ 1 << k) for i in r...  16.3 us
    dot_general x1, matrix products, shards(): jnp.dot(hidden, down_weight[0], preferred_element_type=jnp.float32)  5.22 us
  transfers between devices with their start and end apart: 7, of which 7 were waited for; matrix products, arithmetic and copies ran while one was open for 8% of the time, Pallas kernels for 0%

profile of v2, /device:TPU:6, one launch (start us, length us, event | category | flops | bytes accessed | tf_op | source)
XLA Modules:
  0.0 228.5 jit_solution(7368159951194292911)
XLA Ops:
  10.4 1.4 multiply_reduce_fusion
  16.5 82.3 %all-gather.3.cloned.1.call-done = bf16[768,3072]{1,0:T(8,128)(2,1)} async-done(((bf16[48,3072]{1,0:T(8,128)(2,1)}), bf16[768,3072]{1,0:T(8,128)(2,1)}) %all-gather.3.cloned.1.call-update) | async-done | bytes 4718608 | tf_op jit(solution)/shard_map/all_gather | solution.py:97
  98.8 3.3 %fusion.54 = (bf16[16,16,3072]{2,1,0:T(8,128)(2,1)S(1)}, bf16[16,16,3072]{2,1,0:T(8,128)(2,1)}) fusion(bf16[16,48,3072]{2,1,0:T(8,128)(2,1)} %bitcast.207), kind=kLoop, calls=%fused_computation.104 | loop fusion | bytes 6291456 | tf_op jit(solution)/shard_map/slice | solution.py:99
  102.1 5.2 %convolution_convert_fusion = bf16[256,3072]{1,0:T(8,128)(2,1)} fusion(bf16[1,288,3072]{2,1,0:T(8,128)(2,1)S(1)} %copy-done, bf16[256,3072]{1,0:T(8,128)(2,1)S(1)} %bitcast.215, bf16[1,3072,288]{1,2,0:T(8,128)(2,1)} %param.18), kind=kOutput, calls=%fused_computation | convolution fusion | flops 907124736 | bytes 6684672 | tf_op jit(solution)/shard_map/dot_general | solution.py:139
  109.1 1.5 slice.95
  113.2 3.4 %reshape_reshape.6 = bf16[3072,256]{1,0:T(8,128)(2,1)S(1)} reshape(bf16[16,16,3072]{2,1,0:T(8,128)(2,1)} %get-tuple-element.8) | data formatting | bytes 3145728 | tf_op jit(solution)/shard_map/reshape;reshape | solution.py:103
  118.0 2.2 fusion.3
  122.4 1.8 fusion.55
  124.2 51.9 %reduce-scatter.2.cloned.1.call-done = bf16[1,16,3072]{2,1,0:T(8,128)(2,1)} async-done(((bf16[16,16,3072]{2,1,0:T(8,128)(2,1)}), bf16[1,16,3072]{2,1,0:T(8,128)(2,1)}) %reduce-scatter.2.cloned.1.call-update) | async-done | bytes 98320 | tf_op jit(solution)/shard_map/reduce_scatter | solution.py:140
  176.1 3.4 %convolution_add_fusion = f32[128,3072]{1,0:T(8,128)} fusion(f32[128,3072]{1,0:T(8,128)} %fusion.55, f32[128,16]{0,1:T(8,128)S(1)} %select_reduce_fusion.1, bf16[1,16,3072]{2,1,0:T(8,128)(2,1)} %reduce-scatter.2.cloned.1.call-done), kind=kOutput, calls=%fused_computation.1 | convolution fusion | flops 75890688 | bytes 3252224 | tf_op jit(solution)/shard_map/dot_general | solution.py:147
  179.5 1.8 reshape_reshape.7
  182.2 1.9 collective-permute-start
  184.1 2.0 collective-permute-done
  186.2 1.3 bitcast_add_fusion
  188.4 3.5 %collective-permute-start.1 = (bf16[8,4,3072]{2,1,0:T(4,128)(2,1)S(1)}, bf16[8,4,3072]{2,1,0:T(4,128)(2,1)S(1)}, u32[]{:S(2)}, u32[]{:S(2)}) collective-permute-start(bf16[8,4,3072]{2,1,0:T(4,128)(2,1)S(1)} %fusion.20), channel_id=1, source_target_pairs={{0,2},{1,3},{2,0},{3,1},{4,6},{5,7},{6,4},{7,5},{8,10},{9,11},{10,... | collective-permute-start | bytes 589832 | tf_op jit(solution)/shard_map/ppermute | solution.py:16
  192.0 5.4 %collective-permute-done.1 = bf16[8,4,3072]{2,1,0:T(4,128)(2,1)S(1)} collective-permute-done((bf16[8,4,3072]{2,1,0:T(4,128)(2,1)S(1)}, bf16[8,4,3072]{2,1,0:T(4,128)(2,1)S(1)}, u32[]{:S(2)}, u32[]{:S(2)}) %collective-permute-start.1) | collective-permute-done | bytes 196640 | tf_op jit(solution)/shard_map/ppermute | solution.py:16
  198.7 4.9 %collective-permute-start.2 = (bf16[4,4,3072]{2,1,0:T(4,128)(2,1)S(1)}, bf16[4,4,3072]{2,1,0:T(4,128)(2,1)S(1)}, u32[]{:S(2)}, u32[]{:S(2)}) collective-permute-start(bf16[4,4,3072]{2,1,0:T(4,128)(2,1)S(1)} %fusion.31), channel_id=1, source_target_pairs={{0,4},{1,5},{2,6},{3,7},{4,0},{5,1},{6,2},{7,3},{8,12},{9,13},{10,... | collective-permute-start | bytes 294920 | tf_op jit(solution)/shard_map/ppermute | solution.py:16
  203.7 3.1 %collective-permute-done.2 = bf16[4,4,3072]{2,1,0:T(4,128)(2,1)S(1)} collective-permute-done((bf16[4,4,3072]{2,1,0:T(4,128)(2,1)S(1)}, bf16[4,4,3072]{2,1,0:T(4,128)(2,1)S(1)}, u32[]{:S(2)}, u32[]{:S(2)}) %collective-permute-start.2) | collective-permute-done | bytes 98336 | tf_op jit(solution)/shard_map/ppermute | solution.py:16
  206.9 2.6 %collective-permute-start.3 = (bf16[2,4,3072]{2,1,0:T(4,128)(2,1)S(1)}, bf16[2,4,3072]{2,1,0:T(4,128)(2,1)S(1)}, u32[]{:S(2)}, u32[]{:S(2)}) collective-permute-start(bf16[2,4,3072]{2,1,0:T(4,128)(2,1)S(1)} %fusion.43), channel_id=1, source_target_pairs={{0,8},{1,9},{2,10},{3,11},{4,12},{5,13},{6,14},{7,15},{8,0},{9,1},... | collective-permute-start | bytes 147464 | tf_op jit(solution)/shard_map/ppermute | solution.py:16
  209.5 3.3 %collective-permute-done.3 = bf16[2,4,3072]{2,1,0:T(4,128)(2,1)S(1)} collective-permute-done((bf16[2,4,3072]{2,1,0:T(4,128)(2,1)S(1)}, bf16[2,4,3072]{2,1,0:T(4,128)(2,1)S(1)}, u32[]{:S(2)}, u32[]{:S(2)}) %collective-permute-start.3) | collective-permute-done | bytes 49184 | tf_op jit(solution)/shard_map/ppermute | solution.py:16
  212.9 3.2 %collective-permute-start.4 = (bf16[1,4,3072]{2,1,0:T(4,128)(2,1)S(1)}, bf16[1,4,3072]{2,1,0:T(4,128)(2,1)S(1)}, u32[]{:S(2)}, u32[]{:S(2)}) collective-permute-start(bf16[1,4,3072]{2,1,0:T(4,128)(2,1)S(1)} %fusion.45), channel_id=1, source_target_pairs={{0,16},{1,17},{2,18},{3,19},{4,20},{5,21},{6,22},{7,23},{8,24},{9,... | collective-permute-start | bytes 73736 | tf_op jit(solution)/shard_map/ppermute | solution.py:16
  216.2 1.3 convert_element_type.129
  217.5 2.6 %collective-permute-done.4 = bf16[1,4,3072]{2,1,0:T(4,128)(2,1)S(1)} collective-permute-done((bf16[1,4,3072]{2,1,0:T(4,128)(2,1)S(1)}, bf16[1,4,3072]{2,1,0:T(4,128)(2,1)S(1)}, u32[]{:S(2)}, u32[]{:S(2)}) %collective-permute-start.4) | collective-permute-done | bytes 24608 | tf_op jit(solution)/shard_map/ppermute | solution.py:16
  220.1 1.5 fusion.44
  (87 shorter events, 19.6 us)
Async XLA Ops:
  6.5 95.6 %copy-start = (bf16[1,288,3072]{2,1,0:T(8,128)(2,1)S(1)}, bf16[1,288,3072]{2,1,0:T(8,128)(2,1)}, u32[]{:S(2)}) copy-start(bf16[1,288,3072]{2,1,0:T(8,128)(2,1)} %param.19) | copy-start | bytes 5308420
  6.5 7.7 %copy-start.1 = (bf16[128,3072]{1,0:T(8,128)(2,1)S(1)}, bf16[128,3072]{1,0:T(8,128)(2,1)}, u32[]{:S(2)}) copy-start(bf16[128,3072]{1,0:T(8,128)(2,1)} %param.14) | copy-start | bytes 2359300
  6.5 7.5 %copy-start.5 = (bf16[192,256]{1,0:T(8,128)(2,1)S(1)}, bf16[192,256]{1,0:T(8,128)(2,1)}, u32[]{:S(2)}) copy-start(bf16[192,256]{1,0:T(8,128)(2,1)} %param.15) | copy-start | bytes 294916
  6.5 92.3 %all-gather.3.cloned.1.call-start = ((), (), s32[]{:S(2)}) async-start(), calls=%async_computation.2 | async-start | bytes 5013504 | tf_op jit(solution)/shard_map/all_gather | solution.py:97
  9.2 4.7 %copy-start.9 = (f32[2,128]{1,0:T(2,128)}, f32[2,128]{1,0:T(2,128)S(1)}, u32[]{:S(2)}) copy-start(f32[2,128]{1,0:T(2,128)S(1)} %reduce_window_sum.27) | copy-start | bytes 3076
  10.4 5.6 %copy-start.12 = (bf16[3072,32]{0,1:T(8,128)(2,1)S(1)}, bf16[3072,32]{0,1:T(8,128)(2,1)}, u32[]{:S(2)}) copy-start(bf16[3072,32]{0,1:T(8,128)(2,1)} %param.16) | copy-start | bytes 589828
  14.0 2.4 %copy-start.8 = (s32[128,2]{0,1:T(2,128)S(1)}, s32[128,2]{0,1:T(2,128)}, u32[]{:S(2)}) copy-start(s32[128,2]{0,1:T(2,128)} %param.17) | copy-start | bytes 3076
  15.3 160.8 %reduce-scatter.2.cloned.1.call-start = ((), (), s32[]{:S(2)}) async-start(), calls=%async_computation.1 | async-start | bytes 1671168 | tf_op jit(solution)/shard_map/reduce_scatter | solution.py:140
  107.3 0.8 copy-start.6
  107.3 0.8 copy-start.7
  107.3 0.8 copy-start.10
  107.4 0.5 copy-start.11
  113.2 8.1 %copy-start.4 = (bf16[128,256]{1,0:T(8,128)(2,1)S(1)}, bf16[128,256]{1,0:T(8,128)(2,1)}, u32[]{:S(2)}) copy-start(bf16[128,256]{1,0:T(8,128)(2,1)} %param.12) | copy-start | bytes 196612
  182.2 3.9 %collective-permute-start = (bf16[16,4,3072]{2,1,0:T(4,128)(2,1)}, bf16[16,4,3072]{2,1,0:T(4,128)(2,1)}, u32[]{:S(2)}, u32[]{:S(2)}) collective-permute-start(bf16[16,4,3072]{2,1,0:T(4,128)(2,1)} %fusion.9), channel_id=1, source_target_pairs={{0,1},{1,0},{2,3},{3,2},{4,5},{5,4},{6,7},{7,6},{8,9},{9,8},{10,11... | collective-permute-start | bytes 1179656 | tf_op jit(solution)/shard_map/ppermute | solution.py:16
  187.4 0.9 copy-start.3
  188.4 27.7 %copy-start.2 = (bf16[128,3072]{1,0:T(8,128)(2,1)S(1)}, bf16[128,3072]{1,0:T(8,128)(2,1)}, u32[]{:S(2)}) copy-start(bf16[128,3072]{1,0:T(8,128)(2,1)} %param.14) | copy-start | bytes 2359300
  188.4 9.0 %collective-permute-start.1 = (bf16[8,4,3072]{2,1,0:T(4,128)(2,1)S(1)}, bf16[8,4,3072]{2,1,0:T(4,128)(2,1)S(1)}, u32[]{:S(2)}, u32[]{:S(2)}) collective-permute-start(bf16[8,4,3072]{2,1,0:T(4,128)(2,1)S(1)} %fusion.20), channel_id=1, source_target_pairs={{0,2},{1,3},{2,0},{3,1},{4,6},{5,7},{6,4},{7,5},{8,10},{9,11},{10,... | collective-permute-start | bytes 589832 | tf_op jit(solution)/shard_map/ppermute | solution.py:16
  198.7 8.0 %collective-permute-start.2 = (bf16[4,4,3072]{2,1,0:T(4,128)(2,1)S(1)}, bf16[4,4,3072]{2,1,0:T(4,128)(2,1)S(1)}, u32[]{:S(2)}, u32[]{:S(2)}) collective-permute-start(bf16[4,4,3072]{2,1,0:T(4,128)(2,1)S(1)} %fusion.31), channel_id=1, source_target_pairs={{0,4},{1,5},{2,6},{3,7},{4,0},{5,1},{6,2},{7,3},{8,12},{9,13},{10,... | collective-permute-start | bytes 294920 | tf_op jit(solution)/shard_map/ppermute | solution.py:16
  206.9 6.0 %collective-permute-start.3 = (bf16[2,4,3072]{2,1,0:T(4,128)(2,1)S(1)}, bf16[2,4,3072]{2,1,0:T(4,128)(2,1)S(1)}, u32[]{:S(2)}, u32[]{:S(2)}) collective-permute-start(bf16[2,4,3072]{2,1,0:T(4,128)(2,1)S(1)} %fusion.43), channel_id=1, source_target_pairs={{0,8},{1,9},{2,10},{3,11},{4,12},{5,13},{6,14},{7,15},{8,0},{9,1},... | collective-permute-start | bytes 147464 | tf_op jit(solution)/shard_map/ppermute | solution.py:16
  212.9 7.2 %collective-permute-start.4 = (bf16[1,4,3072]{2,1,0:T(4,128)(2,1)S(1)}, bf16[1,4,3072]{2,1,0:T(4,128)(2,1)S(1)}, u32[]{:S(2)}, u32[]{:S(2)}) collective-permute-start(bf16[1,4,3072]{2,1,0:T(4,128)(2,1)S(1)} %fusion.45), channel_id=1, source_target_pairs={{0,16},{1,17},{2,18},{3,19},{4,20},{5,21},{6,22},{7,23},{8,24},{9,... | collective-permute-start | bytes 73736 | tf_op jit(solution)/shard_map/ppermute | solution.py:16
Sparse Core Ops, SparseCore 0:
  15.4 83.3 all-gather.2
  107.5 68.5 reduce-scatter.1

commit v3 on v2

--- a/solution.py
+++ b/solution.py
@@ -5,17 +5,22 @@
 
 
 def halving_scatter(x, axis):
-    n = x.shape[0]
+    n = x.shape[1]
     me = lax.axis_index(axis)
     buf = x
     for k in range(n.bit_length() - 1):
-        half = buf.reshape(buf.shape[0] // 2, 2, *buf.shape[1:])
+        half = buf.reshape(buf.shape[0], 2, buf.shape[1] // 2, *buf.shape[2:])
         upper = ((me >> k) & 1) == 1
         keep = jnp.where(upper, half[:, 1], half[:, 0])
         send = jnp.where(upper, half[:, 0], half[:, 1])
         got = lax.ppermute(send.astype(jnp.bfloat16), axis, [(i, i ^ (1 << k)) for i in range(n)])
         buf = keep + got.astype(keep.dtype)
-    return buf[0]
+    return buf[:, 0]
+
+
+def bit_reversed(n):
+    bits = n.bit_length() - 1
+    return [int(format(i, f"0{bits}b")[::-1], 2) for i in range(n)]
 
 
 def shards(
@@ -44,7 +49,8 @@
     qloc = split_heads(queries)
     kloc = split_heads(key_matrix)
     vloc = split_heads(values)
-    cum = jnp.cumsum(log_decay, axis=1)
+    upto = (jnp.arange(rows)[:, None] <= jnp.arange(rows)[None, :]).astype(jnp.float32)
+    cum = jnp.dot(log_decay, upto, precision=lax.Precision.HIGHEST)
     last = cum[:, -1:]
     carry_decay = jnp.exp(last[:, 0])
     kscaled = kloc * jnp.exp(last - cum)[:, :, None]
@@ -66,7 +72,9 @@
     capacity = 3 * rows * topk // (2 * n_exp)
     slots = -(-capacity // 16) * 16
     mine = (expert_ids.reshape(-1) == owner).astype(jnp.int32)
-    ranks = jnp.cumsum(mine) - mine
+    pairs = mine.shape[0]
+    before = (jnp.arange(pairs)[:, None] < jnp.arange(pairs)[None, :]).astype(jnp.bfloat16)
+    ranks = jnp.dot(mine.astype(jnp.bfloat16), before, preferred_element_type=jnp.float32).astype(jnp.int32)
     slot_pick = (ranks[None, :] == jnp.arange(slots, dtype=jnp.int32)[:, None]) & (
         mine[None, :] == 1
     )
@@ -130,8 +138,14 @@
     mixed = mixed * lax.rsqrt(jnp.mean(mixed * mixed, axis=-1, keepdims=True) + 1e-06)
     attn = mixed.transpose(1, 0, 2).reshape(rows, heads_here * width).astype(jnp.bfloat16)
 
+    per = rows // n_exp
+    order = bit_reversed(n_exp)
+
+    def chunk_order(a):
+        return a.reshape(n_exp, per, -1).transpose(1, 0, 2)[:, order].reshape(rows, -1)
+
     projected = lax.dot_general(
-        attn, full_weight, (((1,), (1,)), ((), ())), preferred_element_type=jnp.float32
+        chunk_order(attn), full_weight, (((1,), (1,)), ((), ())), preferred_element_type=jnp.float32
     )
     hidden = jax.nn.silu(
         jnp.dot(gathered_rows, up_weight[0], preferred_element_type=jnp.float32)
@@ -142,10 +156,14 @@
         "seq",
         scatter_dimension=0,
         tiled=True,
-    )[0].astype(jnp.float32)
-    combine = jnp.einsum("cbk,bk->bc", slot_pick, gates, precision=lax.Precision.HIGHEST)
-    contribution = jnp.dot(combine, expert_out, precision=lax.Precision.HIGHEST)
-    partial = (projected + contribution).reshape(n_exp, rows // n_exp, -1)
+    )[0]
+    combine = chunk_order(jnp.einsum("cbk,bk->bc", slot_pick, gates, precision=lax.Precision.HIGHEST))
+    combine_hi = combine.astype(jnp.bfloat16)
+    combine_lo = (combine - combine_hi.astype(jnp.float32)).astype(jnp.bfloat16)
+    contribution = jnp.dot(combine_hi, expert_out, preferred_element_type=jnp.float32) + jnp.dot(
+        combine_lo, expert_out, preferred_element_type=jnp.float32
+    )
+    partial = (projected + contribution).reshape(per, n_exp, -1)
     summed = halving_scatter(partial, "exp")
     own_rows = summed.shape[0]
     own = lax.dynamic_slice_in_dim(stream, owner * own_rows, own_rows, 0)

time: 229 us -> 227 us (level)
  other arithmetic: 13.9 us -> 10 us
  matrix products: 16.7 us -> 14.1 us
    reduce_scatter x1, waiting for transfers between devices: 51.9 us -> 54.4 us  [shards(): lax.psum_scatter(expert_part.astype(jnp.bfloat16).reshape(n_seq, slots, -...]
    unnamed x30 -> x40, local copies, waits for them, and re-layouts: 4.23 us -> 5.79 us
    dot_general x2 -> x5, matrix products: 5.25 us -> 4.1 us  [the longest x1 1.57 us: shards(): cum = jnp.dot(log_decay, upto, precision=lax.Precision.HIGHEST)]
  transfers between devices with their start and end apart: 7 -> 7, of which waited for: 7 -> 7; matrix products, arithmetic and copies ran while one was open for 8% -> 7% of each run, Pallas kernels for 0% -> 0%
where the time goes in v3:
time: 227 us
  waiting for transfers between devices  153 us (67%)
  local copies, waits for them, and re-layouts  19.3 us (9%)
  starting transfers between devices  16.4 us (7%)
  matrix products  14.1 us (6%)
  between operations  13.9 us (6%)
  other arithmetic  10 us (4%)
    all_gather x1, waiting for transfers between devices, shards(): gathered = lax.all_gather(slab, 'seq', axis=0, tiled=False)  82.1 us
    reduce_scatter x1, waiting for transfers between devices, shards(): lax.psum_scatter(expert_part.astype(jnp.bfloat16).reshape(n_seq, slots, -...  54.4 us
    ppermute x5, starting transfers between devices, halving_scatter(): lax.ppermute(send.astype(jnp.bfloat16), axis, [(i, i ^ 1 << k) for i in r...  16.4 us
    ppermute x5, waiting for transfers between devices, halving_scatter(): lax.ppermute(send.astype(jnp.bfloat16), axis, [(i, i ^ 1 << k) for i in r...  16.3 us
    unnamed x40, local copies, waits for them, and re-layouts  5.79 us
    dot_general x1, matrix products, shards(): jnp.dot(hidden, down_weight[0], preferred_element_type=jnp.float32)  5.69 us
  transfers between devices with their start and end apart: 7, of which 7 were waited for; matrix products, arithmetic and copies ran while one was open for 7% of the time, Pallas kernels for 0%

profile of v3, /device:TPU:6, one launch (start us, length us, event | category | flops | bytes accessed | tf_op | source)
XLA Modules:
  0.0 226.6 jit_solution(12381419624624513504)
XLA Ops:
  6.6 1.6 fusion.61
  10.3 1.4 multiply_reduce_fusion
  16.6 82.1 %all-gather.3.cloned.1.call-done = bf16[768,3072]{1,0:T(8,128)(2,1)} async-done(((bf16[48,3072]{1,0:T(8,128)(2,1)}), bf16[768,3072]{1,0:T(8,128)(2,1)}) %all-gather.3.cloned.1.call-update) | async-done | bytes 4718608 | tf_op jit(solution)/shard_map/all_gather | solution.py:105
  98.7 3.3 %fusion.60 = (bf16[16,16,3072]{2,1,0:T(8,128)(2,1)S(1)}, bf16[16,16,3072]{2,1,0:T(8,128)(2,1)}) fusion(bf16[16,48,3072]{2,1,0:T(8,128)(2,1)} %bitcast.201), kind=kLoop, calls=%fused_computation.113 | loop fusion | bytes 6291456 | tf_op jit(solution)/shard_map/slice | solution.py:109
  102.0 5.7 %convolution_convert_fusion = bf16[256,3072]{1,0:T(8,128)(2,1)} fusion(bf16[1,288,3072]{2,1,0:T(8,128)(2,1)S(1)} %copy-done, bf16[256,3072]{1,0:T(8,128)(2,1)} %bitcast.209, bf16[1,3072,288]{1,2,0:T(8,128)(2,1)} %param.20), kind=kOutput, calls=%fused_computation.2 | convolution fusion | flops 907124736 | bytes 6684672 | tf_op jit(solution)/shard_map/dot_general | solution.py:153
  110.3 2.7 %slice.87 = bf16[16,11,3072]{2,1,0:T(8,128)(2,1)} slice(bf16[16,48,3072]{2,1,0:T(8,128)(2,1)} %bitcast.203), slice={[0:16], [32:43], [0:3072]} | slice | bytes 2162688 | tf_op jit(solution)/shard_map/slice | solution.py:114
  113.7 2.1 copy.161
  119.0 2.8 %reshape_reshape.6 = bf16[3072,256]{1,0:T(8,128)(2,1)} reshape(bf16[16,16,3072]{2,1,0:T(8,128)(2,1)S(1)} %get-tuple-element.7) | data formatting | bytes 3145728 | tf_op jit(solution)/shard_map/reshape;reshape | solution.py:111
  121.9 54.4 %reduce-scatter.2.cloned.1.call-done = bf16[1,16,3072]{2,1,0:T(8,128)(2,1)} async-done(((bf16[16,16,3072]{2,1,0:T(8,128)(2,1)}), bf16[1,16,3072]{2,1,0:T(8,128)(2,1)}) %reduce-scatter.2.cloned.1.call-update) | async-done | bytes 98320 | tf_op jit(solution)/shard_map/reduce_scatter | solution.py:154
  176.3 1.3 fusion.36
  180.5 1.9 collective-permute-start
  182.4 2.0 collective-permute-done
  184.4 1.1 fusion.7
  186.5 3.4 %collective-permute-start.1 = (bf16[4,8,3072]{2,1,0:T(8,128)(2,1)S(1)}, bf16[4,8,3072]{2,1,0:T(8,128)(2,1)S(1)}, u32[]{:S(2)}, u32[]{:S(2)}) collective-permute-start(bf16[4,8,3072]{2,1,0:T(8,128)(2,1)S(1)} %fusion.24), channel_id=1, source_target_pairs={{0,2},{1,3},{2,0},{3,1},{4,6},{5,7},{6,4},{7,5},{8,10},{9,11},{10,... | collective-permute-start | bytes 589832 | tf_op jit(solution)/shard_map/ppermute | solution.py:16
  189.9 5.4 %collective-permute-done.1 = bf16[4,8,3072]{2,1,0:T(8,128)(2,1)S(1)} collective-permute-done((bf16[4,8,3072]{2,1,0:T(8,128)(2,1)S(1)}, bf16[4,8,3072]{2,1,0:T(8,128)(2,1)S(1)}, u32[]{:S(2)}, u32[]{:S(2)}) %collective-permute-start.1) | collective-permute-done | bytes 196640 | tf_op jit(solution)/shard_map/ppermute | solution.py:16
  195.3 1.2 fusion.14
  196.8 4.9 %collective-permute-start.2 = (bf16[4,4,3072]{2,0,1:T(4,128)(2,1)S(1)}, bf16[4,4,3072]{2,0,1:T(4,128)(2,1)S(1)}, u32[]{:S(2)}, u32[]{:S(2)}) collective-permute-start(bf16[4,4,3072]{2,0,1:T(4,128)(2,1)S(1)} %fusion.33), channel_id=1, source_target_pairs={{0,4},{1,5},{2,6},{3,7},{4,0},{5,1},{6,2},{7,3},{8,12},{9,13},{10,... | collective-permute-start | bytes 294920 | tf_op jit(solution)/shard_map/ppermute | solution.py:16
  201.8 3.1 %collective-permute-done.2 = bf16[4,4,3072]{2,0,1:T(4,128)(2,1)S(1)} collective-permute-done((bf16[4,4,3072]{2,0,1:T(4,128)(2,1)S(1)}, bf16[4,4,3072]{2,0,1:T(4,128)(2,1)S(1)}, u32[]{:S(2)}, u32[]{:S(2)}) %collective-permute-start.2) | collective-permute-done | bytes 98336 | tf_op jit(solution)/shard_map/ppermute | solution.py:16
  204.9 2.8 %collective-permute-start.3 = (bf16[4,2,3072]{2,0,1:T(4,128)(2,1)S(1)}, bf16[4,2,3072]{2,0,1:T(4,128)(2,1)S(1)}, u32[]{:S(2)}, u32[]{:S(2)}) collective-permute-start(bf16[4,2,3072]{2,0,1:T(4,128)(2,1)S(1)} %fusion.46), channel_id=1, source_target_pairs={{0,8},{1,9},{2,10},{3,11},{4,12},{5,13},{6,14},{7,15},{8,0},{9,1},... | collective-permute-start | bytes 147464 | tf_op jit(solution)/shard_map/ppermute | solution.py:16
  207.7 3.2 %collective-permute-done.3 = bf16[4,2,3072]{2,0,1:T(4,128)(2,1)S(1)} collective-permute-done((bf16[4,2,3072]{2,0,1:T(4,128)(2,1)S(1)}, bf16[4,2,3072]{2,0,1:T(4,128)(2,1)S(1)}, u32[]{:S(2)}, u32[]{:S(2)}) %collective-permute-start.3) | collective-permute-done | bytes 49184 | tf_op jit(solution)/shard_map/ppermute | solution.py:16
  211.0 3.4 %collective-permute-start.4 = (bf16[4,1,3072]{2,0,1:T(4,128)(2,1)S(1)}, bf16[4,1,3072]{2,0,1:T(4,128)(2,1)S(1)}, u32[]{:S(2)}, u32[]{:S(2)}) collective-permute-start(bf16[4,1,3072]{2,0,1:T(4,128)(2,1)S(1)} %fusion.49), channel_id=1, source_target_pairs={{0,16},{1,17},{2,18},{3,19},{4,20},{5,21},{6,22},{7,23},{8,24},{9,... | collective-permute-start | bytes 73736 | tf_op jit(solution)/shard_map/ppermute | solution.py:16
  214.4 1.3 convert_element_type.173
  215.7 2.5 %collective-permute-done.4 = bf16[4,1,3072]{2,0,1:T(4,128)(2,1)S(1)} collective-permute-done((bf16[4,1,3072]{2,0,1:T(4,128)(2,1)S(1)}, bf16[4,1,3072]{2,0,1:T(4,128)(2,1)S(1)}, u32[]{:S(2)}, u32[]{:S(2)}) %collective-permute-start.4) | collective-permute-done | bytes 24608 | tf_op jit(solution)/shard_map/ppermute | solution.py:16
  218.2 1.5 fusion.47
  (106 shorter events, 17.5 us)
Async XLA Ops:
  6.5 95.5 %copy-start = (bf16[1,288,3072]{2,1,0:T(8,128)(2,1)S(1)}, bf16[1,288,3072]{2,1,0:T(8,128)(2,1)}, u32[]{:S(2)}) copy-start(bf16[1,288,3072]{2,1,0:T(8,128)(2,1)} %param.21) | copy-start | bytes 5308420
  6.5 7.6 %copy-start.1 = (bf16[128,3072]{1,0:T(8,128)(2,1)S(1)}, bf16[128,3072]{1,0:T(8,128)(2,1)}, u32[]{:S(2)}) copy-start(bf16[128,3072]{1,0:T(8,128)(2,1)} %param.16) | copy-start | bytes 2359300
  6.5 7.4 %copy-start.7 = (bf16[192,256]{1,0:T(8,128)(2,1)S(1)}, bf16[192,256]{1,0:T(8,128)(2,1)}, u32[]{:S(2)}) copy-start(bf16[192,256]{1,0:T(8,128)(2,1)} %param.17) | copy-start | bytes 294916
  6.5 92.2 %all-gather.3.cloned.1.call-start = ((), (), s32[]{:S(2)}) async-start(), calls=%async_computation.2 | async-start | bytes 5013504 | tf_op jit(solution)/shard_map/all_gather | solution.py:105
  8.1 1.5 copy-start.15
  10.3 5.0 %copy-start.17 = (bf16[3072,32]{0,1:T(8,128)(2,1)S(1)}, bf16[3072,32]{0,1:T(8,128)(2,1)}, u32[]{:S(2)}) copy-start(bf16[3072,32]{0,1:T(8,128)(2,1)} %param.18) | copy-start | bytes 589828
  13.9 1.8 copy-start.11
  13.9 2.0 copy-start.16
  15.2 161.1 %reduce-scatter.2.cloned.1.call-start = ((), (), s32[]{:S(2)}) async-start(), calls=%async_computation.1 | async-start | bytes 1671168 | tf_op jit(solution)/shard_map/reduce_scatter | solution.py:154
  115.7 0.7 copy-start.10
  115.8 0.7 copy-start.13
  115.8 1.7 copy-start.8
  115.9 2.0 copy-start.6
  115.9 2.0 copy-start.9
  115.9 2.3 %copy-start.14 = (f32[128,2]{0,1:T(2,128)S(1)}, f32[128,2]{0,1:T(2,128)}, u32[]{:S(2)}) copy-start(f32[128,2]{0,1:T(2,128)} %get-tuple-element.17) | copy-start | bytes 3076
  176.3 1.4 copy-start.5
  177.6 1.4 copy-start.3
  180.5 3.9 %collective-permute-start = (bf16[4,16,3072]{2,1,0:T(8,128)(2,1)}, bf16[4,16,3072]{2,1,0:T(8,128)(2,1)}, u32[]{:S(2)}, u32[]{:S(2)}) collective-permute-start(bf16[4,16,3072]{2,1,0:T(8,128)(2,1)} %fusion.12), channel_id=1, source_target_pairs={{0,1},{1,0},{2,3},{3,2},{4,5},{5,4},{6,7},{7,6},{8,9},{9,8},{10,11... | collective-permute-start | bytes 1179656 | tf_op jit(solution)/shard_map/ppermute | solution.py:16
  185.5 0.9 copy-start.4
  186.5 8.8 %collective-permute-start.1 = (bf16[4,8,3072]{2,1,0:T(8,128)(2,1)S(1)}, bf16[4,8,3072]{2,1,0:T(8,128)(2,1)S(1)}, u32[]{:S(2)}, u32[]{:S(2)}) collective-permute-start(bf16[4,8,3072]{2,1,0:T(8,128)(2,1)S(1)} %fusion.24), channel_id=1, source_target_pairs={{0,2},{1,3},{2,0},{3,1},{4,6},{5,7},{6,4},{7,5},{8,10},{9,11},{10,... | collective-permute-start | bytes 589832 | tf_op jit(solution)/shard_map/ppermute | solution.py:16
  189.9 24.5 %copy-start.2 = (bf16[128,3072]{1,0:T(8,128)(2,1)S(1)}, bf16[128,3072]{1,0:T(8,128)(2,1)}, u32[]{:S(2)}) copy-start(bf16[128,3072]{1,0:T(8,128)(2,1)} %param.16) | copy-start | bytes 2359300
  196.8 8.0 %collective-permute-start.2 = (bf16[4,4,3072]{2,0,1:T(4,128)(2,1)S(1)}, bf16[4,4,3072]{2,0,1:T(4,128)(2,1)S(1)}, u32[]{:S(2)}, u32[]{:S(2)}) collective-permute-start(bf16[4,4,3072]{2,0,1:T(4,128)(2,1)S(1)} %fusion.33), channel_id=1, source_target_pairs={{0,4},{1,5},{2,6},{3,7},{4,0},{5,1},{6,2},{7,3},{8,12},{9,13},{10,... | collective-permute-start | bytes 294920 | tf_op jit(solution)/shard_map/ppermute | solution.py:16
  204.9 6.0 %collective-permute-start.3 = (bf16[4,2,3072]{2,0,1:T(4,128)(2,1)S(1)}, bf16[4,2,3072]{2,0,1:T(4,128)(2,1)S(1)}, u32[]{:S(2)}, u32[]{:S(2)}) collective-permute-start(bf16[4,2,3072]{2,0,1:T(4,128)(2,1)S(1)} %fusion.46), channel_id=1, source_target_pairs={{0,8},{1,9},{2,10},{3,11},{4,12},{5,13},{6,14},{7,15},{8,0},{9,1},... | collective-permute-start | bytes 147464 | tf_op jit(solution)/shard_map/ppermute | solution.py:16
  211.0 7.2 %collective-permute-start.4 = (bf16[4,1,3072]{2,0,1:T(4,128)(2,1)S(1)}, bf16[4,1,3072]{2,0,1:T(4,128)(2,1)S(1)}, u32[]{:S(2)}, u32[]{:S(2)}) collective-permute-start(bf16[4,1,3072]{2,0,1:T(4,128)(2,1)S(1)} %fusion.49), channel_id=1, source_target_pairs={{0,16},{1,17},{2,18},{3,19},{4,20},{5,21},{6,22},{7,23},{8,24},{9,... | collective-permute-start | bytes 73736 | tf_op jit(solution)/shard_map/ppermute | solution.py:16
  (1 other events, 0.6 us)
Sparse Core Ops, SparseCore 0:
  15.3 83.3 all-gather.2
  107.9 68.3 reduce-scatter.1

commit v4 on v3

--- a/solution.py
+++ b/solution.py
@@ -4,23 +4,38 @@
 from jax.sharding import PartitionSpec as P
 
 
+def ring_label(n):
+    if n != 32:
+        return list(range(n))
+
+    def gray(v):
+        return v ^ (v >> 1)
+
+    return [gray(e >> 3) * 8 + gray((e >> 1) & 3) * 2 + (e & 1) for e in range(n)]
+
+
 def halving_scatter(x, axis):
     n = x.shape[1]
+    label = ring_label(n)
+    member_of = {v: e for e, v in enumerate(label)}
     me = lax.axis_index(axis)
+    mine = jnp.asarray(label, jnp.int32)[me]
     buf = x
     for k in range(n.bit_length() - 1):
         half = buf.reshape(buf.shape[0], 2, buf.shape[1] // 2, *buf.shape[2:])
-        upper = ((me >> k) & 1) == 1
+        upper = ((mine >> k) & 1) == 1
         keep = jnp.where(upper, half[:, 1], half[:, 0])
         send = jnp.where(upper, half[:, 0], half[:, 1])
-        got = lax.ppermute(send.astype(jnp.bfloat16), axis, [(i, i ^ (1 << k)) for i in range(n)])
+        pairs = [(e, member_of[label[e] ^ (1 << k)]) for e in range(n)]
+        got = lax.ppermute(send.astype(jnp.bfloat16), axis, pairs)
         buf = keep + got.astype(keep.dtype)
     return buf[:, 0]
 
 
-def bit_reversed(n):
+def chunk_positions(n):
     bits = n.bit_length() - 1
-    return [int(format(i, f"0{bits}b")[::-1], 2) for i in range(n)]
+    member_of = {v: e for e, v in enumerate(ring_label(n))}
+    return [member_of[int(format(p, f"0{bits}b")[::-1], 2)] for p in range(n)]
 
 
 def shards(
@@ -139,7 +154,7 @@
     attn = mixed.transpose(1, 0, 2).reshape(rows, heads_here * width).astype(jnp.bfloat16)
 
     per = rows // n_exp
-    order = bit_reversed(n_exp)
+    order = chunk_positions(n_exp)
 
     def chunk_order(a):
         return a.reshape(n_exp, per, -1).transpose(1, 0, 2)[:, order].reshape(rows, -1)

time: 227 us -> 222 us (0.978)
  other arithmetic: 10 us -> 6.78 us
  between operations: 13.9 us -> 17.1 us
  waiting for transfers between devices: 153 us -> 150 us
    unnamed x40 -> x26, local copies, waits for them, and re-layouts: 5.79 us -> 3.87 us
where the time goes in v4:
time: 222 us
  waiting for transfers between devices  150 us (68%)
  local copies, waits for them, and re-layouts  20.2 us (9%)
  between operations  17.1 us (8%)
  starting transfers between devices  15 us (7%)
  matrix products  12.7 us (6%)
  other arithmetic  6.78 us (3%)
    all_gather x1, waiting for transfers between devices, shards(): gathered = lax.all_gather(slab, 'seq', axis=0, tiled=False)  82.1 us
    reduce_scatter x1, waiting for transfers between devices, shards(): lax.psum_scatter(expert_part.astype(jnp.bfloat16).reshape(n_seq, slots, -...  53.5 us
    ppermute x5, starting transfers between devices, halving_scatter(): got = lax.ppermute(send.astype(jnp.bfloat16), axis, pairs)  14.9 us
    ppermute x5, waiting for transfers between devices, halving_scatter(): got = lax.ppermute(send.astype(jnp.bfloat16), axis, pairs)  14.2 us
    dot_general x1, matrix products, shards(): jnp.dot(hidden, down_weight[0], preferred_element_type=jnp.float32)  5.67 us
  transfers between devices with their start and end apart: 7, of which 7 were waited for; matrix products, arithmetic and copies ran while one was open for 7% of the time, Pallas kernels for 0%

profile of v4, /device:TPU:6, one launch (start us, length us, event | category | flops | bytes accessed | tf_op | source)
XLA Modules:
  0.0 221.6 jit_solution(574214432800181138)
XLA Ops:
  9.2 1.4 multiply_reduce_fusion
  11.7 1.0 convolution_convert_fusion.2
  15.6 82.1 %all-gather.3.cloned.1.call-done = bf16[768,3072]{1,0:T(8,128)(2,1)} async-done(((bf16[48,3072]{1,0:T(8,128)(2,1)}), bf16[768,3072]{1,0:T(8,128)(2,1)}) %all-gather.3.cloned.1.call-update) | async-done | bytes 4718608 | tf_op jit(solution)/shard_map/all_gather | solution.py:120
  97.7 4.0 %fusion.60 = (bf16[16,16,3072]{2,1,0:T(8,128)(2,1)}, bf16[16,16,3072]{2,1,0:T(8,128)(2,1)}) fusion(bf16[16,48,3072]{2,1,0:T(8,128)(2,1)} %bitcast.206), kind=kLoop, calls=%fused_computation.113 | loop fusion | bytes 6291456 | tf_op jit(solution)/shard_map/slice | solution.py:124
  101.6 5.7 %convolution_convert_fusion = bf16[256,3072]{1,0:T(8,128)(2,1)} fusion(bf16[1,288,3072]{2,1,0:T(8,128)(2,1)S(1)} %copy-done, bf16[256,3072]{1,0:T(8,128)(2,1)} %bitcast.214, bf16[1,3072,288]{1,2,0:T(8,128)(2,1)} %param.21), kind=kOutput, calls=%fused_computation.2 | convolution fusion | flops 907124736 | bytes 6684672 | tf_op jit(solution)/shard_map/dot_general | solution.py:168
  110.2 2.8 %slice.87 = bf16[16,11,3072]{2,1,0:T(8,128)(2,1)} slice(bf16[16,48,3072]{2,1,0:T(8,128)(2,1)} %bitcast.208), slice={[0:16], [32:43], [0:3072]} | slice | bytes 2162688 | tf_op jit(solution)/shard_map/slice | solution.py:129
  113.1 2.1 copy.162
  115.6 1.0 fusion.3
  118.0 4.3 %reshape_reshape.6 = bf16[3072,256]{1,0:T(8,128)(2,1)} reshape(bf16[16,16,3072]{2,1,0:T(8,128)(2,1)} %get-tuple-element.7) | data formatting | bytes 3145728 | tf_op jit(solution)/shard_map/reshape;reshape | solution.py:126
  122.4 53.5 %reduce-scatter.2.cloned.1.call-done = bf16[1,16,3072]{2,1,0:T(8,128)(2,1)} async-done(((bf16[16,16,3072]{2,1,0:T(8,128)(2,1)}), bf16[1,16,3072]{2,1,0:T(8,128)(2,1)}) %reduce-scatter.2.cloned.1.call-update) | async-done | bytes 98320 | tf_op jit(solution)/shard_map/reduce_scatter | solution.py:169
  175.9 1.3 fusion.36
  177.7 1.0 copy-done.2
  179.4 1.9 collective-permute-start
  182.0 1.0 collective-permute-done
  183.2 3.3 %collective-permute-start.1 = (bf16[4,8,3072]{2,1,0:T(8,128)(2,1)S(1)}, bf16[4,8,3072]{2,1,0:T(8,128)(2,1)S(1)}, u32[]{:S(2)}, u32[]{:S(2)}) collective-permute-start(bf16[4,8,3072]{2,1,0:T(8,128)(2,1)S(1)} %fusion.24), channel_id=1, source_target_pairs={{0,2},{1,3},{2,0},{3,1},{4,6},{5,7},{6,4},{7,5},{8,10},{9,11},{10,... | collective-permute-start | bytes 589832 | tf_op jit(solution)/shard_map/ppermute | solution.py:30
  187.2 4.9 %collective-permute-done.1 = bf16[4,8,3072]{2,1,0:T(8,128)(2,1)S(1)} collective-permute-done((bf16[4,8,3072]{2,1,0:T(8,128)(2,1)S(1)}, bf16[4,8,3072]{2,1,0:T(8,128)(2,1)S(1)}, u32[]{:S(2)}, u32[]{:S(2)}) %collective-permute-start.1) | collective-permute-done | bytes 196640 | tf_op jit(solution)/shard_map/ppermute | solution.py:30
  192.4 4.6 %collective-permute-start.2 = (bf16[4,4,3072]{2,0,1:T(4,128)(2,1)S(1)}, bf16[4,4,3072]{2,0,1:T(4,128)(2,1)S(1)}, u32[]{:S(2)}, u32[]{:S(2)}) collective-permute-start(bf16[4,4,3072]{2,0,1:T(4,128)(2,1)S(1)} %fusion.33), channel_id=1, source_target_pairs={{0,6},{1,7},{2,4},{3,5},{4,2},{5,3},{6,0},{7,1},{8,14},{9,15},{10,... | collective-permute-start | bytes 294920 | tf_op jit(solution)/shard_map/ppermute | solution.py:30
  197.7 2.5 %collective-permute-done.2 = bf16[4,4,3072]{2,0,1:T(4,128)(2,1)S(1)} collective-permute-done((bf16[4,4,3072]{2,0,1:T(4,128)(2,1)S(1)}, bf16[4,4,3072]{2,0,1:T(4,128)(2,1)S(1)}, u32[]{:S(2)}, u32[]{:S(2)}) %collective-permute-start.2) | collective-permute-done | bytes 98336 | tf_op jit(solution)/shard_map/ppermute | solution.py:30
  200.3 2.7 %collective-permute-start.3 = (bf16[4,2,3072]{2,0,1:T(4,128)(2,1)S(1)}, bf16[4,2,3072]{2,0,1:T(4,128)(2,1)S(1)}, u32[]{:S(2)}, u32[]{:S(2)}) collective-permute-start(bf16[4,2,3072]{2,0,1:T(4,128)(2,1)S(1)} %fusion.46), channel_id=1, source_target_pairs={{0,8},{1,9},{2,10},{3,11},{4,12},{5,13},{6,14},{7,15},{8,0},{9,1},... | collective-permute-start | bytes 147464 | tf_op jit(solution)/shard_map/ppermute | solution.py:30
  203.6 2.6 %collective-permute-done.3 = bf16[4,2,3072]{2,0,1:T(4,128)(2,1)S(1)} collective-permute-done((bf16[4,2,3072]{2,0,1:T(4,128)(2,1)S(1)}, bf16[4,2,3072]{2,0,1:T(4,128)(2,1)S(1)}, u32[]{:S(2)}, u32[]{:S(2)}) %collective-permute-start.3) | collective-permute-done | bytes 49184 | tf_op jit(solution)/shard_map/ppermute | solution.py:30
  206.3 2.4 %collective-permute-start.4 = (bf16[4,1,3072]{2,0,1:T(4,128)(2,1)S(1)}, bf16[4,1,3072]{2,0,1:T(4,128)(2,1)S(1)}, u32[]{:S(2)}, u32[]{:S(2)}) collective-permute-start(bf16[4,1,3072]{2,0,1:T(4,128)(2,1)S(1)} %fusion.49), channel_id=1, source_target_pairs={{0,24},{1,25},{2,26},{3,27},{4,28},{5,29},{6,30},{7,31},{8,16},{9,... | collective-permute-start | bytes 73736 | tf_op jit(solution)/shard_map/ppermute | solution.py:30
  208.7 1.3 convert_element_type.173
  210.0 3.2 %collective-permute-done.4 = bf16[4,1,3072]{2,0,1:T(4,128)(2,1)S(1)} collective-permute-done((bf16[4,1,3072]{2,0,1:T(4,128)(2,1)S(1)}, bf16[4,1,3072]{2,0,1:T(4,128)(2,1)S(1)}, u32[]{:S(2)}, u32[]{:S(2)}) %collective-permute-start.4) | collective-permute-done | bytes 24608 | tf_op jit(solution)/shard_map/ppermute | solution.py:30
  213.3 1.5 fusion.47
  (93 shorter events, 12.3 us)
Async XLA Ops:
  6.5 95.1 %copy-start = (bf16[1,288,3072]{2,1,0:T(8,128)(2,1)S(1)}, bf16[1,288,3072]{2,1,0:T(8,128)(2,1)}, u32[]{:S(2)}) copy-start(bf16[1,288,3072]{2,1,0:T(8,128)(2,1)} %param.22) | copy-start | bytes 5308420
  6.5 6.5 %copy-start.1 = (bf16[128,3072]{1,0:T(8,128)(2,1)S(1)}, bf16[128,3072]{1,0:T(8,128)(2,1)}, u32[]{:S(2)}) copy-start(bf16[128,3072]{1,0:T(8,128)(2,1)} %param.17) | copy-start | bytes 2359300
  6.5 6.3 %copy-start.5 = (bf16[192,256]{1,0:T(8,128)(2,1)S(1)}, bf16[192,256]{1,0:T(8,128)(2,1)}, u32[]{:S(2)}) copy-start(bf16[192,256]{1,0:T(8,128)(2,1)} %param.18) | copy-start | bytes 294916
  6.5 91.1 %all-gather.3.cloned.1.call-start = ((), (), s32[]{:S(2)}) async-start(), calls=%async_computation.2 | async-start | bytes 5013504 | tf_op jit(solution)/shard_map/all_gather | solution.py:120
  9.2 5.0 %copy-start.9 = (bf16[3072,32]{0,1:T(8,128)(2,1)S(1)}, bf16[3072,32]{0,1:T(8,128)(2,1)}, u32[]{:S(2)}) copy-start(bf16[3072,32]{0,1:T(8,128)(2,1)} %param.19) | copy-start | bytes 589828
  12.8 1.8 copy-start.7
  12.8 2.0 copy-start.8
  14.1 161.8 %reduce-scatter.2.cloned.1.call-start = ((), (), s32[]{:S(2)}) async-start(), calls=%async_computation.1 | async-start | bytes 1671168 | tf_op jit(solution)/shard_map/reduce_scatter | solution.py:169
  107.3 0.7 copy-start.10
  107.3 1.9 copy-start.6
  115.2 1.6 copy-start.4
  175.9 1.4 copy-start.3
  177.3 1.4 copy-start.2
  179.4 3.6 %collective-permute-start = (bf16[4,16,3072]{2,1,0:T(8,128)(2,1)S(1)}, bf16[4,16,3072]{2,1,0:T(8,128)(2,1)S(1)}, u32[]{:S(2)}, u32[]{:S(2)}) collective-permute-start(bf16[4,16,3072]{2,1,0:T(8,128)(2,1)S(1)} %fusion.12), channel_id=1, source_target_pairs={{0,1},{1,0},{2,3},{3,2},{4,5},{5,4},{6,7},{7,6},{8,9},{9,8},{10,11... | collective-permute-start | bytes 1179656 | tf_op jit(solution)/shard_map/ppermute | solution.py:30
  183.2 8.8 %collective-permute-start.1 = (bf16[4,8,3072]{2,1,0:T(8,128)(2,1)S(1)}, bf16[4,8,3072]{2,1,0:T(8,128)(2,1)S(1)}, u32[]{:S(2)}, u32[]{:S(2)}) collective-permute-start(bf16[4,8,3072]{2,1,0:T(8,128)(2,1)S(1)} %fusion.24), channel_id=1, source_target_pairs={{0,2},{1,3},{2,0},{3,1},{4,6},{5,7},{6,4},{7,5},{8,10},{9,11},{10,... | collective-permute-start | bytes 589832 | tf_op jit(solution)/shard_map/ppermute | solution.py:30
  192.4 7.7 %collective-permute-start.2 = (bf16[4,4,3072]{2,0,1:T(4,128)(2,1)S(1)}, bf16[4,4,3072]{2,0,1:T(4,128)(2,1)S(1)}, u32[]{:S(2)}, u32[]{:S(2)}) collective-permute-start(bf16[4,4,3072]{2,0,1:T(4,128)(2,1)S(1)} %fusion.33), channel_id=1, source_target_pairs={{0,6},{1,7},{2,4},{3,5},{4,2},{5,3},{6,0},{7,1},{8,14},{9,15},{10,... | collective-permute-start | bytes 294920 | tf_op jit(solution)/shard_map/ppermute | solution.py:30
  200.3 6.0 %collective-permute-start.3 = (bf16[4,2,3072]{2,0,1:T(4,128)(2,1)S(1)}, bf16[4,2,3072]{2,0,1:T(4,128)(2,1)S(1)}, u32[]{:S(2)}, u32[]{:S(2)}) collective-permute-start(bf16[4,2,3072]{2,0,1:T(4,128)(2,1)S(1)} %fusion.46), channel_id=1, source_target_pairs={{0,8},{1,9},{2,10},{3,11},{4,12},{5,13},{6,14},{7,15},{8,0},{9,1},... | collective-permute-start | bytes 147464 | tf_op jit(solution)/shard_map/ppermute | solution.py:30
  206.3 6.9 %collective-permute-start.4 = (bf16[4,1,3072]{2,0,1:T(4,128)(2,1)S(1)}, bf16[4,1,3072]{2,0,1:T(4,128)(2,1)S(1)}, u32[]{:S(2)}, u32[]{:S(2)}) collective-permute-start(bf16[4,1,3072]{2,0,1:T(4,128)(2,1)S(1)} %fusion.49), channel_id=1, source_target_pairs={{0,24},{1,25},{2,26},{3,27},{4,28},{5,29},{6,30},{7,31},{8,16},{9,... | collective-permute-start | bytes 73736 | tf_op jit(solution)/shard_map/ppermute | solution.py:30
Sparse Core Ops, SparseCore 0:
  14.3 83.3 all-gather.2
  107.4 68.4 reduce-scatter.1

commit v5 on v4

--- a/solution.py
+++ b/solution.py
@@ -36,6 +36,23 @@
     bits = n.bit_length() - 1
     member_of = {v: e for e, v in enumerate(ring_label(n))}
     return [member_of[int(format(p, f"0{bits}b")[::-1], 2)] for p in range(n)]
+
+
+def state_prefix(decay, state, axis):
+    n = lax.axis_size(axis)
+    me = lax.axis_index(axis)
+    heads, width = state.shape[0], state.shape[1]
+    pack = jnp.concatenate([state, jnp.broadcast_to(decay[:, None, None], (heads, 8, width))], axis=1)
+    got = lax.ppermute(pack, axis, [(i, i + 1) for i in range(n - 1)])
+    pack = jnp.where(me == 0, jnp.concatenate([jnp.zeros_like(state), jnp.ones((heads, 8, width), state.dtype)], axis=1), got)
+    shift = 1
+    while shift < n:
+        got = lax.ppermute(pack, axis, [(i, i + shift) for i in range(n - shift)])
+        d_mine = pack[:, width:width + 1, :]
+        fresh = jnp.concatenate([d_mine * got[:, :width] + pack[:, :width], d_mine * got[:, width:]], axis=1)
+        pack = jnp.where(me >= shift, fresh, pack)
+        shift *= 2
+    return pack[:, :width]
 
 
 def shards(
@@ -98,20 +115,13 @@
     slot_rows = jnp.dot(token_pick, normed, preferred_element_type=jnp.float32).astype(jnp.bfloat16)
 
     model = normed.shape[1]
-    decay_hi = carry_decay.astype(jnp.bfloat16)
-    decay_lo = (carry_decay - decay_hi.astype(jnp.float32)).astype(jnp.bfloat16)
 
     def as_slab(v):
         v = v.reshape(-1)
         r = -(-v.shape[0] // model)
         return jnp.pad(v, (0, r * model - v.shape[0])).reshape(r, model)
 
-    pieces = [
-        slot_rows,
-        as_slab(out_weight),
-        as_slab(local_state.astype(jnp.bfloat16)),
-        as_slab(jnp.concatenate([decay_hi, decay_lo])),
-    ]
+    pieces = [slot_rows, as_slab(out_weight)]
     sizes = [p.shape[0] for p in pieces]
     slab = jnp.concatenate(pieces)
     total = slab.shape[0]
@@ -125,21 +135,7 @@
         .reshape(n_seq, -1)[:, : out_weight.size]
         .reshape(n_seq * out_weight.shape[0], out_weight.shape[1])
     )
-    states = (
-        gathered[:, offsets[2] : offsets[2] + sizes[2]]
-        .reshape(n_seq, -1)[:, : local_state.size]
-        .reshape(n_seq, heads_here, width, width)
-    )
-    decays = gathered[:, offsets[3], : 2 * heads_here].astype(jnp.float32)
-    decays = decays[:, :heads_here] + decays[:, heads_here:]
-
-    blocks = jnp.arange(n_seq)
-    between = (blocks[:, None] < blocks[None, :]) & (blocks[None, :] < me_seq)
-    factors = jnp.where(between[:, :, None], decays[None, :, :], 1.0)
-    reach = jnp.where((blocks < me_seq)[:, None], jnp.prod(factors, axis=1), 0.0)
-    state_in = jnp.einsum(
-        "jh,jhde->hde", reach, states.astype(jnp.float32), precision=lax.Precision.HIGHEST
-    )
+    state_in = state_prefix(carry_decay, local_state, "seq")
 
     lower = jnp.arange(rows)[:, None] >= jnp.arange(rows)[None, :]
     diff = cum[:, :, None] - cum[:, None, :]

time: 222 us -> 224 us (level)
  starting transfers between devices: 15 us -> 44.2 us
  waiting for transfers between devices: 150 us -> 131 us
  local copies, waits for them, and re-layouts: 20.2 us -> 13.9 us
    ppermute x0 -> x5, starting transfers between devices: none -> 29.7 us  [the longest x4 25.8 us: state_prefix(): got = lax.ppermute(pack, axis, [(i, i + shift) for i in range(n - shift)])]
    all_gather x1, waiting for transfers between devices: 82.1 us -> 62.6 us  [shards(): gathered = lax.all_gather(slab, 'seq', axis=0, tiled=False)]
    reduce_scatter x1, waiting for transfers between devices: 53.5 us -> 43.5 us  [shards(): lax.psum_scatter(expert_part.astype(jnp.bfloat16).reshape(n_seq, slots, -...]
    ppermute x0 -> x5, waiting for transfers between devices: none -> 8.26 us  [the longest x4 5.9 us: state_prefix(): got = lax.ppermute(pack, axis, [(i, i + shift) for i in range(n - shift)])]
    slice x2 -> x4, local copies, waits for them, and re-layouts: 3.56 us -> 0.01 us  [state_prefix(): d_mine = pack[:, width:width + 1, :]]
    unnamed x26, local copies, waits for them, and re-layouts: 3.87 us -> 1.07 us
  transfers between devices with their start and end apart: 7 -> 12, of which waited for: 7 -> 11; matrix products, arithmetic and copies ran while one was open for 7% -> 9% of each run, Pallas kernels for 0% -> 0%
where the time goes in v5:
time: 224 us
  waiting for transfers between devices  131 us (58%)
  starting transfers between devices  44.2 us (20%)
  between operations  17.1 us (8%)
  local copies, waits for them, and re-layouts  13.9 us (6%)
  matrix products  11.2 us (5%)
  other arithmetic  6.71 us (3%)
    all_gather x1, waiting for transfers between devices, shards(): gathered = lax.all_gather(slab, 'seq', axis=0, tiled=False)  62.6 us
    reduce_scatter x1, waiting for transfers between devices, shards(): lax.psum_scatter(expert_part.astype(jnp.bfloat16).reshape(n_seq, slots, -...  43.5 us
    ppermute x4, starting transfers between devices, state_prefix(): got = lax.ppermute(pack, axis, [(i, i + shift) for i in range(n - shift)])  25.8 us
    ppermute x5, waiting for transfers between devices, halving_scatter(): got = lax.ppermute(send.astype(jnp.bfloat16), axis, pairs)  16.1 us
    ppermute x5, starting transfers between devices, halving_scatter(): got = lax.ppermute(send.astype(jnp.bfloat16), axis, pairs)  14.5 us
    ppermute x4, waiting for transfers between devices, state_prefix(): got = lax.ppermute(pack, axis, [(i, i + shift) for i in range(n - shift)])  5.9 us
    dot_general x1, matrix products, shards(): jnp.dot(hidden, down_weight[0], preferred_element_type=jnp.float32)  5.68 us
  transfers between devices with their start and end apart: 12, of which 11 were waited for; matrix products, arithmetic and copies ran while one was open for 9% of the time, Pallas kernels for 0%

profile of v5, /device:TPU:6, one launch (start us, length us, event | category | flops | bytes accessed | tf_op | source)
XLA Modules:
  0.0 223.7 jit_solution(10855534032992657308)
XLA Ops:
  6.6 1.5 multiply_reduce_fusion
  13.7 3.8 %collective-permute-start = (f32[2,136,128]{2,1,0:T(8,128)S(1)}, f32[2,136,128]{2,1,0:T(8,128)S(1)}, u32[]{:S(2)}, u32[]{:S(2)}) collective-permute-start(f32[2,136,128]{2,1,0:T(8,128)S(1)} %pad_maximum_fusion.1), channel_id=1, source_target_pairs={{0,32},{32,64},{64,96},{96,128},{128,160},{160,192},{192,224},{224... | collective-permute-start | bytes 417800 | tf_op jit(solution)/shard_map/ppermute | solution.py:46
  18.1 2.4 %collective-permute-done = f32[2,136,128]{2,1,0:T(8,128)S(1)} collective-permute-done((f32[2,136,128]{2,1,0:T(8,128)S(1)}, f32[2,136,128]{2,1,0:T(8,128)S(1)}, u32[]{:S(2)}, u32[]{:S(2)}) %collective-permute-start) | collective-permute-done | bytes 139296 | tf_op jit(solution)/shard_map/ppermute | solution.py:46
  20.5 4.4 %collective-permute-start.1 = (f32[2,136,128]{2,1,0:T(8,128)S(1)}, f32[2,136,128]{2,1,0:T(8,128)S(1)}, u32[]{:S(2)}, u32[]{:S(2)}) collective-permute-start(f32[2,136,128]{2,1,0:T(8,128)S(1)} %broadcast_select_fusion), channel_id=1, source_target_pairs={{0,32},{32,64},{64,96},{96,128},{128,160},{160,192},{192,224},{224... | collective-permute-start | bytes 417800 | tf_op jit(solution)/shard_map/ppermute | solution.py:50
  25.7 1.7 collective-permute-done.1
  27.5 5.8 %collective-permute-start.2 = (f32[2,136,128]{2,1,0:T(8,128)S(1)}, f32[2,136,128]{2,1,0:T(8,128)S(1)}, u32[]{:S(2)}, u32[]{:S(2)}) collective-permute-start(f32[2,136,128]{2,1,0:T(8,128)S(1)} %maximum_select_fusion), channel_id=1, source_target_pairs={{0,64},{32,96},{64,128},{96,160},{128,192},{160,224},{192,256},{22... | collective-permute-start | bytes 417800 | tf_op jit(solution)/shard_map/ppermute | solution.py:50
  33.4 62.6 %all-gather.3.cloned.1.call-done = bf16[512,3072]{1,0:T(8,128)(2,1)} async-done(((bf16[32,3072]{1,0:T(8,128)(2,1)}), bf16[512,3072]{1,0:T(8,128)(2,1)}) %all-gather.3.cloned.1.call-update) | async-done | bytes 3145744 | tf_op jit(solution)/shard_map/all_gather | solution.py:130
  96.0 3.9 %fusion.55 = (bf16[16,16,3072]{2,1,0:T(8,128)(2,1)}, bf16[16,16,3072]{2,1,0:T(8,128)(2,1)}) fusion(bf16[16,32,3072]{2,1,0:T(8,128)(2,1)} %bitcast.192), kind=kLoop, calls=%fused_computation.113 | loop fusion | bytes 6291456 | tf_op jit(solution)/shard_map/slice | solution.py:134
  99.9 5.7 %convolution_convert_fusion = bf16[256,3072]{1,0:T(8,128)(2,1)} fusion(bf16[1,288,3072]{2,1,0:T(8,128)(2,1)S(1)} %copy-done, bf16[256,3072]{1,0:T(8,128)(2,1)} %bitcast.196, bf16[1,3072,288]{1,2,0:T(8,128)(2,1)} %param.21), kind=kOutput, calls=%fused_computation.2 | convolution fusion | flops 907124736 | bytes 6684672 | tf_op jit(solution)/shard_map/dot_general | solution.py:164
  105.7 4.6 %collective-permute-start.3 = (f32[2,136,128]{2,1,0:T(8,128)S(1)}, f32[2,136,128]{2,1,0:T(8,128)S(1)}, u32[]{:S(2)}, u32[]{:S(2)}) collective-permute-start(f32[2,136,128]{2,1,0:T(8,128)S(1)} %maximum_select_fusion.1), channel_id=1, source_target_pairs={{0,128},{32,160},{64,192},{96,224},{128,256},{160,288},{192,320},{... | collective-permute-start | bytes 417800 | tf_op jit(solution)/shard_map/ppermute | solution.py:50
  112.9 11.0 %collective-permute-start.4 = (f32[2,136,128]{2,1,0:T(8,128)S(1)}, f32[2,136,128]{2,1,0:T(8,128)S(1)}, u32[]{:S(2)}, u32[]{:S(2)}) collective-permute-start(f32[2,136,128]{2,1,0:T(8,128)S(1)} %maximum_select_fusion.2), channel_id=1, source_target_pairs={{0,256},{32,288},{64,320},{96,352},{128,384},{160,416},{192,448},{... | collective-permute-start | bytes 417800 | tf_op jit(solution)/shard_map/ppermute | solution.py:50
  124.1 3.1 %collective-permute-done.4 = f32[2,136,128]{2,1,0:T(8,128)S(1)} collective-permute-done((f32[2,136,128]{2,1,0:T(8,128)S(1)}, f32[2,136,128]{2,1,0:T(8,128)S(1)}, u32[]{:S(2)}, u32[]{:S(2)}) %collective-permute-start.4) | collective-permute-done | bytes 139296 | tf_op jit(solution)/shard_map/ppermute | solution.py:50
  128.7 4.3 %reshape_reshape.6 = bf16[3072,256]{1,0:T(8,128)(2,1)} reshape(bf16[16,16,3072]{2,1,0:T(8,128)(2,1)} %get-tuple-element.7) | data formatting | bytes 3145728 | tf_op jit(solution)/shard_map/reshape;reshape | solution.py:136
  133.0 43.5 %reduce-scatter.2.cloned.1.call-done = bf16[1,16,3072]{2,1,0:T(8,128)(2,1)} async-done(((bf16[16,16,3072]{2,1,0:T(8,128)(2,1)}), bf16[1,16,3072]{2,1,0:T(8,128)(2,1)}) %reduce-scatter.2.cloned.1.call-update) | async-done | bytes 98320 | tf_op jit(solution)/shard_map/reduce_scatter | solution.py:165
  180.0 1.9 collective-permute-start.5
  183.8 5.1 %collective-permute-start.6 = (bf16[4,8,3072]{2,1,0:T(8,128)(2,1)S(1)}, bf16[4,8,3072]{2,1,0:T(8,128)(2,1)S(1)}, u32[]{:S(2)}, u32[]{:S(2)}) collective-permute-start(bf16[4,8,3072]{2,1,0:T(8,128)(2,1)S(1)} %fusion.15), channel_id=1, source_target_pairs={{0,2},{1,3},{2,0},{3,1},{4,6},{5,7},{6,4},{7,5},{8,10},{9,11},{10,... | collective-permute-start | bytes 589832 | tf_op jit(solution)/shard_map/ppermute | solution.py:30
  189.6 4.5 %collective-permute-done.6 = bf16[4,8,3072]{2,1,0:T(8,128)(2,1)S(1)} collective-permute-done((bf16[4,8,3072]{2,1,0:T(8,128)(2,1)S(1)}, bf16[4,8,3072]{2,1,0:T(8,128)(2,1)S(1)}, u32[]{:S(2)}, u32[]{:S(2)}) %collective-permute-start.6) | collective-permute-done | bytes 196640 | tf_op jit(solution)/shard_map/ppermute | solution.py:30
  194.5 3.5 %collective-permute-start.7 = (bf16[4,4,3072]{2,0,1:T(4,128)(2,1)S(1)}, bf16[4,4,3072]{2,0,1:T(4,128)(2,1)S(1)}, u32[]{:S(2)}, u32[]{:S(2)}) collective-permute-start(bf16[4,4,3072]{2,0,1:T(4,128)(2,1)S(1)} %fusion.31), channel_id=1, source_target_pairs={{0,6},{1,7},{2,4},{3,5},{4,2},{5,3},{6,0},{7,1},{8,14},{9,15},{10,... | collective-permute-start | bytes 294920 | tf_op jit(solution)/shard_map/ppermute | solution.py:30
  198.7 3.5 %collective-permute-done.7 = bf16[4,4,3072]{2,0,1:T(4,128)(2,1)S(1)} collective-permute-done((bf16[4,4,3072]{2,0,1:T(4,128)(2,1)S(1)}, bf16[4,4,3072]{2,0,1:T(4,128)(2,1)S(1)}, u32[]{:S(2)}, u32[]{:S(2)}) %collective-permute-start.7) | collective-permute-done | bytes 98336 | tf_op jit(solution)/shard_map/ppermute | solution.py:30
  202.4 2.0 collective-permute-start.8
  205.0 3.4 %collective-permute-done.8 = bf16[4,2,3072]{2,0,1:T(4,128)(2,1)S(1)} collective-permute-done((bf16[4,2,3072]{2,0,1:T(4,128)(2,1)S(1)}, bf16[4,2,3072]{2,0,1:T(4,128)(2,1)S(1)}, u32[]{:S(2)}, u32[]{:S(2)}) %collective-permute-start.8) | collective-permute-done | bytes 49184 | tf_op jit(solution)/shard_map/ppermute | solution.py:30
  208.4 1.9 collective-permute-start.9
  211.7 3.7 %collective-permute-done.9 = bf16[4,1,3072]{2,0,1:T(4,128)(2,1)S(1)} collective-permute-done((bf16[4,1,3072]{2,0,1:T(4,128)(2,1)S(1)}, bf16[4,1,3072]{2,0,1:T(4,128)(2,1)S(1)}, u32[]{:S(2)}, u32[]{:S(2)}) %collective-permute-start.9) | collective-permute-done | bytes 24608 | tf_op jit(solution)/shard_map/ppermute | solution.py:30
  215.4 1.5 fusion.45
  (108 shorter events, 17.1 us)
Async XLA Ops:
  6.5 93.4 %copy-start = (bf16[1,288,3072]{2,1,0:T(8,128)(2,1)S(1)}, bf16[1,288,3072]{2,1,0:T(8,128)(2,1)}, u32[]{:S(2)}) copy-start(bf16[1,288,3072]{2,1,0:T(8,128)(2,1)} %param.22) | copy-start | bytes 5308420
  6.5 6.3 %copy-start.11 = (f32[2,128]{1,0:T(2,128)S(1)}, f32[2,128]{1,0:T(2,128)}, u32[]{:S(2)}) copy-start(f32[2,128]{1,0:T(2,128)} %param.16) | copy-start | bytes 3076
  6.5 6.7 %copy-start.6 = (bf16[128,256]{1,0:T(8,128)(2,1)S(1)}, bf16[128,256]{1,0:T(8,128)(2,1)}, u32[]{:S(2)}) copy-start(bf16[128,256]{1,0:T(8,128)(2,1)} %param.14) | copy-start | bytes 196612
  6.5 6.9 %copy-start.4 = (bf16[128,256]{1,0:T(8,128)(2,1)S(1)}, bf16[128,256]{1,0:T(8,128)(2,1)}, u32[]{:S(2)}) copy-start(bf16[128,256]{1,0:T(8,128)(2,1)} %param.15) | copy-start | bytes 196612
  6.5 89.4 %all-gather.3.cloned.1.call-start = ((), (), s32[]{:S(2)}) async-start(), calls=%async_computation.2 | async-start | bytes 3342336 | tf_op jit(solution)/shard_map/all_gather | solution.py:130
  6.6 11.0 %copy-start.1 = (bf16[128,3072]{1,0:T(8,128)(2,1)S(1)}, bf16[128,3072]{1,0:T(8,128)(2,1)}, u32[]{:S(2)}) copy-start(bf16[128,3072]{1,0:T(8,128)(2,1)} %param.17) | copy-start | bytes 2359300
  6.6 11.0 %copy-start.10 = (bf16[3072,32]{0,1:T(8,128)(2,1)S(1)}, bf16[3072,32]{0,1:T(8,128)(2,1)}, u32[]{:S(2)}) copy-start(bf16[3072,32]{0,1:T(8,128)(2,1)} %param.19) | copy-start | bytes 589828
  10.6 7.5 %copy-start.8 = (s32[128,2]{0,1:T(2,128)S(1)}, s32[128,2]{0,1:T(2,128)}, u32[]{:S(2)}) copy-start(s32[128,2]{0,1:T(2,128)} %param.20) | copy-start | bytes 3076
  10.6 9.9 %copy-start.5 = (f32[2,136,128]{2,1,0:T(8,128)S(1)}, f32[2,136,128]{2,1,0:T(8,128)}, u32[]{:S(2)}) copy-start(f32[2,136,128]{2,1,0:T(8,128)} %constant.63.clone.1) | copy-start | bytes 417796
  12.1 12.9 %copy-start.9 = (s32[32]{0:T(128)S(1)}, s32[32]{0:T(128)}, u32[]{:S(2)}) copy-start(s32[32]{0:T(128)} %constant.78) | copy-start | bytes 388
  12.8 163.7 %reduce-scatter.2.cloned.1.call-start = ((), (), s32[]{:S(2)}) async-start(), calls=%async_computation.1 | async-start | bytes 1671168 | tf_op jit(solution)/shard_map/reduce_scatter | solution.py:165
  13.7 6.7 %collective-permute-start = (f32[2,136,128]{2,1,0:T(8,128)S(1)}, f32[2,136,128]{2,1,0:T(8,128)S(1)}, u32[]{:S(2)}, u32[]{:S(2)}) collective-permute-start(f32[2,136,128]{2,1,0:T(8,128)S(1)} %pad_maximum_fusion.1), channel_id=1, source_target_pairs={{0,32},{32,64},{64,96},{96,128},{128,160},{160,192},{192,224},{224... | collective-permute-start | bytes 417800 | tf_op jit(solution)/shard_map/ppermute | solution.py:46
  20.5 7.0 %collective-permute-start.1 = (f32[2,136,128]{2,1,0:T(8,128)S(1)}, f32[2,136,128]{2,1,0:T(8,128)S(1)}, u32[]{:S(2)}, u32[]{:S(2)}) collective-permute-start(f32[2,136,128]{2,1,0:T(8,128)S(1)} %broadcast_select_fusion), channel_id=1, source_target_pairs={{0,32},{32,64},{64,96},{96,128},{128,160},{160,192},{192,224},{224... | collective-permute-start | bytes 417800 | tf_op jit(solution)/shard_map/ppermute | solution.py:50
  27.5 78.1 %collective-permute-start.2 = (f32[2,136,128]{2,1,0:T(8,128)S(1)}, f32[2,136,128]{2,1,0:T(8,128)S(1)}, u32[]{:S(2)}, u32[]{:S(2)}) collective-permute-start(f32[2,136,128]{2,1,0:T(8,128)S(1)} %maximum_select_fusion), channel_id=1, source_target_pairs={{0,64},{32,96},{64,128},{96,160},{128,192},{160,224},{192,256},{22... | collective-permute-start | bytes 417800 | tf_op jit(solution)/shard_map/ppermute | solution.py:50
  105.6 5.0 %copy-start.12 = (s32[32]{0:T(128)S(1)}, s32[32]{0:T(128)}, u32[]{:S(2)}) copy-start(s32[32]{0:T(128)} %constant.70.clone) | copy-start | bytes 388
  105.6 18.4 %copy-start.7 = (bf16[128,256]{1,0:T(8,128)(2,1)S(1)}, bf16[128,256]{1,0:T(8,128)(2,1)}, u32[]{:S(2)}) copy-start(bf16[128,256]{1,0:T(8,128)(2,1)} %param.13) | copy-start | bytes 196612
  105.7 7.2 %collective-permute-start.3 = (f32[2,136,128]{2,1,0:T(8,128)S(1)}, f32[2,136,128]{2,1,0:T(8,128)S(1)}, u32[]{:S(2)}, u32[]{:S(2)}) collective-permute-start(f32[2,136,128]{2,1,0:T(8,128)S(1)} %maximum_select_fusion.1), channel_id=1, source_target_pairs={{0,128},{32,160},{64,192},{96,224},{128,256},{160,288},{192,320},{... | collective-permute-start | bytes 417800 | tf_op jit(solution)/shard_map/ppermute | solution.py:50
  112.9 14.2 %collective-permute-start.4 = (f32[2,136,128]{2,1,0:T(8,128)S(1)}, f32[2,136,128]{2,1,0:T(8,128)S(1)}, u32[]{:S(2)}, u32[]{:S(2)}) collective-permute-start(f32[2,136,128]{2,1,0:T(8,128)S(1)} %maximum_select_fusion.2), channel_id=1, source_target_pairs={{0,256},{32,288},{64,320},{96,352},{128,384},{160,416},{192,448},{... | collective-permute-start | bytes 417800 | tf_op jit(solution)/shard_map/ppermute | solution.py:50
  177.9 1.4 copy-start.2
  180.0 3.6 %collective-permute-start.5 = (bf16[4,16,3072]{2,1,0:T(8,128)(2,1)S(1)}, bf16[4,16,3072]{2,1,0:T(8,128)(2,1)S(1)}, u32[]{:S(2)}, u32[]{:S(2)}) collective-permute-start(bf16[4,16,3072]{2,1,0:T(8,128)(2,1)S(1)} %fusion.6), channel_id=1, source_target_pairs={{0,1},{1,0},{2,3},{3,2},{4,5},{5,4},{6,7},{7,6},{8,9},{9,8},{10,11... | collective-permute-start | bytes 1179656 | tf_op jit(solution)/shard_map/ppermute | solution.py:30
  183.8 10.3 %collective-permute-start.6 = (bf16[4,8,3072]{2,1,0:T(8,128)(2,1)S(1)}, bf16[4,8,3072]{2,1,0:T(8,128)(2,1)S(1)}, u32[]{:S(2)}, u32[]{:S(2)}) collective-permute-start(bf16[4,8,3072]{2,1,0:T(8,128)(2,1)S(1)} %fusion.15), channel_id=1, source_target_pairs={{0,2},{1,3},{2,0},{3,1},{4,6},{5,7},{6,4},{7,5},{8,10},{9,11},{10,... | collective-permute-start | bytes 589832 | tf_op jit(solution)/shard_map/ppermute | solution.py:30
  194.5 7.7 %collective-permute-start.7 = (bf16[4,4,3072]{2,0,1:T(4,128)(2,1)S(1)}, bf16[4,4,3072]{2,0,1:T(4,128)(2,1)S(1)}, u32[]{:S(2)}, u32[]{:S(2)}) collective-permute-start(bf16[4,4,3072]{2,0,1:T(4,128)(2,1)S(1)} %fusion.31), channel_id=1, source_target_pairs={{0,6},{1,7},{2,4},{3,5},{4,2},{5,3},{6,0},{7,1},{8,14},{9,15},{10,... | collective-permute-start | bytes 294920 | tf_op jit(solution)/shard_map/ppermute | solution.py:30
  202.4 6.0 %collective-permute-start.8 = (bf16[4,2,3072]{2,0,1:T(4,128)(2,1)S(1)}, bf16[4,2,3072]{2,0,1:T(4,128)(2,1)S(1)}, u32[]{:S(2)}, u32[]{:S(2)}) collective-permute-start(bf16[4,2,3072]{2,0,1:T(4,128)(2,1)S(1)} %fusion.44), channel_id=1, source_target_pairs={{0,8},{1,9},{2,10},{3,11},{4,12},{5,13},{6,14},{7,15},{8,0},{9,1},... | collective-permute-start | bytes 147464 | tf_op jit(solution)/shard_map/ppermute | solution.py:30
  208.4 6.9 %collective-permute-start.9 = (bf16[4,1,3072]{2,0,1:T(4,128)(2,1)S(1)}, bf16[4,1,3072]{2,0,1:T(4,128)(2,1)S(1)}, u32[]{:S(2)}, u32[]{:S(2)}) collective-permute-start(bf16[4,1,3072]{2,0,1:T(4,128)(2,1)S(1)} %fusion.47), channel_id=1, source_target_pairs={{0,24},{1,25},{2,26},{3,27},{4,28},{5,29},{6,30},{7,31},{8,16},{9,... | collective-permute-start | bytes 73736 | tf_op jit(solution)/shard_map/ppermute | solution.py:30
  (1 other events, 1.4 us)
Sparse Core Ops, SparseCore 0:
  12.9 83.0 all-gather.2
  105.7 70.7 reduce-scatter.1

commit v6 on v5

--- a/solution.py
+++ b/solution.py
@@ -128,6 +128,7 @@
     padded = -(-total // 16) * 16
     slab = jnp.pad(slab, ((0, padded - total), (0, 0)))
     gathered = lax.all_gather(slab, "seq", axis=0, tiled=False)
+    gathered, state_in = lax.optimization_barrier((gathered, state_prefix(carry_decay, local_state, "seq")))
     offsets = [sum(sizes[:i]) for i in range(len(sizes))]
     gathered_rows = gathered[:, offsets[0] : offsets[0] + sizes[0]].reshape(n_seq * slots, model)
     full_weight = (
@@ -135,8 +136,6 @@
         .reshape(n_seq, -1)[:, : out_weight.size]
         .reshape(n_seq * out_weight.shape[0], out_weight.shape[1])
     )
-    state_in = state_prefix(carry_decay, local_state, "seq")
-
     lower = jnp.arange(rows)[:, None] >= jnp.arange(rows)[None, :]
     diff = cum[:, :, None] - cum[:, None, :]
     weight = jnp.where(lower[None], jnp.exp(jnp.where(lower[None], diff, 0.0)), 0.0)

time: 224 us -> 234 us (1.045)
  starting transfers between devices: 44.2 us -> 67.4 us
  waiting for transfers between devices: 131 us -> 117 us
    all_gather x1, waiting for transfers between devices: 62.6 us -> 24.1 us  [shards(): gathered = lax.all_gather(slab, 'seq', axis=0, tiled=False)]
    ppermute x4, starting transfers between devices: 25.8 us -> 48 us  [state_prefix(): got = lax.ppermute(pack, axis, [(i, i + shift) for i in range(n - shift)])]
    reduce_scatter x1, waiting for transfers between devices: 43.5 us -> 62.5 us  [shards(): lax.psum_scatter(expert_part.astype(jnp.bfloat16).reshape(n_seq, slots, -...]
    ppermute x4, waiting for transfers between devices: 5.9 us -> 13.6 us  [state_prefix(): got = lax.ppermute(pack, axis, [(i, i + shift) for i in range(n - shift)])]
    ppermute x5, waiting for transfers between devices: 16.1 us -> 13.7 us  [halving_scatter(): got = lax.ppermute(send.astype(jnp.bfloat16), axis, pairs)]
  transfers between devices with their start and end apart: 12 -> 12, of which waited for: 11 -> 12; matrix products, arithmetic and copies ran while one was open for 9% -> 4% of each run, Pallas kernels for 0% -> 0%
where the time goes in v6:
time: 234 us; the launch traced here: 233 us
  waiting for transfers between devices  117 us (50%)
  starting transfers between devices  67.4 us (29%)
  between operations  17.1 us (7%)
  local copies, waits for them, and re-layouts  14.5 us (6%)
  matrix products  10.7 us (5%)
  other arithmetic  6.8 us (3%)
    reduce_scatter x1, waiting for transfers between devices, shards(): lax.psum_scatter(expert_part.astype(jnp.bfloat16).reshape(n_seq, slots, -...  62.5 us
    ppermute x4, starting transfers between devices, state_prefix(): got = lax.ppermute(pack, axis, [(i, i + shift) for i in range(n - shift)])  48 us
    all_gather x1, waiting for transfers between devices, shards(): gathered = lax.all_gather(slab, 'seq', axis=0, tiled=False)  24.1 us
    ppermute x5, starting transfers between devices, halving_scatter(): got = lax.ppermute(send.astype(jnp.bfloat16), axis, pairs)  15.5 us
    ppermute x5, waiting for transfers between devices, halving_scatter(): got = lax.ppermute(send.astype(jnp.bfloat16), axis, pairs)  13.7 us
    ppermute x4, waiting for transfers between devices, state_prefix(): got = lax.ppermute(pack, axis, [(i, i + shift) for i in range(n - shift)])  13.6 us
    dot_general x1, matrix products, shards(): jnp.dot(hidden, down_weight[0], preferred_element_type=jnp.float32)  5.22 us
  transfers between devices with their start and end apart: 12, of which 12 were waited for; matrix products, arithmetic and copies ran while one was open for 4% of the time, Pallas kernels for 0%

profile of v6, /device:TPU:6, one launch (start us, length us, event | category | flops | bytes accessed | tf_op | source)
XLA Modules:
  0.0 233.5 jit_solution(9746349916543076240)
XLA Ops:
  13.8 3.8 %collective-permute-start = (f32[2,136,128]{2,1,0:T(8,128)S(1)}, f32[2,136,128]{2,1,0:T(8,128)S(1)}, u32[]{:S(2)}, u32[]{:S(2)}) collective-permute-start(f32[2,136,128]{2,1,0:T(8,128)S(1)} %pad_maximum_fusion.1), channel_id=1, source_target_pairs={{0,32},{32,64},{64,96},{96,128},{128,160},{160,192},{192,224},{224... | collective-permute-start | bytes 417800 | tf_op jit(solution)/shard_map/ppermute | solution.py:46
  17.6 2.9 %collective-permute-done = f32[2,136,128]{2,1,0:T(8,128)S(1)} collective-permute-done((f32[2,136,128]{2,1,0:T(8,128)S(1)}, f32[2,136,128]{2,1,0:T(8,128)S(1)}, u32[]{:S(2)}, u32[]{:S(2)}) %collective-permute-start) | collective-permute-done | bytes 139296 | tf_op jit(solution)/shard_map/ppermute | solution.py:46
  20.5 4.4 %collective-permute-start.1 = (f32[2,136,128]{2,1,0:T(8,128)S(1)}, f32[2,136,128]{2,1,0:T(8,128)S(1)}, u32[]{:S(2)}, u32[]{:S(2)}) collective-permute-start(f32[2,136,128]{2,1,0:T(8,128)S(1)} %broadcast_select_fusion), channel_id=1, source_target_pairs={{0,32},{32,64},{64,96},{96,128},{128,160},{160,192},{192,224},{224... | collective-permute-start | bytes 417800 | tf_op jit(solution)/shard_map/ppermute | solution.py:50
  24.9 2.6 %collective-permute-done.1 = f32[2,136,128]{2,1,0:T(8,128)S(1)} collective-permute-done((f32[2,136,128]{2,1,0:T(8,128)S(1)}, f32[2,136,128]{2,1,0:T(8,128)S(1)}, u32[]{:S(2)}, u32[]{:S(2)}) %collective-permute-start.1) | collective-permute-done | bytes 139296 | tf_op jit(solution)/shard_map/ppermute | solution.py:50
  27.6 5.8 %collective-permute-start.2 = (f32[2,136,128]{2,1,0:T(8,128)S(1)}, f32[2,136,128]{2,1,0:T(8,128)S(1)}, u32[]{:S(2)}, u32[]{:S(2)}) collective-permute-start(f32[2,136,128]{2,1,0:T(8,128)S(1)} %maximum_select_fusion), channel_id=1, source_target_pairs={{0,64},{32,96},{64,128},{96,160},{128,192},{160,224},{192,256},{22... | collective-permute-start | bytes 417800 | tf_op jit(solution)/shard_map/ppermute | solution.py:50
  33.4 3.7 %collective-permute-done.2 = f32[2,136,128]{2,1,0:T(8,128)S(1)} collective-permute-done((f32[2,136,128]{2,1,0:T(8,128)S(1)}, f32[2,136,128]{2,1,0:T(8,128)S(1)}, u32[]{:S(2)}, u32[]{:S(2)}) %collective-permute-start.2) | collective-permute-done | bytes 139296 | tf_op jit(solution)/shard_map/ppermute | solution.py:50
  37.1 16.8 %collective-permute-start.3 = (f32[2,136,128]{2,1,0:T(8,128)S(1)}, f32[2,136,128]{2,1,0:T(8,128)S(1)}, u32[]{:S(2)}, u32[]{:S(2)}) collective-permute-start(f32[2,136,128]{2,1,0:T(8,128)S(1)} %maximum_select_fusion.1), channel_id=1, source_target_pairs={{0,128},{32,160},{64,192},{96,224},{128,256},{160,288},{192,320},{... | collective-permute-start | bytes 417800 | tf_op jit(solution)/shard_map/ppermute | solution.py:50
  53.9 4.1 %collective-permute-done.3 = f32[2,136,128]{2,1,0:T(8,128)S(1)} collective-permute-done((f32[2,136,128]{2,1,0:T(8,128)S(1)}, f32[2,136,128]{2,1,0:T(8,128)S(1)}, u32[]{:S(2)}, u32[]{:S(2)}) %collective-permute-start.3) | collective-permute-done | bytes 139296 | tf_op jit(solution)/shard_map/ppermute | solution.py:50
  58.1 21.1 %collective-permute-start.4 = (f32[2,136,128]{2,1,0:T(8,128)S(1)}, f32[2,136,128]{2,1,0:T(8,128)S(1)}, u32[]{:S(2)}, u32[]{:S(2)}) collective-permute-start(f32[2,136,128]{2,1,0:T(8,128)S(1)} %maximum_select_fusion.2), channel_id=1, source_target_pairs={{0,256},{32,288},{64,320},{96,352},{128,384},{160,416},{192,448},{... | collective-permute-start | bytes 417800 | tf_op jit(solution)/shard_map/ppermute | solution.py:50
  79.2 3.3 %collective-permute-done.4 = f32[2,136,128]{2,1,0:T(8,128)S(1)} collective-permute-done((f32[2,136,128]{2,1,0:T(8,128)S(1)}, f32[2,136,128]{2,1,0:T(8,128)S(1)}, u32[]{:S(2)}, u32[]{:S(2)}) %collective-permute-start.4) | collective-permute-done | bytes 139296 | tf_op jit(solution)/shard_map/ppermute | solution.py:50
  82.5 24.1 %all-gather.3.cloned.1.call-done = bf16[512,3072]{1,0:T(8,128)(2,1)} async-done(((bf16[32,3072]{1,0:T(8,128)(2,1)}), bf16[512,3072]{1,0:T(8,128)(2,1)}) %all-gather.3.cloned.1.call-update) | async-done | bytes 3145744 | tf_op jit(solution)/shard_map/all_gather | solution.py:130
  106.7 3.3 %fusion.50 = (bf16[16,16,3072]{2,1,0:T(8,128)(2,1)}, bf16[16,16,3072]{2,1,0:T(8,128)(2,1)S(1)}) fusion(bf16[16,32,3072]{2,1,0:T(8,128)(2,1)} %bitcast.193), kind=kLoop, calls=%fused_computation.109 | loop fusion | bytes 6291456 | tf_op jit(solution)/shard_map/slice | solution.py:135
  110.0 5.2 %convolution_convert_fusion = bf16[256,3072]{1,0:T(8,128)(2,1)} fusion(bf16[1,288,3072]{2,1,0:T(8,128)(2,1)S(1)} %copy-done, bf16[256,3072]{1,0:T(8,128)(2,1)S(1)} %bitcast.197, bf16[1,3072,288]{1,2,0:T(8,128)(2,1)} %param.21), kind=kOutput, calls=%fused_computation.2 | convolution fusion | flops 907124736 | bytes 6684672 | tf_op jit(solution)/shard_map/dot_general | solution.py:163
  120.9 4.3 %reshape_reshape.6 = bf16[3072,256]{1,0:T(8,128)(2,1)} reshape(bf16[16,16,3072]{2,1,0:T(8,128)(2,1)} %get-tuple-element.11) | data formatting | bytes 3145728 | tf_op jit(solution)/shard_map/reshape;reshape | solution.py:137
  125.2 62.5 %reduce-scatter.2.cloned.1.call-done = bf16[1,16,3072]{2,1,0:T(8,128)(2,1)} async-done(((bf16[16,16,3072]{2,1,0:T(8,128)(2,1)}), bf16[1,16,3072]{2,1,0:T(8,128)(2,1)}) %reduce-scatter.2.cloned.1.call-update) | async-done | bytes 98320 | tf_op jit(solution)/shard_map/reduce_scatter | solution.py:164
  191.2 1.9 collective-permute-start.5
  195.1 3.6 %collective-permute-start.6 = (bf16[4,8,3072]{2,1,0:T(8,128)(2,1)S(1)}, bf16[4,8,3072]{2,1,0:T(8,128)(2,1)S(1)}, u32[]{:S(2)}, u32[]{:S(2)}) collective-permute-start(bf16[4,8,3072]{2,1,0:T(8,128)(2,1)S(1)} %fusion.15), channel_id=1, source_target_pairs={{0,2},{1,3},{2,0},{3,1},{4,6},{5,7},{6,4},{7,5},{8,10},{9,11},{10,... | collective-permute-start | bytes 589832 | tf_op jit(solution)/shard_map/ppermute | solution.py:30
  199.2 4.6 %collective-permute-done.6 = bf16[4,8,3072]{2,1,0:T(8,128)(2,1)S(1)} collective-permute-done((bf16[4,8,3072]{2,1,0:T(8,128)(2,1)S(1)}, bf16[4,8,3072]{2,1,0:T(8,128)(2,1)S(1)}, u32[]{:S(2)}, u32[]{:S(2)}) %collective-permute-start.6) | collective-permute-done | bytes 196640 | tf_op jit(solution)/shard_map/ppermute | solution.py:30
  204.3 4.7 %collective-permute-start.7 = (bf16[4,4,3072]{2,0,1:T(4,128)(2,1)S(1)}, bf16[4,4,3072]{2,0,1:T(4,128)(2,1)S(1)}, u32[]{:S(2)}, u32[]{:S(2)}) collective-permute-start(bf16[4,4,3072]{2,0,1:T(4,128)(2,1)S(1)} %fusion.27), channel_id=1, source_target_pairs={{0,6},{1,7},{2,4},{3,5},{4,2},{5,3},{6,0},{7,1},{8,14},{9,15},{10,... | collective-permute-start | bytes 294920 | tf_op jit(solution)/shard_map/ppermute | solution.py:30
  209.7 2.3 %collective-permute-done.7 = bf16[4,4,3072]{2,0,1:T(4,128)(2,1)S(1)} collective-permute-done((bf16[4,4,3072]{2,0,1:T(4,128)(2,1)S(1)}, bf16[4,4,3072]{2,0,1:T(4,128)(2,1)S(1)}, u32[]{:S(2)}, u32[]{:S(2)}) %collective-permute-start.7) | collective-permute-done | bytes 98336 | tf_op jit(solution)/shard_map/ppermute | solution.py:30
  212.1 2.8 %collective-permute-start.8 = (bf16[4,2,3072]{2,0,1:T(4,128)(2,1)S(1)}, bf16[4,2,3072]{2,0,1:T(4,128)(2,1)S(1)}, u32[]{:S(2)}, u32[]{:S(2)}) collective-permute-start(bf16[4,2,3072]{2,0,1:T(4,128)(2,1)S(1)} %fusion.40), channel_id=1, source_target_pairs={{0,8},{1,9},{2,10},{3,11},{4,12},{5,13},{6,14},{7,15},{8,0},{9,1},... | collective-permute-start | bytes 147464 | tf_op jit(solution)/shard_map/ppermute | solution.py:30
  215.5 2.6 %collective-permute-done.8 = bf16[4,2,3072]{2,0,1:T(4,128)(2,1)S(1)} collective-permute-done((bf16[4,2,3072]{2,0,1:T(4,128)(2,1)S(1)}, bf16[4,2,3072]{2,0,1:T(4,128)(2,1)S(1)}, u32[]{:S(2)}, u32[]{:S(2)}) %collective-permute-start.8) | collective-permute-done | bytes 49184 | tf_op jit(solution)/shard_map/ppermute | solution.py:30
  218.2 2.5 %collective-permute-start.9 = (bf16[4,1,3072]{2,0,1:T(4,128)(2,1)S(1)}, bf16[4,1,3072]{2,0,1:T(4,128)(2,1)S(1)}, u32[]{:S(2)}, u32[]{:S(2)}) collective-permute-start(bf16[4,1,3072]{2,0,1:T(4,128)(2,1)S(1)} %fusion.43), channel_id=1, source_target_pairs={{0,24},{1,25},{2,26},{3,27},{4,28},{5,29},{6,30},{7,31},{8,16},{9,... | collective-permute-start | bytes 73736 | tf_op jit(solution)/shard_map/ppermute | solution.py:30
  222.0 3.1 %collective-permute-done.9 = bf16[4,1,3072]{2,0,1:T(4,128)(2,1)S(1)} collective-permute-done((bf16[4,1,3072]{2,0,1:T(4,128)(2,1)S(1)}, bf16[4,1,3072]{2,0,1:T(4,128)(2,1)S(1)}, u32[]{:S(2)}, u32[]{:S(2)}) %collective-permute-start.9) | collective-permute-done | bytes 24608 | tf_op jit(solution)/shard_map/ppermute | solution.py:30
  (121 shorter events, 20.3 us)
Async XLA Ops:
  6.5 103.5 %copy-start = (bf16[1,288,3072]{2,1,0:T(8,128)(2,1)S(1)}, bf16[1,288,3072]{2,1,0:T(8,128)(2,1)}, u32[]{:S(2)}) copy-start(bf16[1,288,3072]{2,1,0:T(8,128)(2,1)} %param.22) | copy-start | bytes 5308420
  6.5 6.3 %copy-start.9 = (bf16[128,256]{1,0:T(8,128)(2,1)S(1)}, bf16[128,256]{1,0:T(8,128)(2,1)}, u32[]{:S(2)}) copy-start(bf16[128,256]{1,0:T(8,128)(2,1)} %param.14) | copy-start | bytes 196612
  6.5 6.4 %copy-start.17 = (f32[2,128]{1,0:T(2,128)S(1)}, f32[2,128]{1,0:T(2,128)}, u32[]{:S(2)}) copy-start(f32[2,128]{1,0:T(2,128)} %param.16) | copy-start | bytes 3076
  6.5 6.8 %copy-start.4 = (bf16[128,256]{1,0:T(8,128)(2,1)S(1)}, bf16[128,256]{1,0:T(8,128)(2,1)}, u32[]{:S(2)}) copy-start(bf16[128,256]{1,0:T(8,128)(2,1)} %param.15) | copy-start | bytes 196612
  6.5 100.1 %all-gather.3.cloned.1.call-start = ((), (), s32[]{:S(2)}) async-start(), calls=%async_computation.2 | async-start | bytes 3342336 | tf_op jit(solution)/shard_map/all_gather | solution.py:130
  8.1 12.4 %copy-start.7 = (f32[2,136,128]{2,1,0:T(8,128)S(1)}, f32[2,136,128]{2,1,0:T(8,128)}, u32[]{:S(2)}) copy-start(f32[2,136,128]{2,1,0:T(8,128)} %constant.65.clone.1) | copy-start | bytes 417796
  9.5 4.1 %copy-start.13 = (f32[128]{0:T(128)}, f32[128]{0:T(128)S(1)}, u32[]{:S(2)}) copy-start(f32[128]{0:T(128)S(1)} %add_rsqrt_fusion) | copy-start | bytes 1540
  12.7 175.0 %reduce-scatter.2.cloned.1.call-start = ((), (), s32[]{:S(2)}) async-start(), calls=%async_computation.1 | async-start | bytes 1671168 | tf_op jit(solution)/shard_map/reduce_scatter | solution.py:164
  12.9 14.6 %copy-start.5 = (bf16[128,256]{0,1:T(8,128)(2,1)}, bf16[128,256]{0,1:T(8,128)(2,1)S(1)}, u32[]{:S(2)}) copy-start(bf16[128,256]{0,1:T(8,128)(2,1)S(1)} %copy.126) | copy-start | bytes 196612
  13.8 6.7 %collective-permute-start = (f32[2,136,128]{2,1,0:T(8,128)S(1)}, f32[2,136,128]{2,1,0:T(8,128)S(1)}, u32[]{:S(2)}, u32[]{:S(2)}) collective-permute-start(f32[2,136,128]{2,1,0:T(8,128)S(1)} %pad_maximum_fusion.1), channel_id=1, source_target_pairs={{0,32},{32,64},{64,96},{96,128},{128,160},{160,192},{192,224},{224... | collective-permute-start | bytes 417800 | tf_op jit(solution)/shard_map/ppermute | solution.py:46
  20.5 7.0 %collective-permute-start.1 = (f32[2,136,128]{2,1,0:T(8,128)S(1)}, f32[2,136,128]{2,1,0:T(8,128)S(1)}, u32[]{:S(2)}, u32[]{:S(2)}) collective-permute-start(f32[2,136,128]{2,1,0:T(8,128)S(1)} %broadcast_select_fusion), channel_id=1, source_target_pairs={{0,32},{32,64},{64,96},{96,128},{128,160},{160,192},{192,224},{224... | collective-permute-start | bytes 417800 | tf_op jit(solution)/shard_map/ppermute | solution.py:50
  27.6 9.5 %collective-permute-start.2 = (f32[2,136,128]{2,1,0:T(8,128)S(1)}, f32[2,136,128]{2,1,0:T(8,128)S(1)}, u32[]{:S(2)}, u32[]{:S(2)}) collective-permute-start(f32[2,136,128]{2,1,0:T(8,128)S(1)} %maximum_select_fusion), channel_id=1, source_target_pairs={{0,64},{32,96},{64,128},{96,160},{128,192},{160,224},{192,256},{22... | collective-permute-start | bytes 417800 | tf_op jit(solution)/shard_map/ppermute | solution.py:50
  37.1 20.9 %collective-permute-start.3 = (f32[2,136,128]{2,1,0:T(8,128)S(1)}, f32[2,136,128]{2,1,0:T(8,128)S(1)}, u32[]{:S(2)}, u32[]{:S(2)}) collective-permute-start(f32[2,136,128]{2,1,0:T(8,128)S(1)} %maximum_select_fusion.1), channel_id=1, source_target_pairs={{0,128},{32,160},{64,192},{96,224},{128,256},{160,288},{192,320},{... | collective-permute-start | bytes 417800 | tf_op jit(solution)/shard_map/ppermute | solution.py:50
  58.1 24.4 %collective-permute-start.4 = (f32[2,136,128]{2,1,0:T(8,128)S(1)}, f32[2,136,128]{2,1,0:T(8,128)S(1)}, u32[]{:S(2)}, u32[]{:S(2)}) collective-permute-start(f32[2,136,128]{2,1,0:T(8,128)S(1)} %maximum_select_fusion.2), channel_id=1, source_target_pairs={{0,256},{32,288},{64,320},{96,352},{128,384},{160,416},{192,448},{... | collective-permute-start | bytes 417800 | tf_op jit(solution)/shard_map/ppermute | solution.py:50
  115.2 1.8 copy-start.15
  115.2 2.7 %copy-start.18 = (s32[32]{0:T(128)S(1)}, s32[32]{0:T(128)}, u32[]{:S(2)}) copy-start(s32[32]{0:T(128)} %constant.70.clone) | copy-start | bytes 388
  115.2 4.0 %copy-start.6 = (bf16[128,256]{0,1:T(8,128)(2,1)S(1)}, bf16[128,256]{0,1:T(8,128)(2,1)}, u32[]{:S(2)}) copy-start(bf16[128,256]{0,1:T(8,128)(2,1)} %copy-done.5) | copy-start | bytes 196612
  115.3 4.0 %copy-start.8 = (bf16[128,256]{1,0:T(8,128)(2,1)S(1)}, bf16[128,256]{1,0:T(8,128)(2,1)}, u32[]{:S(2)}) copy-start(bf16[128,256]{1,0:T(8,128)(2,1)} %param.13) | copy-start | bytes 196612
  115.3 4.0 %copy-start.12 = (f32[128,2]{0,1:T(2,128)S(1)}, f32[128,2]{0,1:T(2,128)}, u32[]{:S(2)}) copy-start(f32[128,2]{0,1:T(2,128)} %copy-done.11) | copy-start | bytes 3076
  191.2 3.6 %collective-permute-start.5 = (bf16[4,16,3072]{2,1,0:T(8,128)(2,1)S(1)}, bf16[4,16,3072]{2,1,0:T(8,128)(2,1)S(1)}, u32[]{:S(2)}, u32[]{:S(2)}) collective-permute-start(bf16[4,16,3072]{2,1,0:T(8,128)(2,1)S(1)} %fusion.6), channel_id=1, source_target_pairs={{0,1},{1,0},{2,3},{3,2},{4,5},{5,4},{6,7},{7,6},{8,9},{9,8},{10,11... | collective-permute-start | bytes 1179656 | tf_op jit(solution)/shard_map/ppermute | solution.py:30
  195.1 8.8 %collective-permute-start.6 = (bf16[4,8,3072]{2,1,0:T(8,128)(2,1)S(1)}, bf16[4,8,3072]{2,1,0:T(8,128)(2,1)S(1)}, u32[]{:S(2)}, u32[]{:S(2)}) collective-permute-start(bf16[4,8,3072]{2,1,0:T(8,128)(2,1)S(1)} %fusion.15), channel_id=1, source_target_pairs={{0,2},{1,3},{2,0},{3,1},{4,6},{5,7},{6,4},{7,5},{8,10},{9,11},{10,... | collective-permute-start | bytes 589832 | tf_op jit(solution)/shard_map/ppermute | solution.py:30
  204.3 7.7 %collective-permute-start.7 = (bf16[4,4,3072]{2,0,1:T(4,128)(2,1)S(1)}, bf16[4,4,3072]{2,0,1:T(4,128)(2,1)S(1)}, u32[]{:S(2)}, u32[]{:S(2)}) collective-permute-start(bf16[4,4,3072]{2,0,1:T(4,128)(2,1)S(1)} %fusion.27), channel_id=1, source_target_pairs={{0,6},{1,7},{2,4},{3,5},{4,2},{5,3},{6,0},{7,1},{8,14},{9,15},{10,... | collective-permute-start | bytes 294920 | tf_op jit(solution)/shard_map/ppermute | solution.py:30
  212.1 6.0 %collective-permute-start.8 = (bf16[4,2,3072]{2,0,1:T(4,128)(2,1)S(1)}, bf16[4,2,3072]{2,0,1:T(4,128)(2,1)S(1)}, u32[]{:S(2)}, u32[]{:S(2)}) collective-permute-start(bf16[4,2,3072]{2,0,1:T(4,128)(2,1)S(1)} %fusion.40), channel_id=1, source_target_pairs={{0,8},{1,9},{2,10},{3,11},{4,12},{5,13},{6,14},{7,15},{8,0},{9,1},... | collective-permute-start | bytes 147464 | tf_op jit(solution)/shard_map/ppermute | solution.py:30
  218.2 6.9 %collective-permute-start.9 = (bf16[4,1,3072]{2,0,1:T(4,128)(2,1)S(1)}, bf16[4,1,3072]{2,0,1:T(4,128)(2,1)S(1)}, u32[]{:S(2)}, u32[]{:S(2)}) collective-permute-start(bf16[4,1,3072]{2,0,1:T(4,128)(2,1)S(1)} %fusion.43), channel_id=1, source_target_pairs={{0,24},{1,25},{2,26},{3,27},{4,28},{5,29},{6,30},{7,31},{8,16},{9,... | collective-permute-start | bytes 73736 | tf_op jit(solution)/shard_map/ppermute | solution.py:30
  (7 other events, 8.4 us)
Sparse Core Ops, SparseCore 0:
  12.9 93.7 all-gather.2
  115.4 72.2 reduce-scatter.1

commit v7 on v4

--- a/solution.py
+++ b/solution.py
@@ -69,7 +69,12 @@
     last = cum[:, -1:]
     carry_decay = jnp.exp(last[:, 0])
     kscaled = kloc * jnp.exp(last - cum)[:, :, None]
-    local_state = jnp.einsum("hjd,hje->hde", kscaled, vloc, precision=lax.Precision.HIGHEST)
+    kscaled_hi = kscaled.astype(jnp.bfloat16)
+    kscaled_lo = (kscaled - kscaled_hi.astype(jnp.float32)).astype(jnp.bfloat16)
+    vbf = values.reshape(rows, heads_here, width).transpose(1, 0, 2)
+    local_state = jnp.einsum(
+        "hjd,hje->hde", kscaled_hi, vbf, preferred_element_type=jnp.float32
+    ) + jnp.einsum("hjd,hje->hde", kscaled_lo, vbf, preferred_element_type=jnp.float32)
 
     stream = residual.astype(jnp.float32)
     normed = (stream * lax.rsqrt(jnp.mean(stream * stream, axis=-1, keepdims=True) + 1e-05)).astype(
@@ -181,7 +186,7 @@
     partial = (projected + contribution).reshape(per, n_exp, -1)
     summed = halving_scatter(partial, "exp")
     own_rows = summed.shape[0]
-    own = lax.dynamic_slice_in_dim(stream, owner * own_rows, own_rows, 0)
+    own = lax.dynamic_slice_in_dim(residual, owner * own_rows, own_rows, 0).astype(jnp.float32)
     return (own + summed).astype(jnp.bfloat16)
 
 

time: 222 us -> 222 us (level)
  matrix products: 12.7 us -> 15 us
    unnamed x26 -> x36, local copies, waits for them, and re-layouts: 3.87 us -> 4.72 us
  transfers between devices with their start and end apart: 7 -> 7, of which waited for: 7 -> 7; matrix products, arithmetic and copies ran while one was open for 7% -> 6% of each run, Pallas kernels for 0% -> 0%
where the time goes in v7:
time: 222 us
  waiting for transfers between devices  151 us (68%)
  local copies, waits for them, and re-layouts  18.8 us (8%)
  between operations  17.3 us (8%)
  starting transfers between devices  15.2 us (7%)
  matrix products  15 us (7%)
  other arithmetic  4.69 us (2%)
    all_gather x1, waiting for transfers between devices, shards(): gathered = lax.all_gather(slab, 'seq', axis=0, tiled=False)  82.1 us
    reduce_scatter x1, waiting for transfers between devices, shards(): lax.psum_scatter(expert_part.astype(jnp.bfloat16).reshape(n_seq, slots, -...  53.3 us
    ppermute x5, waiting for transfers between devices, halving_scatter(): got = lax.ppermute(send.astype(jnp.bfloat16), axis, pairs)  15.3 us
    ppermute x5, starting transfers between devices, halving_scatter(): got = lax.ppermute(send.astype(jnp.bfloat16), axis, pairs)  15.1 us
    dot_general x1, matrix products, shards(): jnp.dot(hidden, down_weight[0], preferred_element_type=jnp.float32)  5.7 us
    unnamed x36, local copies, waits for them, and re-layouts  4.72 us
  transfers between devices with their start and end apart: 7, of which 7 were waited for; matrix products, arithmetic and copies ran while one was open for 6% of the time, Pallas kernels for 0%

profile of v7, /device:TPU:6, one launch (start us, length us, event | category | flops | bytes accessed | tf_op | source)
XLA Modules:
  0.0 221.7 jit_solution(5382611523821620296)
XLA Ops:
  6.6 1.6 fusion.69
  9.8 1.0 fusion.42
  10.8 1.0 fusion.5
  16.4 82.1 %all-gather.3.cloned.1.call-done = bf16[768,3072]{1,0:T(8,128)(2,1)} async-done(((bf16[48,3072]{1,0:T(8,128)(2,1)}), bf16[768,3072]{1,0:T(8,128)(2,1)}) %all-gather.3.cloned.1.call-update) | async-done | bytes 4718608 | tf_op jit(solution)/shard_map/all_gather | solution.py:125
  98.5 3.3 %fusion.68 = (bf16[16,16,3072]{2,1,0:T(8,128)(2,1)S(1)}, bf16[16,16,3072]{2,1,0:T(8,128)(2,1)}) fusion(bf16[16,48,3072]{2,1,0:T(8,128)(2,1)} %bitcast.211), kind=kLoop, calls=%fused_computation.120 | loop fusion | bytes 6291456 | tf_op jit(solution)/shard_map/slice | solution.py:129
  101.8 5.7 %convolution_convert_fusion = bf16[256,3072]{1,0:T(8,128)(2,1)} fusion(bf16[1,288,3072]{2,1,0:T(8,128)(2,1)S(1)} %copy-done, bf16[256,3072]{1,0:T(8,128)(2,1)} %bitcast.219, bf16[1,3072,288]{1,2,0:T(8,128)(2,1)} %param.21), kind=kOutput, calls=%fused_computation.2 | convolution fusion | flops 907124736 | bytes 6684672 | tf_op jit(solution)/shard_map/dot_general | solution.py:173
  110.1 1.0 convolution_multiply_fusion
  111.8 2.7 %slice.87 = bf16[16,11,3072]{2,1,0:T(8,128)(2,1)} slice(bf16[16,48,3072]{2,1,0:T(8,128)(2,1)} %bitcast.213), slice={[0:16], [32:43], [0:3072]} | slice | bytes 2162688 | tf_op jit(solution)/shard_map/slice | solution.py:134
  114.6 2.1 copy.162
  119.9 2.8 %reshape_reshape.6 = bf16[3072,256]{1,0:T(8,128)(2,1)} reshape(bf16[16,16,3072]{2,1,0:T(8,128)(2,1)S(1)} %get-tuple-element.7) | data formatting | bytes 3145728 | tf_op jit(solution)/shard_map/reshape;reshape | solution.py:131
  122.7 53.3 %reduce-scatter.2.cloned.1.call-done = bf16[1,16,3072]{2,1,0:T(8,128)(2,1)} async-done(((bf16[16,16,3072]{2,1,0:T(8,128)(2,1)}), bf16[1,16,3072]{2,1,0:T(8,128)(2,1)}) %reduce-scatter.2.cloned.1.call-update) | async-done | bytes 98320 | tf_op jit(solution)/shard_map/reduce_scatter | solution.py:174
  176.1 1.3 fusion.40
  177.8 1.0 copy-done.1
  179.6 1.9 collective-permute-start
  182.2 1.0 collective-permute-done
  183.4 3.3 %collective-permute-start.1 = (bf16[4,8,3072]{2,1,0:T(8,128)(2,1)S(1)}, bf16[4,8,3072]{2,1,0:T(8,128)(2,1)S(1)}, u32[]{:S(2)}, u32[]{:S(2)}) collective-permute-start(bf16[4,8,3072]{2,1,0:T(8,128)(2,1)S(1)} %fusion.29), channel_id=1, source_target_pairs={{0,2},{1,3},{2,0},{3,1},{4,6},{5,7},{6,4},{7,5},{8,10},{9,11},{10,... | collective-permute-start | bytes 589832 | tf_op jit(solution)/shard_map/ppermute | solution.py:30
  187.4 4.8 %collective-permute-done.1 = bf16[4,8,3072]{2,1,0:T(8,128)(2,1)S(1)} collective-permute-done((bf16[4,8,3072]{2,1,0:T(8,128)(2,1)S(1)}, bf16[4,8,3072]{2,1,0:T(8,128)(2,1)S(1)}, u32[]{:S(2)}, u32[]{:S(2)}) %collective-permute-start.1) | collective-permute-done | bytes 196640 | tf_op jit(solution)/shard_map/ppermute | solution.py:30
  192.6 4.6 %collective-permute-start.2 = (bf16[4,4,3072]{2,0,1:T(4,128)(2,1)S(1)}, bf16[4,4,3072]{2,0,1:T(4,128)(2,1)S(1)}, u32[]{:S(2)}, u32[]{:S(2)}) collective-permute-start(bf16[4,4,3072]{2,0,1:T(4,128)(2,1)S(1)} %fusion.37), channel_id=1, source_target_pairs={{0,6},{1,7},{2,4},{3,5},{4,2},{5,3},{6,0},{7,1},{8,14},{9,15},{10,... | collective-permute-start | bytes 294920 | tf_op jit(solution)/shard_map/ppermute | solution.py:30
  197.9 2.4 %collective-permute-done.2 = bf16[4,4,3072]{2,0,1:T(4,128)(2,1)S(1)} collective-permute-done((bf16[4,4,3072]{2,0,1:T(4,128)(2,1)S(1)}, bf16[4,4,3072]{2,0,1:T(4,128)(2,1)S(1)}, u32[]{:S(2)}, u32[]{:S(2)}) %collective-permute-start.2) | collective-permute-done | bytes 98336 | tf_op jit(solution)/shard_map/ppermute | solution.py:30
  200.4 2.8 %collective-permute-start.3 = (bf16[4,2,3072]{2,0,1:T(4,128)(2,1)S(1)}, bf16[4,2,3072]{2,0,1:T(4,128)(2,1)S(1)}, u32[]{:S(2)}, u32[]{:S(2)}) collective-permute-start(bf16[4,2,3072]{2,0,1:T(4,128)(2,1)S(1)} %fusion.54), channel_id=1, source_target_pairs={{0,8},{1,9},{2,10},{3,11},{4,12},{5,13},{6,14},{7,15},{8,0},{9,1},... | collective-permute-start | bytes 147464 | tf_op jit(solution)/shard_map/ppermute | solution.py:30
  203.9 2.5 %collective-permute-done.3 = bf16[4,2,3072]{2,0,1:T(4,128)(2,1)S(1)} collective-permute-done((bf16[4,2,3072]{2,0,1:T(4,128)(2,1)S(1)}, bf16[4,2,3072]{2,0,1:T(4,128)(2,1)S(1)}, u32[]{:S(2)}, u32[]{:S(2)}) %collective-permute-start.3) | collective-permute-done | bytes 49184 | tf_op jit(solution)/shard_map/ppermute | solution.py:30
  206.5 2.4 %collective-permute-start.4 = (bf16[4,1,3072]{2,0,1:T(4,128)(2,1)S(1)}, bf16[4,1,3072]{2,0,1:T(4,128)(2,1)S(1)}, u32[]{:S(2)}, u32[]{:S(2)}) collective-permute-start(bf16[4,1,3072]{2,0,1:T(4,128)(2,1)S(1)} %fusion.57), channel_id=1, source_target_pairs={{0,24},{1,25},{2,26},{3,27},{4,28},{5,29},{6,30},{7,31},{8,16},{9,... | collective-permute-start | bytes 73736 | tf_op jit(solution)/shard_map/ppermute | solution.py:30
  208.9 4.5 %collective-permute-done.4 = bf16[4,1,3072]{2,0,1:T(4,128)(2,1)S(1)} collective-permute-done((bf16[4,1,3072]{2,0,1:T(4,128)(2,1)S(1)}, bf16[4,1,3072]{2,0,1:T(4,128)(2,1)S(1)}, u32[]{:S(2)}, u32[]{:S(2)}) %collective-permute-start.4) | collective-permute-done | bytes 24608 | tf_op jit(solution)/shard_map/ppermute | solution.py:30
  213.4 1.4 fusion.55
  (103 shorter events, 13.8 us)
Async XLA Ops:
  6.5 95.2 %copy-start = (bf16[1,288,3072]{2,1,0:T(8,128)(2,1)S(1)}, bf16[1,288,3072]{2,1,0:T(8,128)(2,1)}, u32[]{:S(2)}) copy-start(bf16[1,288,3072]{2,1,0:T(8,128)(2,1)} %param.22) | copy-start | bytes 5308420
  6.5 6.8 %copy-start.2 = (bf16[128,3072]{1,0:T(8,128)(2,1)S(1)}, bf16[128,3072]{1,0:T(8,128)(2,1)}, u32[]{:S(2)}) copy-start(bf16[128,3072]{1,0:T(8,128)(2,1)} %param.17) | copy-start | bytes 2359300
  6.5 7.1 %copy-start.5 = (bf16[192,256]{1,0:T(8,128)(2,1)S(1)}, bf16[192,256]{1,0:T(8,128)(2,1)}, u32[]{:S(2)}) copy-start(bf16[192,256]{1,0:T(8,128)(2,1)} %param.18) | copy-start | bytes 294916
  6.5 91.9 %all-gather.3.cloned.1.call-start = ((), (), s32[]{:S(2)}) async-start(), calls=%async_computation.2 | async-start | bytes 5013504 | tf_op jit(solution)/shard_map/all_gather | solution.py:125
  8.1 1.7 copy-start.12
  11.9 3.1 %copy-start.14 = (bf16[3072,32]{0,1:T(8,128)(2,1)S(1)}, bf16[3072,32]{0,1:T(8,128)(2,1)}, u32[]{:S(2)}) copy-start(bf16[3072,32]{0,1:T(8,128)(2,1)} %param.19) | copy-start | bytes 589828
  13.6 1.8 copy-start.8
  13.7 2.0 copy-start.13
  15.0 161.1 %reduce-scatter.2.cloned.1.call-start = ((), (), s32[]{:S(2)}) async-start(), calls=%async_computation.1 | async-start | bytes 1671168 | tf_op jit(solution)/shard_map/reduce_scatter | solution.py:174
  107.5 0.7 copy-start.15
  109.5 0.6 copy-start.9
  116.8 0.7 copy-start.10
  116.8 1.6 copy-start.6
  116.8 1.9 copy-start.3
  116.8 1.9 copy-start.7
  116.8 2.2 %copy-start.11 = (f32[128,2]{0,1:T(2,128)S(1)}, f32[128,2]{0,1:T(2,128)}, u32[]{:S(2)}) copy-start(f32[128,2]{0,1:T(2,128)} %get-tuple-element.17) | copy-start | bytes 3076
  176.0 1.4 copy-start.4
  177.4 1.4 copy-start.1
  179.6 3.6 %collective-permute-start = (bf16[4,16,3072]{2,1,0:T(8,128)(2,1)S(1)}, bf16[4,16,3072]{2,1,0:T(8,128)(2,1)S(1)}, u32[]{:S(2)}, u32[]{:S(2)}) collective-permute-start(bf16[4,16,3072]{2,1,0:T(8,128)(2,1)S(1)} %fusion.15), channel_id=1, source_target_pairs={{0,1},{1,0},{2,3},{3,2},{4,5},{5,4},{6,7},{7,6},{8,9},{9,8},{10,11... | collective-permute-start | bytes 1179656 | tf_op jit(solution)/shard_map/ppermute | solution.py:30
  183.4 8.8 %collective-permute-start.1 = (bf16[4,8,3072]{2,1,0:T(8,128)(2,1)S(1)}, bf16[4,8,3072]{2,1,0:T(8,128)(2,1)S(1)}, u32[]{:S(2)}, u32[]{:S(2)}) collective-permute-start(bf16[4,8,3072]{2,1,0:T(8,128)(2,1)S(1)} %fusion.29), channel_id=1, source_target_pairs={{0,2},{1,3},{2,0},{3,1},{4,6},{5,7},{6,4},{7,5},{8,10},{9,11},{10,... | collective-permute-start | bytes 589832 | tf_op jit(solution)/shard_map/ppermute | solution.py:30
  192.6 7.7 %collective-permute-start.2 = (bf16[4,4,3072]{2,0,1:T(4,128)(2,1)S(1)}, bf16[4,4,3072]{2,0,1:T(4,128)(2,1)S(1)}, u32[]{:S(2)}, u32[]{:S(2)}) collective-permute-start(bf16[4,4,3072]{2,0,1:T(4,128)(2,1)S(1)} %fusion.37), channel_id=1, source_target_pairs={{0,6},{1,7},{2,4},{3,5},{4,2},{5,3},{6,0},{7,1},{8,14},{9,15},{10,... | collective-permute-start | bytes 294920 | tf_op jit(solution)/shard_map/ppermute | solution.py:30
  200.4 6.0 %collective-permute-start.3 = (bf16[4,2,3072]{2,0,1:T(4,128)(2,1)S(1)}, bf16[4,2,3072]{2,0,1:T(4,128)(2,1)S(1)}, u32[]{:S(2)}, u32[]{:S(2)}) collective-permute-start(bf16[4,2,3072]{2,0,1:T(4,128)(2,1)S(1)} %fusion.54), channel_id=1, source_target_pairs={{0,8},{1,9},{2,10},{3,11},{4,12},{5,13},{6,14},{7,15},{8,0},{9,1},... | collective-permute-start | bytes 147464 | tf_op jit(solution)/shard_map/ppermute | solution.py:30
  206.5 6.9 %collective-permute-start.4 = (bf16[4,1,3072]{2,0,1:T(4,128)(2,1)S(1)}, bf16[4,1,3072]{2,0,1:T(4,128)(2,1)S(1)}, u32[]{:S(2)}, u32[]{:S(2)}) collective-permute-start(bf16[4,1,3072]{2,0,1:T(4,128)(2,1)S(1)} %fusion.57), channel_id=1, source_target_pairs={{0,24},{1,25},{2,26},{3,27},{4,28},{5,29},{6,30},{7,31},{8,16},{9,... | collective-permute-start | bytes 73736 | tf_op jit(solution)/shard_map/ppermute | solution.py:30
Sparse Core Ops, SparseCore 0:
  15.1 83.3 all-gather.2
  107.6 68.3 reduce-scatter.1

commit v8 on v7

--- a/solution.py
+++ b/solution.py
@@ -11,7 +11,7 @@
     def gray(v):
         return v ^ (v >> 1)
 
-    return [gray(e >> 3) * 8 + gray((e >> 1) & 3) * 2 + (e & 1) for e in range(n)]
+    return [gray((e >> 1) & 3) * 8 + gray(e >> 3) * 2 + (e & 1) for e in range(n)]
 
 
 def halving_scatter(x, axis):

time: 222 us -> 222 us (level)
  no operation moved by 1% of the time
where the time goes in v8:
time: 222 us
  waiting for transfers between devices  151 us (68%)
  local copies, waits for them, and re-layouts  18.8 us (8%)
  between operations  17.3 us (8%)
  starting transfers between devices  15.2 us (7%)
  matrix products  15 us (7%)
  other arithmetic  4.69 us (2%)
    all_gather x1, waiting for transfers between devices, shards(): gathered = lax.all_gather(slab, 'seq', axis=0, tiled=False)  82.1 us
    reduce_scatter x1, waiting for transfers between devices, shards(): lax.psum_scatter(expert_part.astype(jnp.bfloat16).reshape(n_seq, slots, -...  53.3 us
    ppermute x5, waiting for transfers between devices, halving_scatter(): got = lax.ppermute(send.astype(jnp.bfloat16), axis, pairs)  15.3 us
    ppermute x5, starting transfers between devices, halving_scatter(): got = lax.ppermute(send.astype(jnp.bfloat16), axis, pairs)  15.1 us
    dot_general x1, matrix products, shards(): jnp.dot(hidden, down_weight[0], preferred_element_type=jnp.float32)  5.7 us
    unnamed x36, local copies, waits for them, and re-layouts  4.72 us
  transfers between devices with their start and end apart: 7, of which 7 were waited for; matrix products, arithmetic and copies ran while one was open for 6% of the time, Pallas kernels for 0%

profile of v8, /device:TPU:6, one launch (start us, length us, event | category | flops | bytes accessed | tf_op | source)
XLA Modules:
  0.0 221.7 jit_solution(641582180795201680)
XLA Ops:
  6.6 1.6 fusion.69
  9.8 1.0 fusion.42
  10.8 1.0 fusion.5
  16.4 82.1 %all-gather.3.cloned.1.call-done = bf16[768,3072]{1,0:T(8,128)(2,1)} async-done(((bf16[48,3072]{1,0:T(8,128)(2,1)}), bf16[768,3072]{1,0:T(8,128)(2,1)}) %all-gather.3.cloned.1.call-update) | async-done | bytes 4718608 | tf_op jit(solution)/shard_map/all_gather | solution.py:125
  98.5 3.3 %fusion.68 = (bf16[16,16,3072]{2,1,0:T(8,128)(2,1)S(1)}, bf16[16,16,3072]{2,1,0:T(8,128)(2,1)}) fusion(bf16[16,48,3072]{2,1,0:T(8,128)(2,1)} %bitcast.211), kind=kLoop, calls=%fused_computation.120 | loop fusion | bytes 6291456 | tf_op jit(solution)/shard_map/slice | solution.py:129
  101.8 5.7 %convolution_convert_fusion = bf16[256,3072]{1,0:T(8,128)(2,1)} fusion(bf16[1,288,3072]{2,1,0:T(8,128)(2,1)S(1)} %copy-done, bf16[256,3072]{1,0:T(8,128)(2,1)} %bitcast.219, bf16[1,3072,288]{1,2,0:T(8,128)(2,1)} %param.21), kind=kOutput, calls=%fused_computation.2 | convolution fusion | flops 907124736 | bytes 6684672 | tf_op jit(solution)/shard_map/dot_general | solution.py:173
  110.1 1.0 convolution_multiply_fusion
  111.8 2.7 %slice.87 = bf16[16,11,3072]{2,1,0:T(8,128)(2,1)} slice(bf16[16,48,3072]{2,1,0:T(8,128)(2,1)} %bitcast.213), slice={[0:16], [32:43], [0:3072]} | slice | bytes 2162688 | tf_op jit(solution)/shard_map/slice | solution.py:134
  114.6 2.1 copy.162
  119.9 2.8 %reshape_reshape.6 = bf16[3072,256]{1,0:T(8,128)(2,1)} reshape(bf16[16,16,3072]{2,1,0:T(8,128)(2,1)S(1)} %get-tuple-element.7) | data formatting | bytes 3145728 | tf_op jit(solution)/shard_map/reshape;reshape | solution.py:131
  122.7 53.3 %reduce-scatter.2.cloned.1.call-done = bf16[1,16,3072]{2,1,0:T(8,128)(2,1)} async-done(((bf16[16,16,3072]{2,1,0:T(8,128)(2,1)}), bf16[1,16,3072]{2,1,0:T(8,128)(2,1)}) %reduce-scatter.2.cloned.1.call-update) | async-done | bytes 98320 | tf_op jit(solution)/shard_map/reduce_scatter | solution.py:174
  176.1 1.3 fusion.40
  177.8 1.0 copy-done.1
  179.6 1.9 collective-permute-start
  182.2 1.0 collective-permute-done
  183.4 2.8 %collective-permute-start.1 = (bf16[4,8,3072]{2,1,0:T(8,128)(2,1)S(1)}, bf16[4,8,3072]{2,1,0:T(8,128)(2,1)S(1)}, u32[]{:S(2)}, u32[]{:S(2)}) collective-permute-start(bf16[4,8,3072]{2,1,0:T(8,128)(2,1)S(1)} %fusion.29), channel_id=1, source_target_pairs={{0,8},{1,9},{2,10},{3,11},{4,12},{5,13},{6,14},{7,15},{8,0},{9,1},... | collective-permute-start | bytes 589832 | tf_op jit(solution)/shard_map/ppermute | solution.py:30
  186.8 5.4 %collective-permute-done.1 = bf16[4,8,3072]{2,1,0:T(8,128)(2,1)S(1)} collective-permute-done((bf16[4,8,3072]{2,1,0:T(8,128)(2,1)S(1)}, bf16[4,8,3072]{2,1,0:T(8,128)(2,1)S(1)}, u32[]{:S(2)}, u32[]{:S(2)}) %collective-permute-start.1) | collective-permute-done | bytes 196640 | tf_op jit(solution)/shard_map/ppermute | solution.py:30
  192.6 2.4 %collective-permute-start.2 = (bf16[4,4,3072]{2,0,1:T(4,128)(2,1)S(1)}, bf16[4,4,3072]{2,0,1:T(4,128)(2,1)S(1)}, u32[]{:S(2)}, u32[]{:S(2)}) collective-permute-start(bf16[4,4,3072]{2,0,1:T(4,128)(2,1)S(1)} %fusion.37), channel_id=1, source_target_pairs={{0,24},{1,25},{2,26},{3,27},{4,28},{5,29},{6,30},{7,31},{8,16},{9,... | collective-permute-start | bytes 294920 | tf_op jit(solution)/shard_map/ppermute | solution.py:30
  195.7 4.6 %collective-permute-done.2 = bf16[4,4,3072]{2,0,1:T(4,128)(2,1)S(1)} collective-permute-done((bf16[4,4,3072]{2,0,1:T(4,128)(2,1)S(1)}, bf16[4,4,3072]{2,0,1:T(4,128)(2,1)S(1)}, u32[]{:S(2)}, u32[]{:S(2)}) %collective-permute-start.2) | collective-permute-done | bytes 98336 | tf_op jit(solution)/shard_map/ppermute | solution.py:30
  200.4 3.3 %collective-permute-start.3 = (bf16[4,2,3072]{2,0,1:T(4,128)(2,1)S(1)}, bf16[4,2,3072]{2,0,1:T(4,128)(2,1)S(1)}, u32[]{:S(2)}, u32[]{:S(2)}) collective-permute-start(bf16[4,2,3072]{2,0,1:T(4,128)(2,1)S(1)} %fusion.54), channel_id=1, source_target_pairs={{0,2},{1,3},{2,0},{3,1},{4,6},{5,7},{6,4},{7,5},{8,10},{9,11},{10,... | collective-permute-start | bytes 147464 | tf_op jit(solution)/shard_map/ppermute | solution.py:30
  204.4 2.0 collective-permute-done.3
  206.5 4.6 %collective-permute-start.4 = (bf16[4,1,3072]{2,0,1:T(4,128)(2,1)S(1)}, bf16[4,1,3072]{2,0,1:T(4,128)(2,1)S(1)}, u32[]{:S(2)}, u32[]{:S(2)}) collective-permute-start(bf16[4,1,3072]{2,0,1:T(4,128)(2,1)S(1)} %fusion.57), channel_id=1, source_target_pairs={{0,6},{1,7},{2,4},{3,5},{4,2},{5,3},{6,0},{7,1},{8,14},{9,15},{10,... | collective-permute-start | bytes 73736 | tf_op jit(solution)/shard_map/ppermute | solution.py:30
  211.1 2.3 %collective-permute-done.4 = bf16[4,1,3072]{2,0,1:T(4,128)(2,1)S(1)} collective-permute-done((bf16[4,1,3072]{2,0,1:T(4,128)(2,1)S(1)}, bf16[4,1,3072]{2,0,1:T(4,128)(2,1)S(1)}, u32[]{:S(2)}, u32[]{:S(2)}) %collective-permute-start.4) | collective-permute-done | bytes 24608 | tf_op jit(solution)/shard_map/ppermute | solution.py:30
  213.4 1.4 fusion.55
  (103 shorter events, 13.8 us)
Async XLA Ops:
  6.5 95.2 %copy-start = (bf16[1,288,3072]{2,1,0:T(8,128)(2,1)S(1)}, bf16[1,288,3072]{2,1,0:T(8,128)(2,1)}, u32[]{:S(2)}) copy-start(bf16[1,288,3072]{2,1,0:T(8,128)(2,1)} %param.22) | copy-start | bytes 5308420
  6.5 6.8 %copy-start.2 = (bf16[128,3072]{1,0:T(8,128)(2,1)S(1)}, bf16[128,3072]{1,0:T(8,128)(2,1)}, u32[]{:S(2)}) copy-start(bf16[128,3072]{1,0:T(8,128)(2,1)} %param.17) | copy-start | bytes 2359300
  6.5 7.1 %copy-start.5 = (bf16[192,256]{1,0:T(8,128)(2,1)S(1)}, bf16[192,256]{1,0:T(8,128)(2,1)}, u32[]{:S(2)}) copy-start(bf16[192,256]{1,0:T(8,128)(2,1)} %param.18) | copy-start | bytes 294916
  6.5 91.9 %all-gather.3.cloned.1.call-start = ((), (), s32[]{:S(2)}) async-start(), calls=%async_computation.2 | async-start | bytes 5013504 | tf_op jit(solution)/shard_map/all_gather | solution.py:125
  8.1 1.7 copy-start.12
  11.9 3.1 %copy-start.14 = (bf16[3072,32]{0,1:T(8,128)(2,1)S(1)}, bf16[3072,32]{0,1:T(8,128)(2,1)}, u32[]{:S(2)}) copy-start(bf16[3072,32]{0,1:T(8,128)(2,1)} %param.19) | copy-start | bytes 589828
  13.6 1.8 copy-start.8
  13.7 2.0 copy-start.13
  15.0 161.1 %reduce-scatter.2.cloned.1.call-start = ((), (), s32[]{:S(2)}) async-start(), calls=%async_computation.1 | async-start | bytes 1671168 | tf_op jit(solution)/shard_map/reduce_scatter | solution.py:174
  107.5 0.7 copy-start.15
  109.5 0.6 copy-start.9
  116.8 0.7 copy-start.10
  116.8 1.6 copy-start.6
  116.8 1.9 copy-start.3
  116.8 1.9 copy-start.7
  116.8 2.2 %copy-start.11 = (f32[128,2]{0,1:T(2,128)S(1)}, f32[128,2]{0,1:T(2,128)}, u32[]{:S(2)}) copy-start(f32[128,2]{0,1:T(2,128)} %get-tuple-element.17) | copy-start | bytes 3076
  176.0 1.4 copy-start.4
  177.4 1.4 copy-start.1
  179.6 3.6 %collective-permute-start = (bf16[4,16,3072]{2,1,0:T(8,128)(2,1)S(1)}, bf16[4,16,3072]{2,1,0:T(8,128)(2,1)S(1)}, u32[]{:S(2)}, u32[]{:S(2)}) collective-permute-start(bf16[4,16,3072]{2,1,0:T(8,128)(2,1)S(1)} %fusion.15), channel_id=1, source_target_pairs={{0,1},{1,0},{2,3},{3,2},{4,5},{5,4},{6,7},{7,6},{8,9},{9,8},{10,11... | collective-permute-start | bytes 1179656 | tf_op jit(solution)/shard_map/ppermute | solution.py:30
  183.4 8.8 %collective-permute-start.1 = (bf16[4,8,3072]{2,1,0:T(8,128)(2,1)S(1)}, bf16[4,8,3072]{2,1,0:T(8,128)(2,1)S(1)}, u32[]{:S(2)}, u32[]{:S(2)}) collective-permute-start(bf16[4,8,3072]{2,1,0:T(8,128)(2,1)S(1)} %fusion.29), channel_id=1, source_target_pairs={{0,8},{1,9},{2,10},{3,11},{4,12},{5,13},{6,14},{7,15},{8,0},{9,1},... | collective-permute-start | bytes 589832 | tf_op jit(solution)/shard_map/ppermute | solution.py:30
  192.6 7.7 %collective-permute-start.2 = (bf16[4,4,3072]{2,0,1:T(4,128)(2,1)S(1)}, bf16[4,4,3072]{2,0,1:T(4,128)(2,1)S(1)}, u32[]{:S(2)}, u32[]{:S(2)}) collective-permute-start(bf16[4,4,3072]{2,0,1:T(4,128)(2,1)S(1)} %fusion.37), channel_id=1, source_target_pairs={{0,24},{1,25},{2,26},{3,27},{4,28},{5,29},{6,30},{7,31},{8,16},{9,... | collective-permute-start | bytes 294920 | tf_op jit(solution)/shard_map/ppermute | solution.py:30
  200.4 6.0 %collective-permute-start.3 = (bf16[4,2,3072]{2,0,1:T(4,128)(2,1)S(1)}, bf16[4,2,3072]{2,0,1:T(4,128)(2,1)S(1)}, u32[]{:S(2)}, u32[]{:S(2)}) collective-permute-start(bf16[4,2,3072]{2,0,1:T(4,128)(2,1)S(1)} %fusion.54), channel_id=1, source_target_pairs={{0,2},{1,3},{2,0},{3,1},{4,6},{5,7},{6,4},{7,5},{8,10},{9,11},{10,... | collective-permute-start | bytes 147464 | tf_op jit(solution)/shard_map/ppermute | solution.py:30
  206.5 6.9 %collective-permute-start.4 = (bf16[4,1,3072]{2,0,1:T(4,128)(2,1)S(1)}, bf16[4,1,3072]{2,0,1:T(4,128)(2,1)S(1)}, u32[]{:S(2)}, u32[]{:S(2)}) collective-permute-start(bf16[4,1,3072]{2,0,1:T(4,128)(2,1)S(1)} %fusion.57), channel_id=1, source_target_pairs={{0,6},{1,7},{2,4},{3,5},{4,2},{5,3},{6,0},{7,1},{8,14},{9,15},{10,... | collective-permute-start | bytes 73736 | tf_op jit(solution)/shard_map/ppermute | solution.py:30
Sparse Core Ops, SparseCore 0:
  15.1 83.3 all-gather.2
  107.6 68.3 reduce-scatter.1

commit v9 on v8

--- a/solution.py
+++ b/solution.py
@@ -77,7 +77,15 @@
     ) + jnp.einsum("hjd,hje->hde", kscaled_lo, vbf, preferred_element_type=jnp.float32)
 
     stream = residual.astype(jnp.float32)
-    normed = (stream * lax.rsqrt(jnp.mean(stream * stream, axis=-1, keepdims=True) + 1e-05)).astype(
+    square = stream * stream
+    square_hi = square.astype(jnp.bfloat16)
+    square_lo = (square - square_hi.astype(jnp.float32)).astype(jnp.bfloat16)
+    ones = jnp.ones((stream.shape[1], 128), jnp.bfloat16)
+    sums = jnp.dot(square_hi, ones, preferred_element_type=jnp.float32) + jnp.dot(
+        square_lo, ones, preferred_element_type=jnp.float32
+    )
+    mean_square = sums[:, :1] / stream.shape[1]
+    normed = (stream * lax.rsqrt(mean_square + 1e-05)).astype(
         jnp.bfloat16
     )
     logits = jnp.dot(normed, router, preferred_element_type=jnp.float32)

time: 222 us -> 220 us (level)
    dot_general x0 -> x2, matrix products: none -> 3.31 us  [the longest x1 1.68 us: shards(): jnp.dot(square_lo, ones, preferred_element_type=jnp.float32)]
    unnamed x36 -> x32, local copies, waits for them, and re-layouts: 4.72 us -> 3.9 us
  transfers between devices with their start and end apart: 7 -> 7, of which waited for: 7 -> 7; matrix products, arithmetic and copies ran while one was open for 6% -> 7% of each run, Pallas kernels for 0% -> 0%
where the time goes in v9:
time: 220 us
  waiting for transfers between devices  151 us (69%)
  between operations  17.2 us (8%)
  local copies, waits for them, and re-layouts  17.1 us (8%)
  matrix products  15.9 us (7%)
  starting transfers between devices  15.3 us (7%)
  other arithmetic  3.22 us (1%)
    all_gather x1, waiting for transfers between devices, shards(): gathered = lax.all_gather(slab, 'seq', axis=0, tiled=False)  82.1 us
    reduce_scatter x1, waiting for transfers between devices, shards(): lax.psum_scatter(expert_part.astype(jnp.bfloat16).reshape(n_seq, slots, -...  53.6 us
    ppermute x5, starting transfers between devices, halving_scatter(): got = lax.ppermute(send.astype(jnp.bfloat16), axis, pairs)  15.2 us
    ppermute x5, waiting for transfers between devices, halving_scatter(): got = lax.ppermute(send.astype(jnp.bfloat16), axis, pairs)  15.2 us
    dot_general x1, matrix products, shards(): jnp.dot(hidden, down_weight[0], preferred_element_type=jnp.float32)  5.69 us
  transfers between devices with their start and end apart: 7, of which 7 were waited for; matrix products, arithmetic and copies ran while one was open for 7% of the time, Pallas kernels for 0%

profile of v9, /device:TPU:6, one launch (start us, length us, event | category | flops | bytes accessed | tf_op | source)
XLA Modules:
  0.0 219.7 jit_solution(67964211989079982)
XLA Ops:
  6.6 1.7 fusion.13
  8.3 1.6 fusion.16
  14.5 82.1 %all-gather.3.cloned.1.call-done = bf16[768,3072]{1,0:T(8,128)(2,1)} async-done(((bf16[48,3072]{1,0:T(8,128)(2,1)}), bf16[768,3072]{1,0:T(8,128)(2,1)}) %all-gather.3.cloned.1.call-update) | async-done | bytes 4718608 | tf_op jit(solution)/shard_map/all_gather | solution.py:133
  96.6 3.3 %fusion.80 = (bf16[16,16,3072]{2,1,0:T(8,128)(2,1)S(1)}, bf16[16,16,3072]{2,1,0:T(8,128)(2,1)}) fusion(bf16[16,48,3072]{2,1,0:T(8,128)(2,1)} %bitcast.213), kind=kLoop, calls=%fused_computation.130 | loop fusion | bytes 6291456 | tf_op jit(solution)/shard_map/slice | solution.py:137
  99.9 5.7 %convolution_convert_fusion = bf16[256,3072]{1,0:T(8,128)(2,1)} fusion(bf16[1,288,3072]{2,1,0:T(8,128)(2,1)S(1)} %copy-done, bf16[256,3072]{1,0:T(8,128)(2,1)} %bitcast.221, bf16[1,3072,288]{1,2,0:T(8,128)(2,1)} %param.21), kind=kOutput, calls=%fused_computation.2 | convolution fusion | flops 907124736 | bytes 6684672 | tf_op jit(solution)/shard_map/dot_general | solution.py:181
  107.5 1.7 convolution_multiply_fusion
  109.9 2.7 %slice.93 = bf16[16,11,3072]{2,1,0:T(8,128)(2,1)} slice(bf16[16,48,3072]{2,1,0:T(8,128)(2,1)} %bitcast.215), slice={[0:16], [32:43], [0:3072]} | slice | bytes 2162688 | tf_op jit(solution)/shard_map/slice | solution.py:142
  112.7 2.1 copy.162
  115.2 1.0 fusion.8
  117.7 2.8 %reshape_reshape.6 = bf16[3072,256]{1,0:T(8,128)(2,1)} reshape(bf16[16,16,3072]{2,1,0:T(8,128)(2,1)S(1)} %get-tuple-element.7) | data formatting | bytes 3145728 | tf_op jit(solution)/shard_map/reshape;reshape | solution.py:139
  120.5 53.6 %reduce-scatter.2.cloned.1.call-done = bf16[1,16,3072]{2,1,0:T(8,128)(2,1)} async-done(((bf16[16,16,3072]{2,1,0:T(8,128)(2,1)}), bf16[1,16,3072]{2,1,0:T(8,128)(2,1)}) %reduce-scatter.2.cloned.1.call-update) | async-done | bytes 98320 | tf_op jit(solution)/shard_map/reduce_scatter | solution.py:182
  174.1 1.3 fusion.49
  175.9 1.0 copy-done.1
  177.6 1.9 collective-permute-start
  180.2 1.0 collective-permute-done
  181.4 2.8 %collective-permute-start.1 = (bf16[4,8,3072]{2,1,0:T(8,128)(2,1)S(1)}, bf16[4,8,3072]{2,1,0:T(8,128)(2,1)S(1)}, u32[]{:S(2)}, u32[]{:S(2)}) collective-permute-start(bf16[4,8,3072]{2,1,0:T(8,128)(2,1)S(1)} %fusion.38), channel_id=1, source_target_pairs={{0,8},{1,9},{2,10},{3,11},{4,12},{5,13},{6,14},{7,15},{8,0},{9,1},... | collective-permute-start | bytes 589832 | tf_op jit(solution)/shard_map/ppermute | solution.py:30
  184.9 5.4 %collective-permute-done.1 = bf16[4,8,3072]{2,1,0:T(8,128)(2,1)S(1)} collective-permute-done((bf16[4,8,3072]{2,1,0:T(8,128)(2,1)S(1)}, bf16[4,8,3072]{2,1,0:T(8,128)(2,1)S(1)}, u32[]{:S(2)}, u32[]{:S(2)}) %collective-permute-start.1) | collective-permute-done | bytes 196640 | tf_op jit(solution)/shard_map/ppermute | solution.py:30
  190.6 2.4 %collective-permute-start.2 = (bf16[4,4,3072]{2,0,1:T(4,128)(2,1)S(1)}, bf16[4,4,3072]{2,0,1:T(4,128)(2,1)S(1)}, u32[]{:S(2)}, u32[]{:S(2)}) collective-permute-start(bf16[4,4,3072]{2,0,1:T(4,128)(2,1)S(1)} %fusion.46), channel_id=1, source_target_pairs={{0,24},{1,25},{2,26},{3,27},{4,28},{5,29},{6,30},{7,31},{8,16},{9,... | collective-permute-start | bytes 294920 | tf_op jit(solution)/shard_map/ppermute | solution.py:30
  193.7 4.6 %collective-permute-done.2 = bf16[4,4,3072]{2,0,1:T(4,128)(2,1)S(1)} collective-permute-done((bf16[4,4,3072]{2,0,1:T(4,128)(2,1)S(1)}, bf16[4,4,3072]{2,0,1:T(4,128)(2,1)S(1)}, u32[]{:S(2)}, u32[]{:S(2)}) %collective-permute-start.2) | collective-permute-done | bytes 98336 | tf_op jit(solution)/shard_map/ppermute | solution.py:30
  198.5 3.4 %collective-permute-start.3 = (bf16[4,2,3072]{2,0,1:T(4,128)(2,1)S(1)}, bf16[4,2,3072]{2,0,1:T(4,128)(2,1)S(1)}, u32[]{:S(2)}, u32[]{:S(2)}) collective-permute-start(bf16[4,2,3072]{2,0,1:T(4,128)(2,1)S(1)} %fusion.63), channel_id=1, source_target_pairs={{0,2},{1,3},{2,0},{3,1},{4,6},{5,7},{6,4},{7,5},{8,10},{9,11},{10,... | collective-permute-start | bytes 147464 | tf_op jit(solution)/shard_map/ppermute | solution.py:30
  202.5 2.0 collective-permute-done.3
  204.5 4.7 %collective-permute-start.4 = (bf16[4,1,3072]{2,0,1:T(4,128)(2,1)S(1)}, bf16[4,1,3072]{2,0,1:T(4,128)(2,1)S(1)}, u32[]{:S(2)}, u32[]{:S(2)}) collective-permute-start(bf16[4,1,3072]{2,0,1:T(4,128)(2,1)S(1)} %fusion.66), channel_id=1, source_target_pairs={{0,6},{1,7},{2,4},{3,5},{4,2},{5,3},{6,0},{7,1},{8,14},{9,15},{10,... | collective-permute-start | bytes 73736 | tf_op jit(solution)/shard_map/ppermute | solution.py:30
  209.2 2.2 %collective-permute-done.4 = bf16[4,1,3072]{2,0,1:T(4,128)(2,1)S(1)} collective-permute-done((bf16[4,1,3072]{2,0,1:T(4,128)(2,1)S(1)}, bf16[4,1,3072]{2,0,1:T(4,128)(2,1)S(1)}, u32[]{:S(2)}, u32[]{:S(2)}) %collective-permute-start.4) | collective-permute-done | bytes 24608 | tf_op jit(solution)/shard_map/ppermute | solution.py:30
  211.5 1.4 fusion.64
  (100 shorter events, 10.1 us)
Async XLA Ops:
  6.5 93.3 %copy-start = (bf16[1,288,3072]{2,1,0:T(8,128)(2,1)S(1)}, bf16[1,288,3072]{2,1,0:T(8,128)(2,1)}, u32[]{:S(2)}) copy-start(bf16[1,288,3072]{2,1,0:T(8,128)(2,1)} %param.22) | copy-start | bytes 5308420
  6.5 3.4 %copy-start.12 = (f32[2,128]{1,0:T(2,128)S(1)}, f32[2,128]{1,0:T(2,128)}, u32[]{:S(2)}) copy-start(f32[2,128]{1,0:T(2,128)} %param.16) | copy-start | bytes 3076
  6.5 3.9 %copy-start.8 = (bf16[128,256]{1,0:T(8,128)(2,1)S(1)}, bf16[128,256]{1,0:T(8,128)(2,1)}, u32[]{:S(2)}) copy-start(bf16[128,256]{1,0:T(8,128)(2,1)} %param.14) | copy-start | bytes 196612
  6.5 4.0 %copy-start.3 = (bf16[128,256]{1,0:T(8,128)(2,1)S(1)}, bf16[128,256]{1,0:T(8,128)(2,1)}, u32[]{:S(2)}) copy-start(bf16[128,256]{1,0:T(8,128)(2,1)} %param.15) | copy-start | bytes 196612
  6.5 90.0 %all-gather.3.cloned.1.call-start = ((), (), s32[]{:S(2)}) async-start(), calls=%async_computation.2 | async-start | bytes 5013504 | tf_op jit(solution)/shard_map/all_gather | solution.py:133
  6.6 4.3 %copy-start.9 = (s32[128,2]{0,1:T(2,128)S(1)}, s32[128,2]{0,1:T(2,128)}, u32[]{:S(2)}) copy-start(s32[128,2]{0,1:T(2,128)} %param.20) | copy-start | bytes 3076
  8.3 3.4 %copy-start.6 = (bf16[192,256]{1,0:T(8,128)(2,1)S(1)}, bf16[192,256]{1,0:T(8,128)(2,1)}, u32[]{:S(2)}) copy-start(bf16[192,256]{1,0:T(8,128)(2,1)} %param.18) | copy-start | bytes 294916
  8.3 3.6 %copy-start.2 = (bf16[128,3072]{1,0:T(8,128)(2,1)S(1)}, bf16[128,3072]{1,0:T(8,128)(2,1)}, u32[]{:S(2)}) copy-start(bf16[128,3072]{1,0:T(8,128)(2,1)} %param.17) | copy-start | bytes 2359300
  10.5 2.6 %copy-start.11 = (bf16[3072,32]{0,1:T(8,128)(2,1)S(1)}, bf16[3072,32]{0,1:T(8,128)(2,1)}, u32[]{:S(2)}) copy-start(bf16[3072,32]{0,1:T(8,128)(2,1)} %param.19) | copy-start | bytes 589828
  11.7 2.0 copy-start.10
  13.1 161.1 %reduce-scatter.2.cloned.1.call-start = ((), (), s32[]{:S(2)}) async-start(), calls=%async_computation.1 | async-start | bytes 1671168 | tf_op jit(solution)/shard_map/reduce_scatter | solution.py:182
  105.6 0.7 copy-start.13
  114.9 1.4 copy-start.7
  114.9 1.6 copy-start.5
  174.1 1.3 copy-start.4
  175.5 1.4 copy-start.1
  177.6 3.6 %collective-permute-start = (bf16[4,16,3072]{2,1,0:T(8,128)(2,1)S(1)}, bf16[4,16,3072]{2,1,0:T(8,128)(2,1)S(1)}, u32[]{:S(2)}, u32[]{:S(2)}) collective-permute-start(bf16[4,16,3072]{2,1,0:T(8,128)(2,1)S(1)} %fusion.22), channel_id=1, source_target_pairs={{0,1},{1,0},{2,3},{3,2},{4,5},{5,4},{6,7},{7,6},{8,9},{9,8},{10,11... | collective-permute-start | bytes 1179656 | tf_op jit(solution)/shard_map/ppermute | solution.py:30
  181.4 8.8 %collective-permute-start.1 = (bf16[4,8,3072]{2,1,0:T(8,128)(2,1)S(1)}, bf16[4,8,3072]{2,1,0:T(8,128)(2,1)S(1)}, u32[]{:S(2)}, u32[]{:S(2)}) collective-permute-start(bf16[4,8,3072]{2,1,0:T(8,128)(2,1)S(1)} %fusion.38), channel_id=1, source_target_pairs={{0,8},{1,9},{2,10},{3,11},{4,12},{5,13},{6,14},{7,15},{8,0},{9,1},... | collective-permute-start | bytes 589832 | tf_op jit(solution)/shard_map/ppermute | solution.py:30
  190.6 7.7 %collective-permute-start.2 = (bf16[4,4,3072]{2,0,1:T(4,128)(2,1)S(1)}, bf16[4,4,3072]{2,0,1:T(4,128)(2,1)S(1)}, u32[]{:S(2)}, u32[]{:S(2)}) collective-permute-start(bf16[4,4,3072]{2,0,1:T(4,128)(2,1)S(1)} %fusion.46), channel_id=1, source_target_pairs={{0,24},{1,25},{2,26},{3,27},{4,28},{5,29},{6,30},{7,31},{8,16},{9,... | collective-permute-start | bytes 294920 | tf_op jit(solution)/shard_map/ppermute | solution.py:30
  198.5 6.0 %collective-permute-start.3 = (bf16[4,2,3072]{2,0,1:T(4,128)(2,1)S(1)}, bf16[4,2,3072]{2,0,1:T(4,128)(2,1)S(1)}, u32[]{:S(2)}, u32[]{:S(2)}) collective-permute-start(bf16[4,2,3072]{2,0,1:T(4,128)(2,1)S(1)} %fusion.63), channel_id=1, source_target_pairs={{0,2},{1,3},{2,0},{3,1},{4,6},{5,7},{6,4},{7,5},{8,10},{9,11},{10,... | collective-permute-start | bytes 147464 | tf_op jit(solution)/shard_map/ppermute | solution.py:30
  204.5 6.9 %collective-permute-start.4 = (bf16[4,1,3072]{2,0,1:T(4,128)(2,1)S(1)}, bf16[4,1,3072]{2,0,1:T(4,128)(2,1)S(1)}, u32[]{:S(2)}, u32[]{:S(2)}) collective-permute-start(bf16[4,1,3072]{2,0,1:T(4,128)(2,1)S(1)} %fusion.66), channel_id=1, source_target_pairs={{0,6},{1,7},{2,4},{3,5},{4,2},{5,3},{6,0},{7,1},{8,14},{9,15},{10,... | collective-permute-start | bytes 73736 | tf_op jit(solution)/shard_map/ppermute | solution.py:30
Sparse Core Ops, SparseCore 0:
  13.2 83.3 all-gather.2
  105.7 68.3 reduce-scatter.1
